TPU v7x, 32 devices: a whole 2x2x4 slice. The times are simulated.
32 devices in a mesh: slab: 16 (over z, x, core), energy: 2 (over y).
Axes of the slice: x: 2, y: 2, z: 4, core: 2. Of those that a mesh axis runs over, the one named last changes fastest.
Arguments:
- mode_floor: float32 [1024], replicated, may hold values from -2.5 to 2.5
- onsite_noise: float32 [256, 1024], P('slab'), may hold values from -0.4 to 0.4
- hopping: float32 [256, 1024], P('slab'), may hold values from 2.3 to 2.7
- lengths: int32 [16], replicated, may hold values from 1 to 16, 128 in all
- energy_index: int32 [8], P('energy'), may hold values from 0 to 4095
- weight_code: int32 [8], P('energy'), may hold values from 1 to 63
- lead_shift: float32 [8, 2, 1024], P('energy'), may hold values from -0.5 to 0.5
- lead_width: float32 [8, 2, 1024], P('energy'), may hold values from 0.2 to 1.2
Outputs:
- density: float32 [256, 1024], P('slab', 'energy')
- bond_density: float32 [256, 1024], P('slab', 'energy')
Inputs may be any that keep to these rules, and one draw needn't show every extreme that they name: `lengths`: entry d counts the slabs of index d of slab, which fill its first slots; the entries sum to 128.
All inputs are finite; a program needn't handle non-finite values.
Results may differ from a plain program's by a relative error of at most 0.029.
Values sent between devices are 32-bit elements; how exact they have to be, the bound alone decides.
No kernel may reach another device: no remote copies, remote signals or barrier semaphores. Data moves between devices by JAX's collectives and lax.ppermute only.
A program may use at most 64 MiB of HBM per device.

v0:
```python
import jax
import jax.numpy as jnp
from jax import lax
from jax.sharding import PartitionSpec as P

broaden = 0.002
e_low = -1.5
e_step = 3.0 / 4096.0
inv_pi = 1.0 / 3.141592653589793


def entering(value, axis, join, neutral, backward):
    count, mine = (lax.axis_size(axis), lax.axis_index(axis))
    pieces = jax.tree.map(lambda part: lax.all_gather(part, axis), value)
    if backward:
        pieces = jax.tree.map(lambda part: part[::-1], pieces)
        mine = count - 1 - mine
    subtotal = jax.tree.map(
        lambda part, zero: jnp.full_like(part, 0) + jnp.asarray(zero, part.dtype), value, neutral
    )

    def turn(position, subtotal):
        longer = join(subtotal, jax.tree.map(lambda part: part[position], pieces))
        return jax.tree.map(lambda new, old: jnp.where(position < mine, new, old), longer, subtotal)

    return lax.fori_loop(0, count - 1, turn, subtotal)


def reciprocal(real_part, imag_part):
    norm = real_part * real_part + imag_part * imag_part
    return (real_part / norm, -imag_part / norm)


def complex_mul(first_re, first_im, second_re, second_im):
    return (
        first_re * second_re - first_im * second_im,
        first_re * second_im + first_im * second_re,
    )


def choose_value(keep_right, keep_left, left_value, right_value, joined_value):
    return jnp.where(keep_right, right_value, jnp.where(keep_left, left_value, joined_value))


def join_segments(left, right):
    square = left[6] * left[6]
    mix_re, mix_im = complex_mul(left[4], left[5], right[0], right[1])
    inv_re, inv_im = reciprocal(1.0 - square * mix_re, -square * mix_im)
    left_sq_re, left_sq_im = complex_mul(left[2], left[3], left[2], left[3])
    head_re, head_im = complex_mul(left_sq_re, left_sq_im, right[0], right[1])
    head_re, head_im = complex_mul(head_re, head_im, inv_re, inv_im)
    right_sq_re, right_sq_im = complex_mul(right[2], right[3], right[2], right[3])
    tail_re, tail_im = complex_mul(right_sq_re, right_sq_im, left[4], left[5])
    tail_re, tail_im = complex_mul(tail_re, tail_im, inv_re, inv_im)
    link_re, link_im = complex_mul(left[2], left[3], right[2], right[3])
    link_re, link_im = complex_mul(link_re, link_im, inv_re, inv_im)
    joined = (
        left[0] + square * head_re,
        left[1] + square * head_im,
        left[6] * link_re,
        left[6] * link_im,
        right[4] + square * tail_re,
        right[5] + square * tail_im,
        right[6],
        jnp.maximum(left[7], right[7]),
    )
    keep_right = left[7] < 0.5
    keep_left = right[7] < 0.5
    return tuple(
        (
            choose_value(keep_right, keep_left, left_value, right_value, joined_value)
            for left_value, right_value, joined_value in zip(left, right, joined)
        )
    )


def join_reverse(earlier, later):
    return join_segments(later, earlier)


def fold_slot(carry, slot_data):
    onsite_re, onsite_im, coupling, live = slot_data
    g_re, g_im = reciprocal(onsite_re, onsite_im)
    single = (g_re, g_im, g_re, g_im, g_re, g_im, coupling, live.reshape(1, 1))
    return (join_segments(carry, single), None)


def forward_step(carry, slot_data):
    prev_re, prev_im, prev_coupling = carry
    onsite_re, onsite_im, coupling, live = slot_data
    square = prev_coupling * prev_coupling
    g_re, g_im = reciprocal(onsite_re - square * prev_re, onsite_im - square * prev_im)
    keep = live > 0.5
    new_carry = (
        jnp.where(keep, g_re, prev_re),
        jnp.where(keep, g_im, prev_im),
        jnp.where(keep, coupling, prev_coupling),
    )
    return (new_carry, (g_re, g_im))


def backward_step(carry, slot_data):
    next_re, next_im = carry
    onsite_re, onsite_im, coupling, live = slot_data
    square = coupling * coupling
    g_re, g_im = reciprocal(onsite_re - square * next_re, onsite_im - square * next_im)
    keep = live > 0.5
    return ((jnp.where(keep, g_re, next_re), jnp.where(keep, g_im, next_im)), (next_re, next_im))


def shards(
    mode_floor, onsite_noise, hopping, lengths, energy_index, weight_code, lead_shift, lead_width
):
    slots = onsite_noise.shape[0]
    modes = onsite_noise.shape[1]
    points = energy_index.shape[0]
    here = lax.axis_index("slab")
    devices = lax.axis_size("slab")
    count = lengths[here]
    place = jnp.arange(slots, dtype=jnp.int32)
    alive = (place < count).astype(jnp.float32)
    first_on = ((here == 0) & (place == 0)).astype(jnp.float32)[:, None, None]
    last_on = ((here == devices - 1) & (place == count - 1)).astype(jnp.float32)[:, None, None]
    energies = e_low + e_step * energy_index.astype(jnp.float32)
    weights = weight_code.astype(jnp.float32) / (32.0 * points * lax.axis_size("energy"))
    levels = mode_floor[None, :] + onsite_noise
    onsite_re = (
        energies[None, :, None]
        - levels[:, None, :]
        - first_on * lead_shift[None, :, 0, :]
        - last_on * lead_shift[None, :, 1, :]
    )
    onsite_im = broaden + first_on * lead_width[None, :, 0, :] + last_on * lead_width[None, :, 1, :]
    coupling_rows = hopping[:, None, :]
    xs = (onsite_re, onsite_im, coupling_rows, alive)
    flat = jnp.zeros((points, modes), jnp.float32)
    empty = (
        flat,
        flat,
        flat,
        flat,
        flat,
        flat,
        jnp.zeros((1, modes), jnp.float32),
        jnp.zeros((1, 1), jnp.float32),
    )
    summary, _ = lax.scan(fold_slot, empty, xs)
    first_re, first_im, cross_re, cross_im, final_re, final_im, coupling, present = summary
    before = entering(
        (first_re, first_im, cross_re, cross_im, final_re, final_im, coupling, present),
        "slab",
        join_segments,
        empty,
        False,
    )
    after = entering(
        (first_re, first_im, cross_re, cross_im, final_re, final_im, coupling, present),
        "slab",
        join_reverse,
        empty,
        True,
    )
    _, (left_re, left_im) = lax.scan(forward_step, (before[4], before[5], before[6]), xs)
    _, (next_re, next_im) = lax.scan(backward_step, (after[0], after[1]), xs, reverse=True)
    square = coupling_rows * coupling_rows
    mix_re, mix_im = complex_mul(left_re, left_im, next_re, next_im)
    inv_re, inv_im = reciprocal(1.0 - square * mix_re, -square * mix_im)
    diag_re, diag_im = complex_mul(left_re, left_im, inv_re, inv_im)
    bond_re, bond_im = complex_mul(diag_re, diag_im, next_re, next_im)
    live_rows = alive[:, None]
    density_term = -inv_pi * jnp.sum(weights[None, :, None] * diag_im, axis=1) * live_rows
    bond_term = (
        -2.0 * inv_pi * jnp.sum(weights[None, :, None] * square * bond_im, axis=1) * live_rows
    )
    density, bond_density = (
        lax.psum_scatter(density_term, "energy", scatter_dimension=1, tiled=True),
        lax.psum_scatter(bond_term, "energy", scatter_dimension=1, tiled=True),
    )
    return (density, bond_density)


def solution(mesh):
    in_specs = (
        P(),
        P("slab", None),
        P("slab", None),
        P(),
        P("energy"),
        P("energy"),
        P("energy", None, None),
        P("energy", None, None),
    )
    out_specs = (P("slab", "energy"), P("slab", "energy"))
    return jax.shard_map(shards, mesh=mesh, in_specs=in_specs, out_specs=out_specs, check_vma=False)
```

profile of v0, /device:TPU:0, one launch (start us, length us, event | category | flops | bytes accessed | tf_op | source)
XLA Modules:
  0.0 419.4 jit_solution(17910417154877079605)
XLA Ops:
  7.3 0.9 broadcast_in_dim.206
  13.9 0.8 copy-done.5
  15.0 47.2 %while.103 = (s32[]{:T(128)}, f32[4,1024]{1,0:T(4,128)S(1)}, f32[4,1024]{1,0:T(4,128)S(1)}, f32[4,1024]{1,0:T(4,128)S(1)}, f32[4,1024]{1,0:T(4,128)S(1)}, /*inde...) while((s32[]{:T(128)}, f32[4,1024]{1,0:T(4,128)S(1)}, ...), condition=%wide.region_1.2_spmd.clone, body=%wide.region_0.1_spmd.clone.sunk | while | flops 455688 | bytes 573684 | solution.py:147
  62.2 23.8 %all-gather.10 = f32[16,4,1024]{2,1,0:T(4,128)S(1)} all-gather(f32[1,4,1024]{2,1,0:T(4,128)S(1)} %bitcast.357), channel_id=5, replica_groups=mesh['slab'=16,'energy'=2] {'slab'}, dimensions={0}, use_global_device_ids=true | all-gather | bytes 278528 | tf_op jit(solution)/shard_map/all_gather | solution.py:14
  86.0 18.1 %all-gather.11 = f32[16,4,1024]{2,1,0:T(4,128)S(1)} all-gather(f32[1,4,1024]{2,1,0:T(4,128)S(1)} %bitcast.354), channel_id=6, replica_groups=mesh['slab'=16,'energy'=2] {'slab'}, dimensions={0}, use_global_device_ids=true | all-gather | bytes 278528 | tf_op jit(solution)/shard_map/all_gather | solution.py:14
  104.1 19.5 %all-gather.12 = f32[16,4,1024]{2,1,0:T(4,128)S(1)} all-gather(f32[1,4,1024]{2,1,0:T(4,128)S(1)} %bitcast.355), channel_id=7, replica_groups=mesh['slab'=16,'energy'=2] {'slab'}, dimensions={0}, use_global_device_ids=true | all-gather | bytes 278528 | tf_op jit(solution)/shard_map/all_gather | solution.py:14
  123.6 18.1 %all-gather.13 = f32[16,4,1024]{2,1,0:T(4,128)S(1)} all-gather(f32[1,4,1024]{2,1,0:T(4,128)S(1)} %bitcast.347), channel_id=8, replica_groups=mesh['slab'=16,'energy'=2] {'slab'}, dimensions={0}, use_global_device_ids=true | all-gather | bytes 278528 | tf_op jit(solution)/shard_map/all_gather | solution.py:14
  141.7 19.5 %all-gather.8 = f32[16,4,1024]{2,1,0:T(4,128)S(1)} all-gather(f32[1,4,1024]{2,1,0:T(4,128)S(1)} %bitcast.346), channel_id=2, replica_groups=mesh['slab'=16,'energy'=2] {'slab'}, dimensions={0}, use_global_device_ids=true | all-gather | bytes 278528 | tf_op jit(solution)/shard_map/all_gather | solution.py:14
  161.2 18.1 %all-gather.9 = f32[16,4,1024]{2,1,0:T(4,128)S(1)} all-gather(f32[1,4,1024]{2,1,0:T(4,128)S(1)} %bitcast.356), channel_id=4, replica_groups=mesh['slab'=16,'energy'=2] {'slab'}, dimensions={0}, use_global_device_ids=true | all-gather | bytes 278528 | tf_op jit(solution)/shard_map/all_gather | solution.py:14
  179.3 18.9 %all-gather.14 = f32[16,1,1024]{2,1,0:T(1,128)S(1)} all-gather(f32[1,1,1024]{2,1,0:T(1,128)S(1)} %bitcast.364), channel_id=9, replica_groups=mesh['slab'=16,'energy'=2] {'slab'}, dimensions={0}, use_global_device_ids=true | all-gather | bytes 69632 | tf_op jit(solution)/shard_map/all_gather | solution.py:14
  200.0 30.4 %all-reduce = f32[16]{0:T(128)} all-reduce(f32[16]{0:T(128)S(1)} %bitcast_dynamic-update-slice_fusion.4), channel_id=3, replica_groups=mesh['slab'=16,'energy'=2] {'slab'}, use_global_device_ids=true, to_apply=%add | all-reduce | flops 16 | bytes 128
  232.6 48.5 %while.104 = (s32[]{:T(128)}, f32[4,1024]{1,0:T(4,128)S(1)}, f32[4,1024]{1,0:T(4,128)S(1)}, f32[1,1024]{1,0:T(1,128)S(1)}, f32[1,1]{1,0:T(1,128)}, /*index=5*/s3...) while((s32[]{:T(128)}, f32[4,1024]{1,0:T(4,128)S(1)}, ...), condition=%wide.region_3.4_spmd.clone, body=%wide.region_2.3_spmd.clone.sunk | while | flops 186378 | bytes 193068 | solution.py:26
  281.2 30.5 %while.101 = (s32[]{:T(128)}, f32[4,1024]{1,0:T(4,128)S(1)}, f32[4,1024]{1,0:T(4,128)S(1)}, f32[1,1024]{1,0:T(1,128)S(1)}, f32[16,4,1024]{2,1,0:T(4,128)S(1)}, /...) while((s32[]{:T(128)}, f32[4,1024]{1,0:T(4,128)S(1)}, ...), condition=%wide.region_5.6_spmd, body=%wide.region_4.5_spmd.sunk | while | flops 51203 | bytes 250004 | solution.py:163
  311.8 47.1 %while.105 = (s32[]{:T(128)}, f32[4,1024]{1,0:T(4,128)S(1)}, f32[4,1024]{1,0:T(4,128)S(1)}, f32[1,1]{1,0:T(1,128)}, s32[]{:T(128)}, /*index=5*/f32[16,1,1]{0,2,1...) while((s32[]{:T(128)}, f32[4,1024]{1,0:T(4,128)S(1)}, ...), condition=%wide.region_7.8_spmd.clone, body=%wide.region_6.7_spmd.clone.sunk | while | flops 182282 | bytes 188676 | solution.py:26
  313.0 0.8 select_select_fusion.11
  316.2 0.8 select_select_fusion.11
  319.3 0.8 select_select_fusion.11
  322.5 0.8 select_select_fusion.11
  325.6 0.8 select_select_fusion.11
  328.7 0.8 select_select_fusion.11
  331.9 0.8 select_select_fusion.11
  335.0 0.8 select_select_fusion.11
  338.2 0.8 select_select_fusion.11
  341.3 0.8 select_select_fusion.11
  344.5 0.8 select_select_fusion.11
  347.6 0.8 select_select_fusion.11
  350.7 0.8 select_select_fusion.11
  353.9 0.8 select_select_fusion.11
  357.0 0.8 select_select_fusion.11
  359.1 31.9 %while.102 = (s32[]{:T(128)}, f32[4,1024]{1,0:T(4,128)S(1)}, f32[4,1024]{1,0:T(4,128)S(1)}, f32[16,4,1024]{2,1,0:T(4,128)S(1)}, f32[16,4,1024]{2,1,0:T(4,128)S(1...) while((s32[]{:T(128)}, f32[4,1024]{1,0:T(4,128)S(1)}, ...), condition=%wide.region_9.10_spmd, body=%wide.region_8.9_spmd.sunk | while | flops 50180 | bytes 176291 | solution.py:164
  394.1 5.9 %reduce-scatter.5.cloned.1.call-done = f32[16,512]{1,0:T(8,128)} async-done(((f32[16,1024]{1,0:T(8,128)}), f32[16,512]{1,0:T(8,128)}) %reduce-scatter.5.cloned.1.call-update) | async-done | bytes 32784 | tf_op jit(solution)/shard_map/reduce_scatter | solution.py:177
  399.9 12.7 %reduce-scatter.3.cloned.1.call-done = f32[16,512]{1,0:T(8,128)} async-done(((f32[16,1024]{1,0:T(8,128)}), f32[16,512]{1,0:T(8,128)}) %reduce-scatter.3.cloned.1.call-update) | async-done | bytes 32784 | tf_op jit(solution)/shard_map/reduce_scatter | solution.py:176
  (434 shorter events, 97.1 us)
Async XLA Ops:
  7.2 392.8 %reduce-scatter.5.cloned.1.call-start = ((), (), s32[]{:S(2)}) async-start(), calls=%async_computation.3 | async-start | bytes 98304 | tf_op jit(solution)/shard_map/reduce_scatter | solution.py:177
  7.3 1.0 copy-start.2
  8.3 4.1 copy-start.6
  9.0 0.7 copy-start.9
  12.4 0.8 copy-start.7
  13.2 0.7 copy-start.10
  13.8 0.8 copy-start.5
  13.8 0.8 copy-start.8
  62.2 23.8 %copy-start.4 = (f32[16,1,1024]{2,1,0:T(1,128)}, f32[16,1,1024]{2,1,0:T(1,128)S(1)}, u32[]{:S(2)}) copy-start(f32[16,1,1024]{2,1,0:T(1,128)S(1)} %get-tuple-element.1810) | copy-start | bytes 196612
  198.2 0.7 copy-start.12
  232.6 0.6 copy-start.13
  235.8 0.6 copy-start.13
  239.1 0.6 copy-start.13
  242.3 0.6 copy-start.13
  245.5 0.6 copy-start.13
  248.7 0.6 copy-start.13
  252.0 0.6 copy-start.13
  255.2 0.6 copy-start.13
  258.4 0.6 copy-start.13
  261.7 0.6 copy-start.13
  264.9 0.6 copy-start.13
  268.1 0.6 copy-start.13
  271.4 0.6 copy-start.13
  274.6 0.6 copy-start.13
  277.8 0.6 copy-start.13
  281.2 30.5 %copy-start.3 = (f32[16,1,1024]{2,0,1:T(8,128)S(1)}, f32[16,1,1024]{2,0,1:T(8,128)}, u32[]{:S(2)}) copy-start(f32[16,1,1024]{2,0,1:T(8,128)} %copy.32) | copy-start | bytes 196612
  359.1 32.0 %copy-start.11 = (s32[4]{0:T(128)S(1)}, s32[4]{0:T(128)}, u32[]{:S(2)}) copy-start(s32[4]{0:T(128)} %param.23) | copy-start | bytes 52
  359.1 32.0 %copy-start = (f32[16,1024]{1,0:T(8,128)S(1)}, f32[16,1024]{1,0:T(8,128)}, u32[]{:S(2)}) copy-start(f32[16,1024]{1,0:T(8,128)} %get-tuple-element.1140) | copy-start | bytes 196612
  359.1 32.0 %copy-start.1 = (f32[16,1024]{1,0:T(8,128)S(1)}, f32[16,1024]{1,0:T(8,128)}, u32[]{:S(2)}) copy-start(f32[16,1024]{1,0:T(8,128)} %get-tuple-element.1141) | copy-start | bytes 196612
  392.6 20.0 %reduce-scatter.3.cloned.1.call-start = ((), (), s32[]{:S(2)}) async-start(), calls=%async_computation.2 | async-start | bytes 98304 | tf_op jit(solution)/shard_map/reduce_scatter | solution.py:176
Sparse Core Ops, SparseCore 0:
  392.7 7.1 reduce-scatter.4
  402.7 9.8 reduce-scatter.2
where the time goes:
time: 423 us; the launch traced here: 419 us
  blocking collectives  166 us (39%)
  loops' own time  109 us (26%)
  local copies, waits for them, and re-layouts  64.7 us (15%)
  other arithmetic  45.9 us (11%)
  waiting for transfers between devices  18.5 us (4%)
  between operations  15.2 us (4%)
    all_gather x7, blocking collectives, entering(): pieces = jax.tree.map(lambda part: lax.all_gather(part, axis), value)  136 us
    another operation x2, loops' own time, entering(): return lax.fori_loop(0, count - 1, turn, subtotal)  54.9 us
    another operation x1, loops' own time, shards(): summary, _ = lax.scan(fold_slot, empty, xs)  33.4 us
    unnamed x1, blocking collectives  30.4 us
    dynamic_slice x48, local copies, waits for them, and re-layouts, shards(): summary, _ = lax.scan(fold_slot, empty, xs)  28.8 us
    dynamic_slice x30, local copies, waits for them, and re-layouts, turn(): longer = join(subtotal, jax.tree.map(lambda part: part[position], pieces))  17.7 us
    select_n x30, other arithmetic, turn(): jnp.where(position < mine, new, old)  13.2 us
    reduce_scatter x1, waiting for transfers between devices, shards(): lax.psum_scatter(density_term, 'energy', scatter_dimension=1, tiled=True)  12.7 us
  transfers between devices with their start and end apart: 2, of which 2 were waited for; matrix products, arithmetic and copies ran while one was open for 0% of the time, Pallas kernels for 0%

commit v1 on v0

v1 whole, which is shorter than its diff:
```python
import jax
import jax.numpy as jnp
from jax import lax
from jax.sharding import PartitionSpec as P

broaden = 0.002
e_low = -1.5
e_step = 3.0 / 4096.0
inv_pi = 1.0 / 3.141592653589793


def reciprocal(real_part, imag_part):
    norm = real_part * real_part + imag_part * imag_part
    return (real_part / norm, -imag_part / norm)


def complex_mul(first_re, first_im, second_re, second_im):
    return (
        first_re * second_re - first_im * second_im,
        first_re * second_im + first_im * second_re,
    )


def join_segments(left, right):
    square = left[6] * left[6]
    mix_re, mix_im = complex_mul(left[4], left[5], right[0], right[1])
    inv_re, inv_im = reciprocal(1.0 - square * mix_re, -square * mix_im)
    left_sq_re, left_sq_im = complex_mul(left[2], left[3], left[2], left[3])
    head_re, head_im = complex_mul(left_sq_re, left_sq_im, right[0], right[1])
    head_re, head_im = complex_mul(head_re, head_im, inv_re, inv_im)
    right_sq_re, right_sq_im = complex_mul(right[2], right[3], right[2], right[3])
    tail_re, tail_im = complex_mul(right_sq_re, right_sq_im, left[4], left[5])
    tail_re, tail_im = complex_mul(tail_re, tail_im, inv_re, inv_im)
    link_re, link_im = complex_mul(left[2], left[3], right[2], right[3])
    link_re, link_im = complex_mul(link_re, link_im, inv_re, inv_im)
    return (
        left[0] + square * head_re,
        left[1] + square * head_im,
        left[6] * link_re,
        left[6] * link_im,
        right[4] + square * tail_re,
        right[5] + square * tail_im,
        right[6],
    )


def forward_pass(onsite_re, onsite_im, hopping, live, start_re, start_im, start_coupling):
    prev_re, prev_im, prev_coupling = start_re, start_im, start_coupling
    out_re, out_im = [], []
    for slot in range(onsite_re.shape[0]):
        square = prev_coupling * prev_coupling
        g_re, g_im = reciprocal(onsite_re[slot] - square * prev_re, onsite_im[slot] - square * prev_im)
        out_re.append(g_re)
        out_im.append(g_im)
        keep = live[slot]
        prev_re = jnp.where(keep, g_re, prev_re)
        prev_im = jnp.where(keep, g_im, prev_im)
        prev_coupling = jnp.where(keep, hopping[slot], prev_coupling)
    return out_re, out_im


def backward_pass(onsite_re, onsite_im, hopping, live, start_re, start_im):
    next_re, next_im = start_re, start_im
    out_re, out_im = [None] * onsite_re.shape[0], [None] * onsite_re.shape[0]
    for slot in reversed(range(onsite_re.shape[0])):
        out_re[slot], out_im[slot] = next_re, next_im
        square = hopping[slot] * hopping[slot]
        g_re, g_im = reciprocal(onsite_re[slot] - square * next_re, onsite_im[slot] - square * next_im)
        keep = live[slot]
        next_re = jnp.where(keep, g_re, next_re)
        next_im = jnp.where(keep, g_im, next_im)
    return out_re, out_im, next_re, next_im


def shards(
    mode_floor, onsite_noise, hopping, lengths, energy_index, weight_code, lead_shift, lead_width
):
    slots = onsite_noise.shape[0]
    modes = onsite_noise.shape[1]
    points = energy_index.shape[0]
    here = lax.axis_index("slab")
    devices = lax.axis_size("slab")
    count = lengths[here]
    place = jnp.arange(slots, dtype=jnp.int32)
    live = [place[slot] < count for slot in range(slots)]
    alive = (place < count).astype(jnp.float32)
    first_on = ((here == 0) & (place == 0)).astype(jnp.float32)[:, None, None]
    last_on = ((here == devices - 1) & (place == count - 1)).astype(jnp.float32)[:, None, None]
    energies = e_low + e_step * energy_index.astype(jnp.float32)
    weights = weight_code.astype(jnp.float32) / (32.0 * points * lax.axis_size("energy"))
    levels = mode_floor[None, :] + onsite_noise
    onsite_re = (
        energies[None, :, None]
        - levels[:, None, :]
        - first_on * lead_shift[None, :, 0, :]
        - last_on * lead_shift[None, :, 1, :]
    )
    onsite_im = broaden + first_on * lead_width[None, :, 0, :] + last_on * lead_width[None, :, 1, :]
    onsite_im = onsite_im + jnp.zeros_like(onsite_re)
    coupling_rows = hopping[:, None, :]
    zero = jnp.zeros((points, modes), jnp.float32)
    zero_row = jnp.zeros((1, modes), jnp.float32)

    def single(slot):
        g_re, g_im = reciprocal(onsite_re[slot], onsite_im[slot])
        return (g_re, g_im, g_re, g_im, g_re, g_im, coupling_rows[slot])

    summary = single(0)
    for slot in range(1, slots):
        joined = join_segments(summary, single(slot))
        summary = tuple(jnp.where(live[slot], new, old) for new, old in zip(joined, summary))
    first_re, first_im, cross_re, cross_im, final_re, final_im, coupling = summary

    packed = jnp.concatenate(
        [first_re, first_im, cross_re, cross_im, final_re, final_im, coupling], axis=0
    )
    every = lax.all_gather(packed, "slab")

    def part(device, index):
        return every[device, index * points:(index + 1) * points]

    into_re, into_im, into_coupling = zero, zero, zero_row
    run_re, run_im = zero, zero
    for device in range(devices - 1):
        pp = every[device - 1, 6 * points:6 * points + 1] if device > 0 else zero_row
        pp = pp * pp
        c_re, c_im = complex_mul(part(device, 2), part(device, 3), part(device, 2), part(device, 3))
        m_re, m_im = complex_mul(run_re, run_im, part(device, 0), part(device, 1))
        inv_re, inv_im = reciprocal(1.0 - pp * m_re, -pp * m_im)
        t_re, t_im = complex_mul(c_re, c_im, run_re, run_im)
        t_re, t_im = complex_mul(t_re, t_im, inv_re, inv_im)
        run_re = part(device, 4) + pp * t_re
        run_im = part(device, 5) + pp * t_im
        take = device + 1 == here
        into_re = jnp.where(take, run_re, into_re)
        into_im = jnp.where(take, run_im, into_im)
        into_coupling = jnp.where(take, every[device, 6 * points:6 * points + 1], into_coupling)
    from_re, from_im = zero, zero
    run_re, run_im = zero, zero
    for device in range(devices - 1, 0, -1):
        pp = every[device, 6 * points:6 * points + 1]
        pp = pp * pp
        c_re, c_im = complex_mul(part(device, 2), part(device, 3), part(device, 2), part(device, 3))
        m_re, m_im = complex_mul(part(device, 4), part(device, 5), run_re, run_im)
        inv_re, inv_im = reciprocal(1.0 - pp * m_re, -pp * m_im)
        h_re, h_im = complex_mul(c_re, c_im, run_re, run_im)
        h_re, h_im = complex_mul(h_re, h_im, inv_re, inv_im)
        run_re = part(device, 0) + pp * h_re
        run_im = part(device, 1) + pp * h_im
        take = device - 1 == here
        from_re = jnp.where(take, run_re, from_re)
        from_im = jnp.where(take, run_im, from_im)

    left_re, left_im = forward_pass(
        onsite_re, onsite_im, coupling_rows, live, into_re, into_im, into_coupling
    )
    next_re, next_im, _, _ = backward_pass(onsite_re, onsite_im, coupling_rows, live, from_re, from_im)
    left_re, left_im = jnp.stack(left_re), jnp.stack(left_im)
    next_re, next_im = jnp.stack(next_re), jnp.stack(next_im)
    square = coupling_rows * coupling_rows
    mix_re, mix_im = complex_mul(left_re, left_im, next_re, next_im)
    inv_re, inv_im = reciprocal(1.0 - square * mix_re, -square * mix_im)
    diag_re, diag_im = complex_mul(left_re, left_im, inv_re, inv_im)
    bond_re, bond_im = complex_mul(diag_re, diag_im, next_re, next_im)
    live_rows = alive[:, None]
    density_term = -inv_pi * jnp.sum(weights[None, :, None] * diag_im, axis=1) * live_rows
    bond_term = (
        -2.0 * inv_pi * jnp.sum(weights[None, :, None] * square * bond_im, axis=1) * live_rows
    )
    both = lax.psum_scatter(
        jnp.stack([density_term, bond_term]), "energy", scatter_dimension=2, tiled=True
    )
    return (both[0], both[1])


def solution(mesh):
    in_specs = (
        P(),
        P("slab", None),
        P("slab", None),
        P(),
        P("energy"),
        P("energy"),
        P("energy", None, None),
        P("energy", None, None),
    )
    out_specs = (P("slab", "energy"), P("slab", "energy"))
    return jax.shard_map(shards, mesh=mesh, in_specs=in_specs, out_specs=out_specs, check_vma=False)
```

time: 423 us -> 122 us (0.29)
  blocking collectives: 166 us -> 0 us
  loops' own time: 109 us -> 0 us
  local copies, waits for them, and re-layouts: 64.7 us -> 10.4 us
  waiting for transfers between devices: 18.5 us -> 51.3 us
  other arithmetic: 45.9 us -> 22.8 us
  between operations: 15.2 us -> 35.9 us
    all_gather x7 -> x0, blocking collectives: 136 us -> none  [entering(): pieces = jax.tree.map(lambda part: lax.all_gather(part, axis), value)]
    another operation x5 -> x0, loops' own time: 109 us -> none  [the longest x2 54.9 us: entering(): return lax.fori_loop(0, count - 1, turn, subtotal)]
    dynamic_slice x78 -> x0, local copies, waits for them, and re-layouts: 46.5 us -> none  [the longest x48 28.8 us: shards(): summary, _ = lax.scan(fold_slot, empty, xs)]
    all_gather x0 -> x1, waiting for transfers between devices: none -> 42 us  [shards(): every = lax.all_gather(packed, 'slab')]
    unnamed x1 -> x0, blocking collectives: 30.4 us -> none
    select_n x126 -> x25, other arithmetic: 28 us -> 4.71 us  [the longest x6 2.95 us: shards(): jnp.where(live[slot], new, old)]
    reduce_scatter x2 -> x1, waiting for transfers between devices: 18.5 us -> 9.2 us  [shards(): lax.psum_scatter(jnp.stack([density_term, bond_term]), 'energy', scatter_...]
    while x46 -> x0, local copies, waits for them, and re-layouts: 9.22 us -> none
  transfers between devices with their start and end apart: 2 -> 2, of which waited for: 2 -> 2; matrix products, arithmetic and copies ran while one was open for 0% -> 1% of each run, Pallas kernels for 0% -> 0%
where the time goes in v1:
time: 122 us; the launch traced here: 121 us
  waiting for transfers between devices  51.3 us (42%)
  between operations  35.9 us (29%)
  other arithmetic  22.8 us (19%)
  local copies, waits for them, and re-layouts  10.4 us (9%)
    all_gather x1, waiting for transfers between devices, shards(): every = lax.all_gather(packed, 'slab')  42 us
    reduce_scatter x1, waiting for transfers between devices, shards(): lax.psum_scatter(jnp.stack([density_term, bond_term]), 'energy', scatter_...  9.2 us
    mul x50, other arithmetic, shards(): inv_re, inv_im = reciprocal(1.0 - pp * m_re, -pp * m_im)  6.64 us
    sub x51, other arithmetic, complex_mul(): first_re * second_re - first_im * second_im  2.97 us
    select_n x6, other arithmetic, shards(): jnp.where(live[slot], new, old)  2.95 us
    concatenate x1, local copies, waits for them, and re-layouts, shards(): jnp.concatenate([first_re, first_im, cross_re, cross_im, final_re, final_...  2.48 us
  transfers between devices with their start and end apart: 2, of which 2 were waited for; matrix products, arithmetic and copies ran while one was open for 1% of the time, Pallas kernels for 0%

profile of v1, /device:TPU:0, one launch (start us, length us, event | category | flops | bytes accessed | tf_op | source)
XLA Modules:
  0.0 120.6 jit_solution(9528126628747074279)
XLA Ops:
  7.2 0.7 fusion.407
  7.9 1.2 %dynamic_slice.3 = s32[1]{0:T(128)} dynamic-slice(s32[16]{0:T(128)} %param.11, s32[]{:T(128)S(6)} %select_n.2712), dynamic_slice_sizes={1} | dynamic-slice | bytes 12 | tf_op jit(solution)/shard_map/dynamic_slice | solution.py:83
  27.6 0.9 fusion.405
  29.1 0.9 fusion.406
  30.0 0.7 multiply_add_fusion.251
  30.6 1.0 slice_multiply_fusion.29
  31.6 1.3 %broadcast_select_fusion.28 = (f32[1,1024]{1,0:T(1,128)S(1)}, f32[1,1024]{1,0:T(1,128)S(1)}, f32[1,1024]{1,0:T(1,128)S(1)}, f32[1,1024]{1,0:T(1,128)S(1)}, f32[1...) fusion(pred[]{:T(512)S(6)} %lt.62, ...), kind=kLoop, calls=%fused_computation.1582 | loop fusion | flops 15360 | bytes 126991 | tf_op jit(solution)/shard_map/jit(_where)/select_n | solution.py:111
  33.0 0.9 broadcast_add_fusion
  35.3 0.4 multiply_select_fusion
  35.8 0.5 add_select_fusion.15
  36.3 0.5 add_select_fusion
  36.9 2.5 %concatenate.3 = f32[25,1024]{1,0:T(8,128)} concatenate(f32[4,1024]{1,0:T(4,128)S(1)} %add_select_fusion.15, f32[4,1024]{1,0:T(4,128)S(1)} %add_select_fusion, f32[4,1024]{1,0:T(4,128)S(1)} %get-tuple-element.638, f32[4,1024]{1,0:T(4,128)S(1)} %get-tuple-element.362, f32[4,1024]{1,0:T(4,128)S(1)} %get-tuple-element.637, f32[4,1024]{1,0:T(4,128)S(1)} %get-tuple-element.359, ...), dimensions={0} | concatenate | bytes 204800 | tf_op jit(solution)/shard_map/concatenate | solution.py:114
  41.0 0.6 compare_select_fusion
  41.7 42.0 %all-gather.4.cloned.1.call-done = f32[16,25,1024]{2,1,0:T(8,128)} async-done(((f32[1,25,1024]{2,1,0:T(8,128)}), f32[16,25,1024]{2,1,0:T(8,128)}) %all-gather.4.cloned.1.call-update) | async-done | bytes 1638416 | tf_op jit(solution)/shard_map/all_gather | solution.py:117
  83.7 1.2 slice_multiply_fusion.5
  85.1 1.1 fusion.336
  86.3 1.0 add_multiply_fusion.58
  87.3 0.9 multiply_subtract_fusion.43
  88.1 0.9 fusion.12
  89.0 0.9 fusion.25
  89.9 0.9 add_multiply_fusion.57
  90.8 0.9 fusion.22
  91.7 1.0 fusion.199
  93.7 0.4 divide_select_fusion
  100.4 0.4 stack.175
  100.8 0.4 stack.155
  101.2 0.4 stack.183
  101.6 0.4 stack.165
  102.0 0.3 multiply_reduce_fusion.1
  102.5 0.7 pad_maximum_fusion
  103.1 9.2 %reduce-scatter.2.cloned.1.call-done = f32[2,16,512]{2,1,0:T(8,128)} async-done(((f32[2,16,1024]{2,1,0:T(8,128)}), f32[2,16,512]{2,1,0:T(8,128)}) %reduce-scatter.2.cloned.1.call-update) | async-done | bytes 65552 | tf_op jit(solution)/shard_map/reduce_scatter | solution.py:170
  112.3 1.4 %slice_bitcast_fusion = (f32[16,512]{1,0:T(8,128)}, f32[16,512]{1,0:T(8,128)}) fusion(f32[2,16,512]{2,1,0:T(8,128)} %reduce-scatter.2.cloned.1.call-done), kind=kLoop, calls=%fused_computation.13 | loop fusion | bytes 131072 | tf_op jit(solution)/shard_map/squeeze | solution.py:173
  (245 shorter events, 8.4 us)
Async XLA Ops:
  7.2 76.5 %all-gather.4.cloned.1.call-start = ((), (), s32[]{:S(2)}) async-start(), calls=%async_computation.2 | async-start | bytes 2228224 | tf_op jit(solution)/shard_map/all_gather | solution.py:117
  35.8 5.8 %copy-start.2 = (s32[4]{0:T(128)S(1)}, s32[4]{0:T(128)}, u32[]{:S(2)}) copy-start(s32[4]{0:T(128)} %param.13) | copy-start | bytes 52
  35.8 5.8 %copy-start.1 = (f32[16,1024]{1,0:T(8,128)S(1)}, f32[16,1024]{1,0:T(8,128)}, u32[]{:S(2)}) copy-start(f32[16,1024]{1,0:T(8,128)} %param.10) | copy-start | bytes 196612
  39.4 72.9 %reduce-scatter.2.cloned.1.call-start = ((), (), s32[]{:S(2)}) async-start(), calls=%async_computation.1 | async-start | bytes 196608 | tf_op jit(solution)/shard_map/reduce_scatter | solution.py:170
  83.7 8.9 %copy-start = (f32[16,25,1024]{2,1,0:T(8,128)S(1)}, f32[16,25,1024]{2,1,0:T(8,128)}, u32[]{:S(2)}) copy-start(f32[16,25,1024]{2,1,0:T(8,128)} %all-gather.4.cloned.1.call-done) | copy-start | bytes 4915204
Sparse Core Ops, SparseCore 0:
  39.6 44.0 all-gather.3
  103.3 9.0 reduce-scatter.1

commit v2 on v1

v2 whole, which is shorter than its diff:
```python
import jax
import jax.numpy as jnp
from jax import lax
from jax.experimental import pallas as pl
from jax.experimental.pallas import tpu as pltpu
from jax.sharding import PartitionSpec as P

broaden = 0.002
e_low = -1.5
e_step = 3.0 / 4096.0
inv_pi = 1.0 / 3.141592653589793


def reciprocal(real_part, imag_part):
    norm = real_part * real_part + imag_part * imag_part
    return (real_part / norm, -imag_part / norm)


def complex_mul(first_re, first_im, second_re, second_im):
    return (
        first_re * second_re - first_im * second_im,
        first_re * second_im + first_im * second_re,
    )


def join_segments(left, right):
    square = left[6] * left[6]
    mix_re, mix_im = complex_mul(left[4], left[5], right[0], right[1])
    inv_re, inv_im = reciprocal(1.0 - square * mix_re, -square * mix_im)
    left_sq_re, left_sq_im = complex_mul(left[2], left[3], left[2], left[3])
    head_re, head_im = complex_mul(left_sq_re, left_sq_im, right[0], right[1])
    head_re, head_im = complex_mul(head_re, head_im, inv_re, inv_im)
    right_sq_re, right_sq_im = complex_mul(right[2], right[3], right[2], right[3])
    tail_re, tail_im = complex_mul(right_sq_re, right_sq_im, left[4], left[5])
    tail_re, tail_im = complex_mul(tail_re, tail_im, inv_re, inv_im)
    link_re, link_im = complex_mul(left[2], left[3], right[2], right[3])
    link_re, link_im = complex_mul(link_re, link_im, inv_re, inv_im)
    return (
        left[0] + square * head_re,
        left[1] + square * head_im,
        left[6] * link_re,
        left[6] * link_im,
        right[4] + square * tail_re,
        right[5] + square * tail_im,
        right[6],
    )


def summary_kernel(count_ref, are_ref, aim_ref, hop_ref, out_ref):
    points = are_ref.shape[1]

    def single(slot):
        g_re, g_im = reciprocal(are_ref[slot], aim_ref[slot])
        return (g_re, g_im, g_re, g_im, g_re, g_im, hop_ref[slot])

    def body(slot, summary):
        return join_segments(summary, single(slot))

    summary = lax.fori_loop(1, count_ref[0], body, single(0))
    for field in range(6):
        out_ref[field * points:(field + 1) * points] = summary[field]
    out_ref[6 * points] = summary[6]


def final_kernel(
    here_ref, count_ref, weight_ref, every_ref, are_ref, aim_ref, hop_ref,
    dens_ref, bond_ref, left_re_ref, left_im_ref,
):
    points = are_ref.shape[1]
    devices = every_ref.shape[0]
    here = here_ref[0]
    count = count_ref[0]

    def field(device, index):
        return every_ref[device, index * points:(index + 1) * points]

    def coupling_of(device):
        return every_ref[device, 6 * points]

    def into_body(device, run):
        run_re, run_im = run
        pp = coupling_of(jnp.maximum(device - 1, 0))
        pp = pp * pp
        c_re, c_im = complex_mul(field(device, 2), field(device, 3), field(device, 2), field(device, 3))
        m_re, m_im = complex_mul(run_re, run_im, field(device, 0), field(device, 1))
        inv_re, inv_im = reciprocal(1.0 - pp * m_re, -pp * m_im)
        t_re, t_im = complex_mul(c_re, c_im, run_re, run_im)
        t_re, t_im = complex_mul(t_re, t_im, inv_re, inv_im)
        return (field(device, 4) + pp * t_re, field(device, 5) + pp * t_im)

    zero = jnp.zeros(are_ref.shape[1:], jnp.float32)
    into_re, into_im = lax.fori_loop(0, here, into_body, (zero, zero))
    into_coupling = coupling_of(jnp.maximum(here - 1, 0))

    def from_body(step, run):
        run_re, run_im = run
        device = devices - 1 - step
        pp = coupling_of(device)
        pp = pp * pp
        c_re, c_im = complex_mul(field(device, 2), field(device, 3), field(device, 2), field(device, 3))
        m_re, m_im = complex_mul(field(device, 4), field(device, 5), run_re, run_im)
        inv_re, inv_im = reciprocal(1.0 - pp * m_re, -pp * m_im)
        h_re, h_im = complex_mul(c_re, c_im, run_re, run_im)
        h_re, h_im = complex_mul(h_re, h_im, inv_re, inv_im)
        return (field(device, 0) + pp * h_re, field(device, 1) + pp * h_im)

    from_re, from_im = lax.fori_loop(0, devices - 1 - here, from_body, (zero, zero))

    def forward_body(slot, carry):
        prev_re, prev_im, prev_coupling = carry
        square = prev_coupling * prev_coupling
        g_re, g_im = reciprocal(are_ref[slot] - square * prev_re, aim_ref[slot] - square * prev_im)
        left_re_ref[slot] = g_re
        left_im_ref[slot] = g_im
        return (g_re, g_im, hop_ref[slot])

    lax.fori_loop(0, count, forward_body, (into_re, into_im, into_coupling))
    dens_ref[...] = jnp.zeros(dens_ref.shape, jnp.float32)
    bond_ref[...] = jnp.zeros(bond_ref.shape, jnp.float32)

    def backward_body(step, carry):
        next_re, next_im = carry
        slot = count - 1 - step
        left_re, left_im = left_re_ref[slot], left_im_ref[slot]
        square = hop_ref[slot] * hop_ref[slot]
        mix_re, mix_im = complex_mul(left_re, left_im, next_re, next_im)
        inv_re, inv_im = reciprocal(1.0 - square * mix_re, -square * mix_im)
        diag_re, diag_im = complex_mul(left_re, left_im, inv_re, inv_im)
        _, bond_im = complex_mul(diag_re, diag_im, next_re, next_im)
        dens = weight_ref[0] * diag_im[0]
        bond = weight_ref[0] * (square * bond_im[0])
        for point in range(1, points):
            dens = dens + weight_ref[point] * diag_im[point]
            bond = bond + weight_ref[point] * (square * bond_im[point])
        dens_ref[slot] = -inv_pi * dens
        bond_ref[slot] = -2.0 * inv_pi * bond
        return reciprocal(are_ref[slot] - square * next_re, aim_ref[slot] - square * next_im)

    lax.fori_loop(0, count, backward_body, (from_re, from_im))


def shards(
    mode_floor, onsite_noise, hopping, lengths, energy_index, weight_code, lead_shift, lead_width
):
    slots = onsite_noise.shape[0]
    modes = onsite_noise.shape[1]
    points = energy_index.shape[0]
    rows = modes // 128
    here = lax.axis_index("slab")
    devices = lax.axis_size("slab")
    count = lengths[here]
    place = jnp.arange(slots, dtype=jnp.int32)
    first_on = ((here == 0) & (place == 0)).astype(jnp.float32)[:, None, None, None]
    last_on = ((here == devices - 1) & (place == count - 1)).astype(jnp.float32)[:, None, None, None]
    energies = e_low + e_step * energy_index.astype(jnp.float32)
    weights = weight_code.astype(jnp.float32) / (32.0 * points * lax.axis_size("energy"))
    levels = (mode_floor[None, :] + onsite_noise).reshape(slots, 1, rows, 128)
    shift = lead_shift.reshape(1, points, 2, rows, 128)
    width = lead_width.reshape(1, points, 2, rows, 128)
    onsite_re = (
        energies[None, :, None, None]
        - levels
        - first_on * shift[:, :, 0]
        - last_on * shift[:, :, 1]
    )
    onsite_im = broaden + first_on * width[:, :, 0] + last_on * width[:, :, 1]
    onsite_im = onsite_im + jnp.zeros_like(onsite_re)
    coupling_rows = hopping.reshape(slots, rows, 128)
    count_arr = count.reshape(1)
    here_arr = here.astype(jnp.int32).reshape(1)
    smem = pl.BlockSpec(memory_space=pltpu.SMEM)
    vmem = pl.BlockSpec(memory_space=pltpu.VMEM)

    packed = pl.pallas_call(
        summary_kernel,
        out_shape=jax.ShapeDtypeStruct((6 * points + 1, rows, 128), jnp.float32),
        in_specs=[smem, vmem, vmem, vmem],
        out_specs=vmem,
    )(count_arr, onsite_re, onsite_im, coupling_rows)
    every = lax.all_gather(packed, "slab")
    density, bond_density = pl.pallas_call(
        final_kernel,
        out_shape=(
            jax.ShapeDtypeStruct((slots, rows, 128), jnp.float32),
            jax.ShapeDtypeStruct((slots, rows, 128), jnp.float32),
        ),
        in_specs=[smem, smem, smem, vmem, vmem, vmem, vmem],
        out_specs=(vmem, vmem),
        scratch_shapes=[
            pltpu.VMEM((slots, points, rows, 128), jnp.float32),
            pltpu.VMEM((slots, points, rows, 128), jnp.float32),
        ],
    )(here_arr, count_arr, weights, every, onsite_re, onsite_im, coupling_rows)
    both = jnp.stack([density.reshape(slots, modes), bond_density.reshape(slots, modes)])
    both = lax.psum_scatter(both, "energy", scatter_dimension=2, tiled=True)
    return (both[0], both[1])


def solution(mesh):
    in_specs = (
        P(),
        P("slab", None),
        P("slab", None),
        P(),
        P("energy"),
        P("energy"),
        P("energy", None, None),
        P("energy", None, None),
    )
    out_specs = (P("slab", "energy"), P("slab", "energy"))
    return jax.shard_map(shards, mesh=mesh, in_specs=in_specs, out_specs=out_specs, check_vma=False)
```

time: 122 us -> 84.5 us (0.69)
  between operations: 35.9 us -> 14.7 us
  other arithmetic: 22.8 us -> 3.73 us
  Pallas kernels: 0 us -> 7.11 us
  local copies, waits for them, and re-layouts: 10.4 us -> 7.42 us
    mul x73 -> x0, other arithmetic: 11.7 us -> none  [the longest x50 6.64 us: shards(): inv_re, inv_im = reciprocal(1.0 - pp * m_re, -pp * m_im)]
    pallas_call x0 -> x2, Pallas kernels: none -> 7.11 us  [the longest x1 3.97 us: shards(): pl.pallas_call(final_kernel, out_shape=(jax.ShapeDtypeStruct((slots, rows...]
    select_n x25 -> x0, other arithmetic: 4.71 us -> none  [the longest x6 2.95 us: shards(): jnp.where(live[slot], new, old)]
    sub x52 -> x0, other arithmetic: 3.04 us -> none  [the longest x51 2.97 us: complex_mul(): first_re * second_re - first_im * second_im]
    concatenate x1 -> x0, local copies, waits for them, and re-layouts: 2.48 us -> none  [shards(): jnp.concatenate([first_re, first_im, cross_re, cross_im, final_re, final_...]
    slice x3 -> x0, local copies, waits for them, and re-layouts: 2.44 us -> none  [the longest x1 0.87 us: shards(): lead_width[None, :, 0, :]]
    reshape x0 -> x2, local copies, waits for them, and re-layouts: none -> 1.57 us  [the longest x1 0.79 us: shards(): width = lead_width.reshape(1, points, 2, rows, 128)]
    unnamed x8 -> x4, local copies, waits for them, and re-layouts: 0.03 us -> 1.49 us
where the time goes in v2:
time: 84.5 us; the launch traced here: 83.8 us
  waiting for transfers between devices  50.7 us (60%)
  between operations  14.7 us (17%)
  local copies, waits for them, and re-layouts  7.42 us (9%)
  Pallas kernels  7.11 us (8%)
  other arithmetic  3.73 us (4%)
    all_gather x1, waiting for transfers between devices, shards(): every = lax.all_gather(packed, 'slab')  41.4 us
    reduce_scatter x1, waiting for transfers between devices, shards(): both = lax.psum_scatter(both, 'energy', scatter_dimension=2, tiled=True)  9.31 us
    pallas_call x1, Pallas kernels, shards(): pl.pallas_call(final_kernel, out_shape=(jax.ShapeDtypeStruct((slots, rows...  3.97 us
    pallas_call x1, Pallas kernels, shards(): pl.pallas_call(summary_kernel, out_shape=jax.ShapeDtypeStruct((6 * points...  3.13 us
    another operation x2, local copies, waits for them, and re-layouts, shards(): jnp.stack([density.reshape(slots, modes), bond_density.reshape(slots, mod...  1.71 us
  transfers between devices with their start and end apart: 2, of which 2 were waited for; matrix products, arithmetic and copies ran while one was open for 1% of the time, Pallas kernels for 0%

profile of v2, /device:TPU:0, one launch (start us, length us, event | category | flops | bytes accessed | tf_op | source)
XLA Modules:
  0.0 83.8 jit_solution(6994452392407703338)
XLA Ops:
  7.2 0.0 copy-start
  7.2 0.0 all-gather.3.cloned.1.call-start
  7.2 0.7 multiply_add_fusion.1
  7.9 0.8 reshape.39
  8.7 0.8 reshape.40
  9.5 0.9 %add_bitcast_fusion = f32[2,8,8,128]{3,1,2,0:T(8,128)S(1)} fusion(f32[16,1024]{1,0:T(8,128)} %param.9, f32[1024]{0:T(1024)} %param.8), kind=kLoop, calls=%fused_computation.3 | loop fusion | flops 16384 | bytes 135168
  10.3 1.5 %copy.23 = f32[2,8,8,128]{3,2,1,0:T(8,128)} copy(f32[2,8,8,128]{3,1,2,0:T(8,128)} %bitcast.32) | data formatting | bytes 131072
  11.8 1.2 %dynamic_slice.3.count_ref = s32[1]{0:T(128)} dynamic-slice(s32[16]{0:T(128)} %param.11, s32[]{:T(128)S(6)} %select_n.3), dynamic_slice_sizes={1} | dynamic-slice | bytes 12 | tf_op jit(solution)/shard_map/dynamic_slice | solution.py:151
  13.7 1.0 %multiply_add_fusion = (f32[16,4,8,128]{3,2,1,0:T(8,128)}, f32[16,4,8,128]{3,2,1,0:T(8,128)}) fusion(f32[4,8,128]{2,1,0:T(8,128)S(1)} %get-tuple-element.9, f32[4,8,128]{2,1,0:T(8,128)S(1)} %get-tuple-element.8, f32[16]{0:T(128)S(1)} %get-tuple-element.16, f32[16]{0:T(128)S(1)} %get-tuple-element.17, f32[4,8,128]{2,1,0:T(8,128)S(1)} %get-tuple-element.14, ...), kind=kLoop, calls=%fused_computation | loop fusion | flops 589824 | bytes 655504 | tf_op jit(solution)/shard_map/add | solution.py:166
  14.7 3.1 %shard_map.95 = f32[25,8,128]{2,1,0:T(8,128)} custom-call(s32[1]{0:T(128)} %dynamic_slice.3.count_ref, f32[16,4,8,128]{3,2,1,0:T(8,128)} %get-tuple-element.13.are_ref, f32[16,4,8,128]{3,2,1,0:T(8,128)} %get-tuple-element.12.aim_ref, f32[16,8,128]{2,1,0:T(8,128)} %bitcast.29), custom_call_target="tpu_custom_call" | custom-call | tf_op jit(solution)/shard_map/pallas_call | solution.py:174
  17.8 0.0 all-gather.3.cloned.1.call-update
  17.9 0.0 reduce-scatter.2.cloned.1.call-start
  17.9 0.0 copy-done
  17.9 0.6 convert_multiply_fusion.weight_ref
  18.5 41.4 %all-gather.3.cloned.1.call-done = f32[400,8,128]{2,1,0:T(8,128)} async-done(((f32[25,8,128]{2,1,0:T(8,128)}), f32[400,8,128]{2,1,0:T(8,128)}) %all-gather.3.cloned.1.call-update) | async-done | bytes 1638416 | tf_op jit(solution)/shard_map/all_gather | solution.py:180
  59.9 4.0 %shard_map.96 = (f32[16,8,128]{2,1,0:T(8,128)}, f32[16,8,128]{2,1,0:T(8,128)}) custom-call(s32[1]{0:T(128)} %bitcast.here_ref, s32[1]{0:T(128)} %dynamic_slice.3.count_ref, f32[4]{0:T(128)} %convert_multiply_fusion.weight_ref, f32[16,25,8,128]{3,2,1,0:T(8,128)} %bitcast.28, f32[16,4,8,128]{3,2,1,0:T(8,128)} %get-tuple-element.13.are_ref, ...), custom_call_target="tpu_custom_call" | custom-call | tf_op jit(solution)/shard_map/pallas_call | solution.py:181
  63.9 0.9 %stack_reshape.6 = f32[1,16,1024]{2,1,0:T(8,128)S(1)} reshape(f32[16,8,128]{2,1,0:T(8,128)} %get-tuple-element.4) | data formatting | bytes 131072 | tf_op jit(solution)/shard_map/stack;reshape | solution.py:194
  64.7 0.9 %stack_reshape.7 = f32[1,16,1024]{2,1,0:T(8,128)S(1)} reshape(f32[16,8,128]{2,1,0:T(8,128)} %get-tuple-element.5) | data formatting | bytes 131072 | tf_op jit(solution)/shard_map/stack;reshape | solution.py:194
  65.6 0.7 pad_maximum_fusion
  66.2 0.0 reduce-scatter.2.cloned.1.call-update
  66.3 9.3 %reduce-scatter.2.cloned.1.call-done = f32[2,16,512]{2,1,0:T(8,128)} async-done(((f32[2,16,1024]{2,1,0:T(8,128)}), f32[2,16,512]{2,1,0:T(8,128)}) %reduce-scatter.2.cloned.1.call-update) | async-done | bytes 65552 | tf_op jit(solution)/shard_map/reduce_scatter | solution.py:195
  75.6 1.4 %slice_bitcast_fusion = (f32[16,512]{1,0:T(8,128)}, f32[16,512]{1,0:T(8,128)}) fusion(f32[2,16,512]{2,1,0:T(8,128)} %reduce-scatter.2.cloned.1.call-done), kind=kLoop, calls=%fused_computation.4 | loop fusion | bytes 131072 | tf_op jit(solution)/shard_map/squeeze | solution.py:196
  (3 shorter events, 0.0 us)
Async XLA Ops:
  7.2 10.7 %copy-start = (s32[4]{0:T(128)S(1)}, s32[4]{0:T(128)}, u32[]{:S(2)}) copy-start(s32[4]{0:T(128)} %param.13) | copy-start | bytes 52
  7.2 52.7 %all-gather.3.cloned.1.call-start = ((), (), s32[]{:S(2)}) async-start(), calls=%async_computation.2 | async-start | bytes 1740800 | tf_op jit(solution)/shard_map/all_gather | solution.py:180
  17.9 57.7 %reduce-scatter.2.cloned.1.call-start = ((), (), s32[]{:S(2)}) async-start(), calls=%async_computation.1 | async-start | bytes 196608 | tf_op jit(solution)/shard_map/reduce_scatter | solution.py:195
Sparse Core Ops, SparseCore 0:
  18.0 41.8 all-gather.2
  66.4 9.1 reduce-scatter.1

commit v3 on v2

--- a/solution.py
+++ b/solution.py
@@ -46,8 +46,8 @@
     )
 
 
-def summary_kernel(count_ref, are_ref, aim_ref, hop_ref, out_ref):
-    points = are_ref.shape[1]
+def summary_kernel(count_ref, are_ref, aim_ref, hop_ref, *out_refs):
+    per = are_ref.shape[1] // len(out_refs)
 
     def single(slot):
         g_re, g_im = reciprocal(are_ref[slot], aim_ref[slot])
@@ -56,55 +56,59 @@
     def body(slot, summary):
         return join_segments(summary, single(slot))
 
-    summary = lax.fori_loop(1, count_ref[0], body, single(0))
-    for field in range(6):
-        out_ref[field * points:(field + 1) * points] = summary[field]
-    out_ref[6 * points] = summary[6]
-
-
-def final_kernel(
-    here_ref, count_ref, weight_ref, every_ref, are_ref, aim_ref, hop_ref,
-    dens_ref, bond_ref, left_re_ref, left_im_ref,
-):
+    first_re, first_im, cross_re, cross_im, final_re, final_im, coupling = lax.fori_loop(
+        1, count_ref[0], body, single(0)
+    )
+    square = coupling * coupling
+    sq_re, sq_im = complex_mul(cross_re, cross_im, cross_re, cross_im)
+    fields = (first_re, first_im, square * final_re, square * final_im, square * sq_re, square * sq_im)
+    for group, out_ref in enumerate(out_refs):
+        for index, value in enumerate(fields):
+            out_ref[index * per:(index + 1) * per] = value[group * per:(group + 1) * per]
+
+
+def final_kernel(here_ref, count_ref, weight_ref, *refs):
+    every_refs = refs[:len(refs) - 7]
+    are_ref, aim_ref, hop_ref, dens_ref, bond_ref, left_re_ref, left_im_ref = refs[len(refs) - 7:]
     points = are_ref.shape[1]
-    devices = every_ref.shape[0]
+    per = points // len(every_refs)
+    devices = every_refs[0].shape[0]
     here = here_ref[0]
     count = count_ref[0]
-
-    def field(device, index):
-        return every_ref[device, index * points:(index + 1) * points]
-
-    def coupling_of(device):
-        return every_ref[device, 6 * points]
-
-    def into_body(device, run):
-        run_re, run_im = run
-        pp = coupling_of(jnp.maximum(device - 1, 0))
-        pp = pp * pp
-        c_re, c_im = complex_mul(field(device, 2), field(device, 3), field(device, 2), field(device, 3))
-        m_re, m_im = complex_mul(run_re, run_im, field(device, 0), field(device, 1))
-        inv_re, inv_im = reciprocal(1.0 - pp * m_re, -pp * m_im)
-        t_re, t_im = complex_mul(c_re, c_im, run_re, run_im)
-        t_re, t_im = complex_mul(t_re, t_im, inv_re, inv_im)
-        return (field(device, 4) + pp * t_re, field(device, 5) + pp * t_im)
-
-    zero = jnp.zeros(are_ref.shape[1:], jnp.float32)
-    into_re, into_im = lax.fori_loop(0, here, into_body, (zero, zero))
-    into_coupling = coupling_of(jnp.maximum(here - 1, 0))
-
-    def from_body(step, run):
-        run_re, run_im = run
-        device = devices - 1 - step
-        pp = coupling_of(device)
-        pp = pp * pp
-        c_re, c_im = complex_mul(field(device, 2), field(device, 3), field(device, 2), field(device, 3))
-        m_re, m_im = complex_mul(field(device, 4), field(device, 5), run_re, run_im)
-        inv_re, inv_im = reciprocal(1.0 - pp * m_re, -pp * m_im)
-        h_re, h_im = complex_mul(c_re, c_im, run_re, run_im)
-        h_re, h_im = complex_mul(h_re, h_im, inv_re, inv_im)
-        return (field(device, 0) + pp * h_re, field(device, 1) + pp * h_im)
-
-    from_re, from_im = lax.fori_loop(0, devices - 1 - here, from_body, (zero, zero))
+    zero = jnp.zeros((per,) + are_ref.shape[2:], jnp.float32)
+    into_parts_re, into_parts_im, from_parts_re, from_parts_im = [], [], [], []
+    for every_ref in every_refs:
+
+        def field(device, index, every_ref=every_ref):
+            return every_ref[device, index * per:(index + 1) * per]
+
+        def into_body(device, run):
+            run_re, run_im = run
+            m_re, m_im = complex_mul(run_re, run_im, field(device, 0), field(device, 1))
+            inv_re, inv_im = reciprocal(1.0 - m_re, -m_im)
+            t_re, t_im = complex_mul(field(device, 4), field(device, 5), run_re, run_im)
+            t_re, t_im = complex_mul(t_re, t_im, inv_re, inv_im)
+            return (field(device, 2) + t_re, field(device, 3) + t_im)
+
+        def from_body(step, run):
+            run_re, run_im = run
+            device = devices - 1 - step
+            m_re, m_im = complex_mul(field(device, 2), field(device, 3), run_re, run_im)
+            inv_re, inv_im = reciprocal(1.0 - m_re, -m_im)
+            h_re, h_im = complex_mul(field(device, 4), field(device, 5), run_re, run_im)
+            h_re, h_im = complex_mul(h_re, h_im, inv_re, inv_im)
+            return (field(device, 0) + h_re, field(device, 1) + h_im)
+
+        into_re, into_im = lax.fori_loop(0, here, into_body, (zero, zero))
+        from_re, from_im = lax.fori_loop(0, devices - 1 - here, from_body, (zero, zero))
+        into_parts_re.append(into_re)
+        into_parts_im.append(into_im)
+        from_parts_re.append(from_re)
+        from_parts_im.append(from_im)
+    into_re = jnp.concatenate(into_parts_re, axis=0)
+    into_im = jnp.concatenate(into_parts_im, axis=0)
+    from_re = jnp.concatenate(from_parts_re, axis=0)
+    from_im = jnp.concatenate(from_parts_im, axis=0)
 
     def forward_body(slot, carry):
         prev_re, prev_im, prev_coupling = carry
@@ -114,7 +118,8 @@
         left_im_ref[slot] = g_im
         return (g_re, g_im, hop_ref[slot])
 
-    lax.fori_loop(0, count, forward_body, (into_re, into_im, into_coupling))
+    ones = jnp.ones(hop_ref.shape[1:], jnp.float32)
+    lax.fori_loop(0, count, forward_body, (into_re, into_im, ones))
     dens_ref[...] = jnp.zeros(dens_ref.shape, jnp.float32)
     bond_ref[...] = jnp.zeros(bond_ref.shape, jnp.float32)
 
@@ -171,26 +176,30 @@
     smem = pl.BlockSpec(memory_space=pltpu.SMEM)
     vmem = pl.BlockSpec(memory_space=pltpu.VMEM)
 
+    groups = 2 if points % 2 == 0 else 1
+    per = points // groups
     packed = pl.pallas_call(
         summary_kernel,
-        out_shape=jax.ShapeDtypeStruct((6 * points + 1, rows, 128), jnp.float32),
+        out_shape=tuple(
+            jax.ShapeDtypeStruct((6 * per, rows, 128), jnp.float32) for _ in range(groups)
+        ),
         in_specs=[smem, vmem, vmem, vmem],
-        out_specs=vmem,
+        out_specs=tuple(vmem for _ in range(groups)),
     )(count_arr, onsite_re, onsite_im, coupling_rows)
-    every = lax.all_gather(packed, "slab")
+    every = [lax.all_gather(part, "slab") for part in packed]
     density, bond_density = pl.pallas_call(
         final_kernel,
         out_shape=(
             jax.ShapeDtypeStruct((slots, rows, 128), jnp.float32),
             jax.ShapeDtypeStruct((slots, rows, 128), jnp.float32),
         ),
-        in_specs=[smem, smem, smem, vmem, vmem, vmem, vmem],
+        in_specs=[smem, smem, smem] + [vmem] * (groups + 3),
         out_specs=(vmem, vmem),
         scratch_shapes=[
             pltpu.VMEM((slots, points, rows, 128), jnp.float32),
             pltpu.VMEM((slots, points, rows, 128), jnp.float32),
         ],
-    )(here_arr, count_arr, weights, every, onsite_re, onsite_im, coupling_rows)
+    )(here_arr, count_arr, weights, *every, onsite_re, onsite_im, coupling_rows)
     both = jnp.stack([density.reshape(slots, modes), bond_density.reshape(slots, modes)])
     both = lax.psum_scatter(both, "energy", scatter_dimension=2, tiled=True)
     return (both[0], both[1])

time: 84.5 us -> 89.1 us (1.054)
  blocking collectives: 0 us -> 48.1 us
  waiting for transfers between devices: 50.7 us -> 9.33 us
  other arithmetic: 3.73 us -> 2.22 us
    all_gather x0 -> x2, blocking collectives: none -> 48.1 us  [shards(): every = [lax.all_gather(part, 'slab') for part in packed]]
    all_gather x1 -> x0, waiting for transfers between devices: 41.4 us -> none  [shards(): every = lax.all_gather(packed, 'slab')]
    unnamed x4 -> x20, local copies, waits for them, and re-layouts: 1.49 us -> 4.06 us
  transfers between devices with their start and end apart: 2 -> 1, of which waited for: 2 -> 1; matrix products, arithmetic and copies ran while one was open for 1% -> 0% of each run, Pallas kernels for 0% -> 0%
where the time goes in v3:
time: 89.1 us; the launch traced here: 88.7 us
  blocking collectives  48.1 us (54%)
  between operations  14.8 us (17%)
  waiting for transfers between devices  9.33 us (10%)
  local copies, waits for them, and re-layouts  7.8 us (9%)
  Pallas kernels  6.42 us (7%)
  other arithmetic  2.22 us (2%)
    all_gather x2, blocking collectives, shards(): every = [lax.all_gather(part, 'slab') for part in packed]  48.1 us
    reduce_scatter x1, waiting for transfers between devices, shards(): both = lax.psum_scatter(both, 'energy', scatter_dimension=2, tiled=True)  9.31 us
    unnamed x20, local copies, waits for them, and re-layouts  4.06 us
    pallas_call x1, Pallas kernels, shards(): pl.pallas_call(final_kernel, out_shape=(jax.ShapeDtypeStruct((slots, rows...  3.71 us
    pallas_call x1, Pallas kernels, shards(): pl.pallas_call(summary_kernel, out_shape=tuple((jax.ShapeDtypeStruct((6 *...  2.72 us
  transfers between devices with their start and end apart: 1, of which 1 were waited for; matrix products, arithmetic and copies ran while one was open for 0% of the time, Pallas kernels for 0%

profile of v3, /device:TPU:0, one launch (start us, length us, event | category | flops | bytes accessed | tf_op | source)
XLA Modules:
  0.0 88.7 jit_solution(11659679665803923441)
XLA Ops:
  7.2 0.0 reduce-scatter.2.cloned.1.call-start
  7.2 0.0 copy-start.6
  7.2 0.6 copy-done.6
  7.9 0.0 copy-start.7
  7.9 0.6 copy-done.7
  8.5 0.0 copy-start.4
  8.5 0.5 convert_multiply_fusion.weight_ref
  9.1 0.0 copy-start
  9.1 0.8 reshape.39
  9.9 0.0 copy-done.4
  9.9 0.0 copy-start.5
  10.0 0.0 copy-done
  10.0 0.6 copy-done.5
  10.6 0.0 copy-start.1
  10.6 0.8 copy-done.1
  11.5 0.6 copy.23
  12.1 0.0 copy-start.8
  12.1 0.7 copy-done.8
  12.7 0.6 dynamic_slice.3.count_ref
  14.0 1.0 %multiply_add_fusion = (f32[16,4,8,128]{3,2,1,0:T(8,128)}, f32[16,4,8,128]{3,2,1,0:T(8,128)}) fusion(f32[4,8,128]{2,1,0:T(8,128)S(1)} %get-tuple-element.13, f32[4,8,128]{2,1,0:T(8,128)S(1)} %get-tuple-element.12, f32[16]{0:T(128)S(1)} %get-tuple-element.20, f32[16]{0:T(128)S(1)} %get-tuple-element.21, f32[4,8,128]{2,1,0:T(8,128)S(1)} %get-tuple-element.18, ...), kind=kLoop, calls=%fused_computation | loop fusion | flops 589824 | bytes 655504 | tf_op jit(solution)/shard_map/add | solution.py:171
  15.0 2.7 %shard_map.95 = (f32[12,8,128]{2,1,0:T(8,128)}, f32[12,8,128]{2,1,0:T(8,128)}) custom-call(s32[1]{0:T(128)} %dynamic_slice.3.count_ref, f32[16,4,8,128]{3,2,1,0:T(8,128)} %get-tuple-element.17.are_ref.refs_2_, f32[16,4,8,128]{3,2,1,0:T(8,128)} %get-tuple-element.16.aim_ref.refs_3_, f32[16,8,128]{2,1,0:T(8,128)} %bitcast.31), custom_call_target="tpu_custom_call" | custom-call | tf_op jit(solution)/shard_map/pallas_call | solution.py:181
  17.7 0.0 copy-start.3
  17.7 27.2 %all-gather = f32[192,8,128]{2,1,0:T(8,128)} all-gather(f32[12,8,128]{2,1,0:T(8,128)} %get-tuple-element.6), channel_id=2, replica_groups=mesh['slab'=16,'energy'=2] {'slab'}, dimensions={0}, use_global_device_ids=true | all-gather | bytes 835584 | tf_op jit(solution)/shard_map/all_gather | solution.py:189
  44.9 0.0 copy-done.3
  44.9 21.0 %all-gather.1 = f32[192,8,128]{2,1,0:T(8,128)} all-gather(f32[12,8,128]{2,1,0:T(8,128)S(1)} %copy-done.3), channel_id=3, replica_groups=mesh['slab'=16,'energy'=2] {'slab'}, dimensions={0}, use_global_device_ids=true | all-gather | bytes 835584 | tf_op jit(solution)/shard_map/all_gather | solution.py:189
  65.8 3.7 %shard_map.96 = (f32[16,8,128]{2,1,0:T(8,128)}, f32[16,8,128]{2,1,0:T(8,128)}) custom-call(s32[1]{0:T(128)} %bitcast.here_ref, s32[1]{0:T(128)} %dynamic_slice.3.count_ref, f32[4]{0:T(128)} %convert_multiply_fusion.weight_ref, f32[16,12,8,128]{3,2,1,0:T(8,128)} %bitcast.29, f32[16,12,8,128]{3,2,1,0:T(8,128)} %bitcast.30, ...), custom_call_target="tpu_custom_call" | custom-call | tf_op jit(solution)/shard_map/pallas_call | solution.py:190
  69.5 0.9 %stack_reshape.6 = f32[1,16,1024]{2,1,0:T(8,128)S(1)} reshape(f32[16,8,128]{2,1,0:T(8,128)} %get-tuple-element.8) | data formatting | bytes 131072 | tf_op jit(solution)/shard_map/stack;reshape | solution.py:203
  70.4 0.0 copy-done.2
  70.5 0.7 pad_maximum_fusion
  71.1 0.0 reduce-scatter.2.cloned.1.call-update
  71.2 9.3 %reduce-scatter.2.cloned.1.call-done = f32[2,16,512]{2,1,0:T(8,128)} async-done(((f32[2,16,1024]{2,1,0:T(8,128)}), f32[2,16,512]{2,1,0:T(8,128)}) %reduce-scatter.2.cloned.1.call-update) | async-done | bytes 65552 | tf_op jit(solution)/shard_map/reduce_scatter | solution.py:204
  80.5 1.4 %slice_bitcast_fusion = (f32[16,512]{1,0:T(8,128)}, f32[16,512]{1,0:T(8,128)}) fusion(f32[2,16,512]{2,1,0:T(8,128)} %reduce-scatter.2.cloned.1.call-done), kind=kLoop, calls=%fused_computation.4 | loop fusion | bytes 131072 | tf_op jit(solution)/shard_map/squeeze | solution.py:205
  (8 shorter events, 0.1 us)
Async XLA Ops:
  7.2 73.3 %reduce-scatter.2.cloned.1.call-start = ((), (), s32[]{:S(2)}) async-start(), calls=%async_computation.1 | async-start | bytes 196608 | tf_op jit(solution)/shard_map/reduce_scatter | solution.py:204
  7.2 0.7 copy-start.6
  7.9 0.7 copy-start.7
  8.5 1.4 %copy-start.4 = (f32[4,2,1024]{2,1,0:T(2,128)S(1)}, f32[4,2,1024]{2,1,0:T(2,128)}, u32[]{:S(2)}) copy-start(f32[4,2,1024]{2,1,0:T(2,128)} %param.15) | copy-start | bytes 98308
  9.1 0.9 copy-start
  9.9 0.7 copy-start.5
  10.6 0.8 copy-start.1
  12.1 0.7 copy-start.8
  17.7 27.2 %copy-start.3 = (f32[12,8,128]{2,1,0:T(8,128)S(1)}, f32[12,8,128]{2,1,0:T(8,128)}, u32[]{:S(2)}) copy-start(f32[12,8,128]{2,1,0:T(8,128)} %get-tuple-element.7) | copy-start | bytes 147460
  69.5 0.9 %copy-start.2 = (f32[16,8,128]{2,1,0:T(8,128)S(1)}, f32[16,8,128]{2,1,0:T(8,128)}, u32[]{:S(2)}) copy-start(f32[16,8,128]{2,1,0:T(8,128)} %get-tuple-element.9) | copy-start | bytes 196612
Sparse Core Ops, SparseCore 0:
  71.3 9.1 reduce-scatter.1

commit v4 on v2

--- a/solution.py
+++ b/solution.py
@@ -1,3 +1,5 @@
+import functools
+
 import jax
 import jax.numpy as jnp
 from jax import lax
@@ -56,54 +58,46 @@
     def body(slot, summary):
         return join_segments(summary, single(slot))
 
-    summary = lax.fori_loop(1, count_ref[0], body, single(0))
-    for field in range(6):
-        out_ref[field * points:(field + 1) * points] = summary[field]
-    out_ref[6 * points] = summary[6]
-
-
-def final_kernel(
-    here_ref, count_ref, weight_ref, every_ref, are_ref, aim_ref, hop_ref,
-    dens_ref, bond_ref, left_re_ref, left_im_ref,
-):
+    first_re, first_im, cross_re, cross_im, final_re, final_im, coupling = lax.fori_loop(
+        1, count_ref[0], body, single(0)
+    )
+    square = coupling * coupling
+    sq_re, sq_im = complex_mul(cross_re, cross_im, cross_re, cross_im)
+    fields = (first_re, first_im, square * final_re, square * final_im, square * sq_re, square * sq_im)
+    for index, value in enumerate(fields):
+        out_ref[index * points:(index + 1) * points] = value
+
+
+def final_kernel(here_ref, count_ref, weight_ref, every_ref, are_ref, aim_ref, hop_ref,
+                 dens_ref, bond_ref, left_re_ref, left_im_ref, *, mixed):
     points = are_ref.shape[1]
     devices = every_ref.shape[0]
     here = here_ref[0]
     count = count_ref[0]
 
     def field(device, index):
-        return every_ref[device, index * points:(index + 1) * points]
-
-    def coupling_of(device):
-        return every_ref[device, 6 * points]
+        block = jnp.bitwise_xor(device, here) if mixed else device
+        return every_ref[block, index * points:(index + 1) * points]
 
     def into_body(device, run):
         run_re, run_im = run
-        pp = coupling_of(jnp.maximum(device - 1, 0))
-        pp = pp * pp
-        c_re, c_im = complex_mul(field(device, 2), field(device, 3), field(device, 2), field(device, 3))
         m_re, m_im = complex_mul(run_re, run_im, field(device, 0), field(device, 1))
-        inv_re, inv_im = reciprocal(1.0 - pp * m_re, -pp * m_im)
-        t_re, t_im = complex_mul(c_re, c_im, run_re, run_im)
+        inv_re, inv_im = reciprocal(1.0 - m_re, -m_im)
+        t_re, t_im = complex_mul(field(device, 4), field(device, 5), run_re, run_im)
         t_re, t_im = complex_mul(t_re, t_im, inv_re, inv_im)
-        return (field(device, 4) + pp * t_re, field(device, 5) + pp * t_im)
-
-    zero = jnp.zeros(are_ref.shape[1:], jnp.float32)
-    into_re, into_im = lax.fori_loop(0, here, into_body, (zero, zero))
-    into_coupling = coupling_of(jnp.maximum(here - 1, 0))
+        return (field(device, 2) + t_re, field(device, 3) + t_im)
 
     def from_body(step, run):
         run_re, run_im = run
         device = devices - 1 - step
-        pp = coupling_of(device)
-        pp = pp * pp
-        c_re, c_im = complex_mul(field(device, 2), field(device, 3), field(device, 2), field(device, 3))
-        m_re, m_im = complex_mul(field(device, 4), field(device, 5), run_re, run_im)
-        inv_re, inv_im = reciprocal(1.0 - pp * m_re, -pp * m_im)
-        h_re, h_im = complex_mul(c_re, c_im, run_re, run_im)
+        m_re, m_im = complex_mul(field(device, 2), field(device, 3), run_re, run_im)
+        inv_re, inv_im = reciprocal(1.0 - m_re, -m_im)
+        h_re, h_im = complex_mul(field(device, 4), field(device, 5), run_re, run_im)
         h_re, h_im = complex_mul(h_re, h_im, inv_re, inv_im)
-        return (field(device, 0) + pp * h_re, field(device, 1) + pp * h_im)
-
+        return (field(device, 0) + h_re, field(device, 1) + h_im)
+
+    zero = jnp.zeros(are_ref.shape[1:], jnp.float32)
+    into_re, into_im = lax.fori_loop(0, here, into_body, (zero, zero))
     from_re, from_im = lax.fori_loop(0, devices - 1 - here, from_body, (zero, zero))
 
     def forward_body(slot, carry):
@@ -114,7 +108,8 @@
         left_im_ref[slot] = g_im
         return (g_re, g_im, hop_ref[slot])
 
-    lax.fori_loop(0, count, forward_body, (into_re, into_im, into_coupling))
+    ones = jnp.ones(hop_ref.shape[1:], jnp.float32)
+    lax.fori_loop(0, count, forward_body, (into_re, into_im, ones))
     dens_ref[...] = jnp.zeros(dens_ref.shape, jnp.float32)
     bond_ref[...] = jnp.zeros(bond_ref.shape, jnp.float32)
 
@@ -173,13 +168,22 @@
 
     packed = pl.pallas_call(
         summary_kernel,
-        out_shape=jax.ShapeDtypeStruct((6 * points + 1, rows, 128), jnp.float32),
+        out_shape=jax.ShapeDtypeStruct((6 * points, rows, 128), jnp.float32),
         in_specs=[smem, vmem, vmem, vmem],
         out_specs=vmem,
     )(count_arr, onsite_re, onsite_im, coupling_rows)
-    every = lax.all_gather(packed, "slab")
+    mixed = devices & (devices - 1) == 0
+    if mixed:
+        every = packed[None]
+        distance = 1
+        while distance < devices:
+            pairs = [(device, device ^ distance) for device in range(devices)]
+            every = jnp.concatenate([every, lax.ppermute(every, "slab", pairs)], axis=0)
+            distance *= 2
+    else:
+        every = lax.all_gather(packed, "slab")
     density, bond_density = pl.pallas_call(
-        final_kernel,
+        functools.partial(final_kernel, mixed=mixed),
         out_shape=(
             jax.ShapeDtypeStruct((slots, rows, 128), jnp.float32),
             jax.ShapeDtypeStruct((slots, rows, 128), jnp.float32),
@@ -192,7 +196,14 @@
         ],
     )(here_arr, count_arr, weights, every, onsite_re, onsite_im, coupling_rows)
     both = jnp.stack([density.reshape(slots, modes), bond_density.reshape(slots, modes)])
-    both = lax.psum_scatter(both, "energy", scatter_dimension=2, tiled=True)
+    if lax.axis_size("energy") == 2:
+        halves = both.reshape(2, slots, 2, modes // 2)
+        lower = lax.axis_index("energy") == 0
+        mine = jnp.where(lower, halves[:, :, 0], halves[:, :, 1])
+        theirs = jnp.where(lower, halves[:, :, 1], halves[:, :, 0])
+        both = mine + lax.ppermute(theirs, "energy", [(0, 1), (1, 0)])
+    else:
+        both = lax.psum_scatter(both, "energy", scatter_dimension=2, tiled=True)
     return (both[0], both[1])
 
 

time: 84.5 us -> 82.4 us (0.975)
  between operations: 14.7 us -> 1.41 us
  starting transfers between devices: 0.08 us -> 9.34 us
  other arithmetic: 3.73 us -> 5.89 us
    ppermute x0 -> x5, waiting for transfers between devices: none -> 51 us  [the longest x4 48.1 us: shards(): every = jnp.concatenate([every, lax.ppermute(every, 'slab', pairs)], axis=0)]
    all_gather x1 -> x0, waiting for transfers between devices: 41.4 us -> none  [shards(): every = lax.all_gather(packed, 'slab')]
    ppermute x0 -> x5, starting transfers between devices: none -> 9.34 us  [the longest x4 7.96 us: shards(): every = jnp.concatenate([every, lax.ppermute(every, 'slab', pairs)], axis=0)]
    reduce_scatter x1 -> x0, waiting for transfers between devices: 9.31 us -> none  [shards(): both = lax.psum_scatter(both, 'energy', scatter_dimension=2, tiled=True)]
    concatenate x0 -> x3, other arithmetic: none -> 2.77 us  [shards(): every = jnp.concatenate([every, lax.ppermute(every, 'slab', pairs)], axis=0)]
    unnamed x4 -> x13, local copies, waits for them, and re-layouts: 1.49 us -> 2.74 us
    another operation x2 -> x3, local copies, waits for them, and re-layouts: 1.71 us -> 1.76 us  [shards(): jnp.stack([density.reshape(slots, modes), bond_density.reshape(slots, mod...]
  transfers between devices with their start and end apart: 2 -> 5, of which waited for: 2 -> 5; matrix products, arithmetic and copies ran while one was open for 1% -> 1% of each run, Pallas kernels for 0% -> 0%
where the time goes in v4:
time: 82.4 us; the launch traced here: 82 us
  waiting for transfers between devices  51 us (62%)
  starting transfers between devices  9.34 us (11%)
  local copies, waits for them, and re-layouts  7.99 us (10%)
  Pallas kernels  6.33 us (8%)
  other arithmetic  5.89 us (7%)
  between operations  1.41 us (2%)
    ppermute x4, waiting for transfers between devices, shards(): every = jnp.concatenate([every, lax.ppermute(every, 'slab', pairs)], axis=0)  48.1 us
    ppermute x4, starting transfers between devices, shards(): every = jnp.concatenate([every, lax.ppermute(every, 'slab', pairs)], axis=0)  7.96 us
    pallas_call x1, Pallas kernels, shards(): pl.pallas_call(functools.partial(final_kernel, mixed=mixed), out_shape=(j...  3.56 us
    ppermute x1, waiting for transfers between devices, shards(): both = mine + lax.ppermute(theirs, 'energy', [(0, 1), (1, 0)])  2.96 us
    concatenate x3, other arithmetic, shards(): every = jnp.concatenate([every, lax.ppermute(every, 'slab', pairs)], axis=0)  2.77 us
    pallas_call x1, Pallas kernels, shards(): pl.pallas_call(summary_kernel, out_shape=jax.ShapeDtypeStruct((6 * points...  2.77 us
    unnamed x13, local copies, waits for them, and re-layouts  2.74 us
    another operation x3, local copies, waits for them, and re-layouts, shards(): jnp.stack([density.reshape(slots, modes), bond_density.reshape(slots, mod...  1.76 us
  transfers between devices with their start and end apart: 5, of which 5 were waited for; matrix products, arithmetic and copies ran while one was open for 1% of the time, Pallas kernels for 0%

profile of v4, /device:TPU:0, one launch (start us, length us, event | category | flops | bytes accessed | tf_op | source)
XLA Modules:
  0.0 82.0 jit_solution(2812267104337749861)
XLA Ops:
  0.6 0.8 reshape.49
  1.4 0.8 reshape.48
  2.2 0.9 %add_bitcast_fusion = f32[2,8,8,128]{3,1,2,0:T(8,128)S(1)} fusion(f32[16,1024]{1,0:T(8,128)} %param.9, f32[1024]{0:T(1024)} %param.8), kind=kLoop, calls=%fused_computation.9 | loop fusion | flops 16384 | bytes 135168
  3.1 0.7 multiply_add_fusion.1
  3.8 1.5 %copy.21 = f32[2,8,8,128]{3,2,1,0:T(8,128)} copy(f32[2,8,8,128]{3,1,2,0:T(8,128)} %bitcast.40) | data formatting | bytes 131072
  5.2 1.2 %dynamic_slice.3.count_ref = s32[1]{0:T(128)} dynamic-slice(s32[16]{0:T(128)} %param.11, s32[]{:T(128)S(6)} %select_n.22), dynamic_slice_sizes={1} | dynamic-slice | bytes 12 | tf_op jit(solution)/shard_map/dynamic_slice | solution.py:146
  7.1 1.0 %multiply_add_fusion = (f32[16,4,8,128]{3,2,1,0:T(8,128)}, f32[16,4,8,128]{3,2,1,0:T(8,128)}) fusion(f32[4,8,128]{2,1,0:T(8,128)S(1)} %get-tuple-element.9, f32[4,8,128]{2,1,0:T(8,128)S(1)} %get-tuple-element.8, f32[16]{0:T(128)S(1)} %get-tuple-element.16, f32[16]{0:T(128)S(1)} %get-tuple-element.17, f32[4,8,128]{2,1,0:T(8,128)S(1)} %get-tuple-element.14, ...), kind=kLoop, calls=%fused_computation.2 | loop fusion | flops 589824 | bytes 655504 | tf_op jit(solution)/shard_map/add | solution.py:161
  8.1 0.0 copy-start.2
  8.1 2.8 %shard_map.95 = f32[24,8,128]{2,1,0:T(8,128)} custom-call(s32[1]{0:T(128)} %dynamic_slice.3.count_ref, f32[16,4,8,128]{3,2,1,0:T(8,128)} %get-tuple-element.13.are_ref, f32[16,4,8,128]{3,2,1,0:T(8,128)} %get-tuple-element.12.aim_ref, f32[16,8,128]{2,1,0:T(8,128)} %bitcast.37), custom_call_target="tpu_custom_call" | custom-call | tf_op jit(solution)/shard_map/pallas_call | solution.py:169
  10.9 0.8 %collective-permute-start = (f32[1,24,8,128]{3,2,1,0:T(8,128)}, f32[1,24,8,128]{3,2,1,0:T(8,128)S(1)}, u32[]{:S(2)}, u32[]{:S(2)}) collective-permute-start(f32[1,24,8,128]{3,2,1,0:T(8,128)} %bitcast.33), channel_id=1, source_target_pairs={{0,2},{2,0},{4,6},{6,4},{8,10},{10,8},{12,14},{14,12},{16,18},{18,... | collective-permute-start | bytes 294920 | tf_op jit(solution)/shard_map/ppermute | solution.py:181
  11.7 1.2 %collective-permute-done = f32[1,24,8,128]{3,2,1,0:T(8,128)S(1)} collective-permute-done((f32[1,24,8,128]{3,2,1,0:T(8,128)}, f32[1,24,8,128]{3,2,1,0:T(8,128)S(1)}, u32[]{:S(2)}, u32[]{:S(2)}) %collective-permute-start) | collective-permute-done | bytes 98336 | tf_op jit(solution)/shard_map/ppermute | solution.py:181
  12.9 0.9 %pad_maximum_fusion.2 = f32[2,24,8,128]{3,2,1,0:T(8,128)S(1)} fusion(f32[1,24,8,128]{3,2,1,0:T(8,128)S(1)} %collective-permute-done, f32[1,24,8,128]{3,2,1,0:T(8,128)} %bitcast.34), kind=kLoop, calls=%fused_computation.4 | loop fusion | flops 49152 | bytes 393216 | tf_op jit(solution)/shard_map/concatenate | solution.py:181
  13.8 2.2 %collective-permute-start.1 = (f32[2,24,8,128]{3,2,1,0:T(8,128)S(1)}, f32[2,24,8,128]{3,2,1,0:T(8,128)S(1)}, u32[]{:S(2)}, u32[]{:S(2)}) collective-permute-start(f32[2,24,8,128]{3,2,1,0:T(8,128)S(1)} %pad_maximum_fusion.2), channel_id=1, source_target_pairs={{0,4},{2,6},{4,0},{6,2},{8,12},{10,14},{12,8},{14,10},{16,20},{18,... | collective-permute-start | bytes 589832 | tf_op jit(solution)/shard_map/ppermute | solution.py:181
  16.0 5.4 %collective-permute-done.1 = f32[2,24,8,128]{3,2,1,0:T(8,128)S(1)} collective-permute-done((f32[2,24,8,128]{3,2,1,0:T(8,128)S(1)}, f32[2,24,8,128]{3,2,1,0:T(8,128)S(1)}, u32[]{:S(2)}, u32[]{:S(2)}) %collective-permute-start.1) | collective-permute-done | bytes 196640 | tf_op jit(solution)/shard_map/ppermute | solution.py:181
  21.4 0.9 %pad_maximum_fusion.1 = f32[4,24,8,128]{3,2,1,0:T(8,128)S(1)} fusion(f32[2,24,8,128]{3,2,1,0:T(8,128)S(1)} %collective-permute-done.1, f32[1,24,8,128]{3,2,1,0:T(8,128)S(1)} %collective-permute-done, f32[1,24,8,128]{3,2,1,0:T(8,128)} %bitcast.35), kind=kLoop, calls=%fused_computation.1 | loop fusion | flops 196608 | bytes 786432 | tf_op jit(solution)/shard_map/concatenate | solution.py:181
  22.3 2.1 %collective-permute-start.2 = (f32[4,24,8,128]{3,2,1,0:T(8,128)S(1)}, f32[4,24,8,128]{3,2,1,0:T(8,128)S(1)}, u32[]{:S(2)}, u32[]{:S(2)}) collective-permute-start(f32[4,24,8,128]{3,2,1,0:T(8,128)S(1)} %pad_maximum_fusion.1), channel_id=1, source_target_pairs={{0,8},{2,10},{4,12},{6,14},{8,0},{10,2},{12,4},{14,6},{16,24},{18,... | collective-permute-start | bytes 1179656 | tf_op jit(solution)/shard_map/ppermute | solution.py:181
  24.4 8.8 %collective-permute-done.2 = f32[4,24,8,128]{3,2,1,0:T(8,128)S(1)} collective-permute-done((f32[4,24,8,128]{3,2,1,0:T(8,128)S(1)}, f32[4,24,8,128]{3,2,1,0:T(8,128)S(1)}, u32[]{:S(2)}, u32[]{:S(2)}) %collective-permute-start.2) | collective-permute-done | bytes 393248 | tf_op jit(solution)/shard_map/ppermute | solution.py:181
  33.2 0.9 %pad_maximum_fusion = f32[8,24,8,128]{3,2,1,0:T(8,128)S(1)} fusion(f32[4,24,8,128]{3,2,1,0:T(8,128)S(1)} %collective-permute-done.2, f32[2,24,8,128]{3,2,1,0:T(8,128)S(1)} %collective-permute-done.1, f32[1,24,8,128]{3,2,1,0:T(8,128)S(1)} %collective-permute-done, f32[1,24,8,128]{3,2,1,0:T(8,128)} %bitcast.36), kind=kLoop, calls=%fused_computation | loop fusion | flops 589824 | bytes 1572864 | tf_op jit(solution)/shard_map/concatenate | solution.py:181
  34.2 2.8 %collective-permute-start.3 = (f32[8,24,8,128]{3,2,1,0:T(8,128)S(1)}, f32[8,24,8,128]{3,2,1,0:T(8,128)S(1)}, u32[]{:S(2)}, u32[]{:S(2)}) collective-permute-start(f32[8,24,8,128]{3,2,1,0:T(8,128)S(1)} %pad_maximum_fusion), channel_id=1, source_target_pairs={{0,16},{2,18},{4,20},{6,22},{8,24},{10,26},{12,28},{14,30},{16,0},... | collective-permute-start | bytes 2359304 | tf_op jit(solution)/shard_map/ppermute | solution.py:181
  37.0 0.0 copy-done.2
  37.0 0.6 convert_multiply_fusion.weight_ref
  37.6 0.0 copy-done
  37.7 32.7 %collective-permute-done.3 = f32[8,24,8,128]{3,2,1,0:T(8,128)S(1)} collective-permute-done((f32[8,24,8,128]{3,2,1,0:T(8,128)S(1)}, f32[8,24,8,128]{3,2,1,0:T(8,128)S(1)}, u32[]{:S(2)}, u32[]{:S(2)}) %collective-permute-start.3) | collective-permute-done | bytes 786464 | tf_op jit(solution)/shard_map/ppermute | solution.py:181
  70.4 0.1 constant_dynamic-update-slice_fusion.every_ref
  70.4 0.0 copy-start.1
  70.4 1.2 %copy-done.1 = f32[16,24,8,128]{3,2,1,0:T(8,128)} copy-done((f32[16,24,8,128]{3,2,1,0:T(8,128)}, f32[16,24,8,128]{3,2,1,0:T(8,128)S(1)}, u32[]{:S(2)}) %copy-start.1) | copy-done | bytes 1572888
  71.6 3.6 %shard_map.96 = (f32[16,8,128]{2,1,0:T(8,128)}, f32[16,8,128]{2,1,0:T(8,128)}) custom-call(s32[1]{0:T(128)} %bitcast.here_ref, s32[1]{0:T(128)} %dynamic_slice.3.count_ref, f32[4]{0:T(128)} %convert_multiply_fusion.weight_ref, f32[16,24,8,128]{3,2,1,0:T(8,128)} %copy-done.1, f32[16,4,8,128]{3,2,1,0:T(8,128)} %get-tuple-element.13.are_ref, ...), custom_call_target="tpu_custom_call" | custom-call | tf_op jit(solution)/shard_map/pallas_call | solution.py:185
  75.2 0.9 %stack.7 = f32[1,16,2,512]{3,2,1,0:T(2,128)S(1)} reshape(f32[16,8,128]{2,1,0:T(8,128)} %get-tuple-element.4) | data formatting | bytes 131072 | tf_op jit(solution)/shard_map/stack | solution.py:198
  76.1 0.9 %stack.8 = f32[1,16,2,512]{3,2,1,0:T(2,128)S(1)} reshape(f32[16,8,128]{2,1,0:T(8,128)} %get-tuple-element.5) | data formatting | bytes 131072 | tf_op jit(solution)/shard_map/stack | solution.py:198
  77.0 1.4 %collective-permute-start.4 = (f32[2,16,512]{2,1,0:T(8,128)S(1)}, f32[2,16,512]{2,1,0:T(8,128)S(1)}, u32[]{:S(2)}, u32[]{:S(2)}) collective-permute-start(f32[2,16,512]{2,1,0:T(8,128)S(1)} %select_bitcast_fusion), channel_id=1, source_target_pairs={{0,1},{1,0},{2,3},{3,2},{4,5},{5,4},{6,7},{7,6},{8,9},{9,8},{10,11... | collective-permute-start | bytes 196616 | tf_op jit(solution)/shard_map/ppermute | solution.py:204
  78.4 3.0 %collective-permute-done.4 = f32[2,16,512]{2,1,0:T(8,128)S(1)} collective-permute-done((f32[2,16,512]{2,1,0:T(8,128)S(1)}, f32[2,16,512]{2,1,0:T(8,128)S(1)}, u32[]{:S(2)}, u32[]{:S(2)}) %collective-permute-start.4) | collective-permute-done | bytes 65568 | tf_op jit(solution)/shard_map/ppermute | solution.py:204
  81.3 0.6 slice_bitcast_fusion
  (12 shorter events, 0.1 us)
Async XLA Ops:
  8.1 28.9 %copy-start.2 = (s32[4]{0:T(128)S(1)}, s32[4]{0:T(128)}, u32[]{:S(2)}) copy-start(s32[4]{0:T(128)} %param.13) | copy-start | bytes 52
  10.9 26.7 %copy-start = (f32[24,8,128]{2,1,0:T(8,128)S(1)}, f32[24,8,128]{2,1,0:T(8,128)}, u32[]{:S(2)}) copy-start(f32[24,8,128]{2,1,0:T(8,128)} %shard_map.95) | copy-start | bytes 294916
  10.9 2.0 %collective-permute-start = (f32[1,24,8,128]{3,2,1,0:T(8,128)}, f32[1,24,8,128]{3,2,1,0:T(8,128)S(1)}, u32[]{:S(2)}, u32[]{:S(2)}) collective-permute-start(f32[1,24,8,128]{3,2,1,0:T(8,128)} %bitcast.33), channel_id=1, source_target_pairs={{0,2},{2,0},{4,6},{6,4},{8,10},{10,8},{12,14},{14,12},{16,18},{18,... | collective-permute-start | bytes 294920 | tf_op jit(solution)/shard_map/ppermute | solution.py:181
  13.8 7.6 %collective-permute-start.1 = (f32[2,24,8,128]{3,2,1,0:T(8,128)S(1)}, f32[2,24,8,128]{3,2,1,0:T(8,128)S(1)}, u32[]{:S(2)}, u32[]{:S(2)}) collective-permute-start(f32[2,24,8,128]{3,2,1,0:T(8,128)S(1)} %pad_maximum_fusion.2), channel_id=1, source_target_pairs={{0,4},{2,6},{4,0},{6,2},{8,12},{10,14},{12,8},{14,10},{16,20},{18,... | collective-permute-start | bytes 589832 | tf_op jit(solution)/shard_map/ppermute | solution.py:181
  22.3 10.9 %collective-permute-start.2 = (f32[4,24,8,128]{3,2,1,0:T(8,128)S(1)}, f32[4,24,8,128]{3,2,1,0:T(8,128)S(1)}, u32[]{:S(2)}, u32[]{:S(2)}) collective-permute-start(f32[4,24,8,128]{3,2,1,0:T(8,128)S(1)} %pad_maximum_fusion.1), channel_id=1, source_target_pairs={{0,8},{2,10},{4,12},{6,14},{8,0},{10,2},{12,4},{14,6},{16,24},{18,... | collective-permute-start | bytes 1179656 | tf_op jit(solution)/shard_map/ppermute | solution.py:181
  34.2 36.2 %collective-permute-start.3 = (f32[8,24,8,128]{3,2,1,0:T(8,128)S(1)}, f32[8,24,8,128]{3,2,1,0:T(8,128)S(1)}, u32[]{:S(2)}, u32[]{:S(2)}) collective-permute-start(f32[8,24,8,128]{3,2,1,0:T(8,128)S(1)} %pad_maximum_fusion), channel_id=1, source_target_pairs={{0,16},{2,18},{4,20},{6,22},{8,24},{10,26},{12,28},{14,30},{16,0},... | collective-permute-start | bytes 2359304 | tf_op jit(solution)/shard_map/ppermute | solution.py:181
  70.4 1.2 %copy-start.1 = (f32[16,24,8,128]{3,2,1,0:T(8,128)}, f32[16,24,8,128]{3,2,1,0:T(8,128)S(1)}, u32[]{:S(2)}) copy-start(f32[16,24,8,128]{3,2,1,0:T(8,128)S(1)} %constant_dynamic-update-slice_fusion.every_ref) | copy-start | bytes 4718596
  77.0 4.3 %collective-permute-start.4 = (f32[2,16,512]{2,1,0:T(8,128)S(1)}, f32[2,16,512]{2,1,0:T(8,128)S(1)}, u32[]{:S(2)}, u32[]{:S(2)}) collective-permute-start(f32[2,16,512]{2,1,0:T(8,128)S(1)} %select_bitcast_fusion), channel_id=1, source_target_pairs={{0,1},{1,0},{2,3},{3,2},{4,5},{5,4},{6,7},{7,6},{8,9},{9,8},{10,11... | collective-permute-start | bytes 196616 | tf_op jit(solution)/shard_map/ppermute | solution.py:204

commit v5 on v4

--- a/solution.py
+++ b/solution.py
@@ -174,12 +174,15 @@
     )(count_arr, onsite_re, onsite_im, coupling_rows)
     mixed = devices & (devices - 1) == 0
     if mixed:
-        every = packed[None]
-        distance = 1
-        while distance < devices:
+        every = packed
+        distance = devices // 2
+        level = 0
+        while distance >= 1:
             pairs = [(device, device ^ distance) for device in range(devices)]
-            every = jnp.concatenate([every, lax.ppermute(every, "slab", pairs)], axis=0)
-            distance *= 2
+            every = jnp.stack([every, lax.ppermute(every, "slab", pairs)], axis=level)
+            distance //= 2
+            level += 1
+        every = every.reshape((devices,) + packed.shape)
     else:
         every = lax.all_gather(packed, "slab")
     density, bond_density = pl.pallas_call(

time: 82.4 us -> 52.2 us (0.63)
  waiting for transfers between devices: 51 us -> 23.8 us
  starting transfers between devices: 9.34 us -> 7.03 us
  other arithmetic: 5.89 us -> 4.33 us
    ppermute x4, waiting for transfers between devices: 48.1 us -> 20.9 us  [shards(): every = jnp.stack([every, lax.ppermute(every, 'slab', pairs)], axis=level)]
    concatenate x3 -> x0, other arithmetic: 2.77 us -> none  [shards(): every = jnp.concatenate([every, lax.ppermute(every, 'slab', pairs)], axis=0)]
    ppermute x4, starting transfers between devices: 7.96 us -> 5.65 us  [shards(): every = jnp.stack([every, lax.ppermute(every, 'slab', pairs)], axis=level)]
    another operation x0 -> x4, other arithmetic: none -> 1.27 us  [shards(): every = jnp.stack([every, lax.ppermute(every, 'slab', pairs)], axis=level)]
    another operation x0 -> x1, local copies, waits for them, and re-layouts: none -> 1.27 us  [shards(): every = jnp.stack([every, lax.ppermute(every, 'slab', pairs)], axis=level)]
    unnamed x13 -> x5, local copies, waits for them, and re-layouts: 2.74 us -> 1.51 us
where the time goes in v5:
time: 52.2 us; the launch traced here: 51.6 us
  waiting for transfers between devices  23.8 us (46%)
  local copies, waits for them, and re-layouts  7.99 us (15%)
  starting transfers between devices  7.03 us (13%)
  Pallas kernels  6.99 us (13%)
  other arithmetic  4.33 us (8%)
  between operations  1.4 us (3%)
    ppermute x4, waiting for transfers between devices, shards(): every = jnp.stack([every, lax.ppermute(every, 'slab', pairs)], axis=level)  20.9 us
    ppermute x4, starting transfers between devices, shards(): every = jnp.stack([every, lax.ppermute(every, 'slab', pairs)], axis=level)  5.65 us
    pallas_call x1, Pallas kernels, shards(): pl.pallas_call(functools.partial(final_kernel, mixed=mixed), out_shape=(j...  3.88 us
    pallas_call x1, Pallas kernels, shards(): pl.pallas_call(summary_kernel, out_shape=jax.ShapeDtypeStruct((6 * points...  3.12 us
    ppermute x1, waiting for transfers between devices, shards(): both = mine + lax.ppermute(theirs, 'energy', [(0, 1), (1, 0)])  2.95 us
    another operation x3, local copies, waits for them, and re-layouts, shards(): jnp.stack([density.reshape(slots, modes), bond_density.reshape(slots, mod...  1.76 us
    unnamed x5, local copies, waits for them, and re-layouts  1.51 us
    ppermute x1, starting transfers between devices, shards(): both = mine + lax.ppermute(theirs, 'energy', [(0, 1), (1, 0)])  1.38 us
  transfers between devices with their start and end apart: 5, of which 5 were waited for; matrix products, arithmetic and copies ran while one was open for 1% of the time, Pallas kernels for 0%

profile of v5, /device:TPU:0, one launch (start us, length us, event | category | flops | bytes accessed | tf_op | source)
XLA Modules:
  0.0 51.6 jit_solution(15295472488038598440)
XLA Ops:
  0.6 0.8 %reshape.51 = f32[1,4,2,8,128]{4,3,2,1,0:T(8,128)S(1)} reshape(f32[4,2,1024]{2,1,0:T(2,128)} %param.14) | data formatting | bytes 65536 | tf_op jit(solution)/shard_map/reshape | solution.py:153
  1.4 0.8 %reshape.52 = f32[1,4,2,8,128]{4,3,2,1,0:T(8,128)S(1)} reshape(f32[4,2,1024]{2,1,0:T(2,128)} %param.15) | data formatting | bytes 65536 | tf_op jit(solution)/shard_map/reshape | solution.py:154
  2.2 0.9 %add_bitcast_fusion = f32[2,8,8,128]{3,1,2,0:T(8,128)S(1)} fusion(f32[16,1024]{1,0:T(8,128)} %param.9, f32[1024]{0:T(1024)} %param.8), kind=kLoop, calls=%fused_computation.10 | loop fusion | flops 16384 | bytes 135168
  3.1 0.7 %multiply_add_fusion.1 = f32[4]{0:T(128)S(1)} fusion(s32[4]{0:T(128)} %param.12), kind=kLoop, calls=%fused_computation.19 | loop fusion | flops 12 | bytes 32 | tf_op jit(solution)/shard_map/add | solution.py:150
  3.8 1.5 %copy.22 = f32[2,8,8,128]{3,2,1,0:T(8,128)} copy(f32[2,8,8,128]{3,1,2,0:T(8,128)} %bitcast.52) | data formatting | bytes 131072
  5.2 1.2 %dynamic_slice.3.count_ref = s32[1]{0:T(128)} dynamic-slice(s32[16]{0:T(128)} %param.11, s32[]{:T(128)S(6)} %select_n.22), dynamic_slice_sizes={1} | dynamic-slice | bytes 12 | tf_op jit(solution)/shard_map/dynamic_slice | solution.py:146
  7.2 1.0 %multiply_add_fusion = (f32[16,4,8,128]{3,2,1,0:T(8,128)}, f32[16,4,8,128]{3,2,1,0:T(8,128)}) fusion(f32[4,8,128]{2,1,0:T(8,128)S(1)} %get-tuple-element.15, f32[4,8,128]{2,1,0:T(8,128)S(1)} %get-tuple-element.14, f32[16]{0:T(128)S(1)} %get-tuple-element.22, f32[16]{0:T(128)S(1)} %get-tuple-element.23, f32[4,8,128]{2,1,0:T(8,128)S(1)} %get-tuple-element.20, ...), kind=kLoop, calls=%fused_computation.3 | loop fusion | flops 589824 | bytes 655504 | tf_op jit(solution)/shard_map/add | solution.py:161
  8.1 3.1 %shard_map.95 = f32[24,8,128]{2,1,0:T(8,128)} custom-call(s32[1]{0:T(128)} %dynamic_slice.3.count_ref, f32[16,4,8,128]{3,2,1,0:T(8,128)} %get-tuple-element.19.are_ref, f32[16,4,8,128]{3,2,1,0:T(8,128)} %get-tuple-element.18.aim_ref, f32[16,8,128]{2,1,0:T(8,128)} %bitcast.45), custom_call_target="tpu_custom_call" | custom-call | tf_op jit(solution)/shard_map/pallas_call | solution.py:169
  11.2 4.0 %collective-permute-start = (f32[24,8,128]{2,1,0:T(8,128)}, f32[24,8,128]{2,1,0:T(8,128)S(1)}, u32[]{:S(2)}, u32[]{:S(2)}) collective-permute-start(f32[24,8,128]{2,1,0:T(8,128)} %shard_map.95), channel_id=1, source_target_pairs={{0,16},{2,18},{4,20},{6,22},{8,24},{10,26},{12,28},{14,30},{16,0},... | collective-permute-start | bytes 294920 | tf_op jit(solution)/shard_map/ppermute | solution.py:182
  15.3 5.1 %collective-permute-done = f32[24,8,128]{2,1,0:T(8,128)S(1)} collective-permute-done((f32[24,8,128]{2,1,0:T(8,128)}, f32[24,8,128]{2,1,0:T(8,128)S(1)}, u32[]{:S(2)}, u32[]{:S(2)}) %collective-permute-start) | collective-permute-done | bytes 98336 | tf_op jit(solution)/shard_map/ppermute | solution.py:182
  20.4 0.9 %fusion = (f32[2,1,24,8,128]{4,3,2,0,1:T(8,128)S(1)}, f32[2,24,8,128]{3,2,1,0:T(8,128)S(1)}) fusion(f32[1,24,8,128]{3,2,1,0:T(8,128)S(1)} %bitcast.51, f32[1,24,8,128]{3,2,1,0:T(8,128)} %bitcast.48), kind=kLoop, calls=%fused_computation.21 | loop fusion | flops 49152 | bytes 589824 | tf_op jit(solution)/shard_map/stack | solution.py:182
  21.3 0.9 %collective-permute-start.1 = (f32[2,24,8,128]{3,2,1,0:T(8,128)S(1)}, f32[2,24,8,128]{3,2,1,0:T(8,128)S(1)}, u32[]{:S(2)}, u32[]{:S(2)}) collective-permute-start(f32[2,24,8,128]{3,2,1,0:T(8,128)S(1)} %get-tuple-element.11), channel_id=1, source_target_pairs={{0,8},{2,10},{4,12},{6,14},{8,0},{10,2},{12,4},{14,6},{16,24},{18,... | collective-permute-start | bytes 589832 | tf_op jit(solution)/shard_map/ppermute | solution.py:182
  22.2 5.3 %collective-permute-done.1 = f32[2,24,8,128]{3,2,1,0:T(8,128)S(1)} collective-permute-done((f32[2,24,8,128]{3,2,1,0:T(8,128)S(1)}, f32[2,24,8,128]{3,2,1,0:T(8,128)S(1)}, u32[]{:S(2)}, u32[]{:S(2)}) %collective-permute-start.1) | collective-permute-done | bytes 196640 | tf_op jit(solution)/shard_map/ppermute | solution.py:182
  27.5 0.0 copy-start
  27.5 0.1 fusion.1
  27.5 0.7 %collective-permute-start.2 = (f32[2,2,24,8,128]{4,3,2,0,1:T(8,128)S(1)}, f32[2,2,24,8,128]{4,3,2,0,1:T(8,128)S(1)}, u32[]{:S(2)}, u32[]{:S(2)}) collective-permute-start(f32[2,2,24,8,128]{4,3,2,0,1:T(8,128)S(1)} %get-tuple-element.9), channel_id=1, source_target_pairs={{0,4},{2,6},{4,0},{6,2},{8,12},{10,14},{12,8},{14,10},{16,20},{18,... | collective-permute-start | bytes 1179656 | tf_op jit(solution)/shard_map/ppermute | solution.py:182
  28.2 8.8 %collective-permute-done.2 = f32[2,2,24,8,128]{4,3,2,0,1:T(8,128)S(1)} collective-permute-done((f32[2,2,24,8,128]{4,3,2,0,1:T(8,128)S(1)}, f32[2,2,24,8,128]{4,3,2,0,1:T(8,128)S(1)}, u32[]{:S(2)}, u32[]{:S(2)}) %collective-permute-start.2) | collective-permute-done | bytes 393248 | tf_op jit(solution)/shard_map/ppermute | solution.py:182
  37.0 0.2 fusion.2
  37.1 0.1 collective-permute-start.3
  37.2 0.0 copy-done
  37.2 0.5 %convert_multiply_fusion.weight_ref = f32[4]{0:T(128)} fusion(s32[4]{0:T(128)S(1)} %copy-done), kind=kLoop, calls=%fused_computation.20 | loop fusion | flops 8 | bytes 32 | tf_op jit(solution)/shard_map/div | solution.py:151
  37.8 1.7 %collective-permute-done.3 = f32[2,2,2,24,8,128]{5,4,3,0,1,2:T(8,128)S(1)} collective-permute-done((f32[2,2,2,24,8,128]{5,4,3,0,1,2:T(8,128)S(1)}, f32[2,2,2,24,8,128]{5,4,3,0,1,2:T(8,128)S(1)}, u32[]{:S(2)}, u32[]{:S(2)}) %collective-permute-start.3) | collective-permute-done | bytes 786464 | tf_op jit(solution)/shard_map/ppermute | solution.py:182
  39.5 0.1 pad_maximum_fusion
  39.6 1.3 %copy.14 = f32[2,2,2,2,24,8,128]{6,5,4,3,2,1,0:T(8,128)} copy(f32[2,2,2,2,24,8,128]{6,5,4,0,1,2,3:T(8,128)S(1)} %pad_maximum_fusion) | data formatting | bytes 3145728 | tf_op jit(solution)/shard_map/stack | solution.py:182
  40.9 3.9 %shard_map.96 = (f32[16,8,128]{2,1,0:T(8,128)}, f32[16,8,128]{2,1,0:T(8,128)}) custom-call(s32[1]{0:T(128)} %bitcast.here_ref, s32[1]{0:T(128)} %dynamic_slice.3.count_ref, f32[4]{0:T(128)} %convert_multiply_fusion.weight_ref, f32[16,24,8,128]{3,2,1,0:T(8,128)} %bitcast.43, f32[16,4,8,128]{3,2,1,0:T(8,128)} %get-tuple-element.19.are_ref, ...), custom_call_target="tpu_custom_call" | custom-call | tf_op jit(solution)/shard_map/pallas_call | solution.py:188
  44.8 0.9 %stack.55 = f32[1,16,2,512]{3,2,1,0:T(2,128)S(1)} reshape(f32[16,8,128]{2,1,0:T(8,128)} %get-tuple-element.4) | data formatting | bytes 131072 | tf_op jit(solution)/shard_map/stack | solution.py:201
  45.7 0.9 %stack.56 = f32[1,16,2,512]{3,2,1,0:T(2,128)S(1)} reshape(f32[16,8,128]{2,1,0:T(8,128)} %get-tuple-element.5) | data formatting | bytes 131072 | tf_op jit(solution)/shard_map/stack | solution.py:201
  46.6 1.4 %collective-permute-start.4 = (f32[2,16,512]{2,1,0:T(8,128)S(1)}, f32[2,16,512]{2,1,0:T(8,128)S(1)}, u32[]{:S(2)}, u32[]{:S(2)}) collective-permute-start(f32[2,16,512]{2,1,0:T(8,128)S(1)} %select_bitcast_fusion), channel_id=1, source_target_pairs={{0,1},{1,0},{2,3},{3,2},{4,5},{5,4},{6,7},{7,6},{8,9},{9,8},{10,11... | collective-permute-start | bytes 196616 | tf_op jit(solution)/shard_map/ppermute | solution.py:207
  48.0 3.0 %collective-permute-done.4 = f32[2,16,512]{2,1,0:T(8,128)S(1)} collective-permute-done((f32[2,16,512]{2,1,0:T(8,128)S(1)}, f32[2,16,512]{2,1,0:T(8,128)S(1)}, u32[]{:S(2)}, u32[]{:S(2)}) %collective-permute-start.4) | collective-permute-done | bytes 65568 | tf_op jit(solution)/shard_map/ppermute | solution.py:207
  50.9 0.6 %slice_bitcast_fusion = (f32[16,512]{1,0:T(8,128)}, f32[16,512]{1,0:T(8,128)}) fusion(f32[2,16,512]{2,1,0:T(8,128)S(1)} %bitcast_add_fusion), kind=kLoop, calls=%fused_computation.11 | loop fusion | bytes 131072 | tf_op jit(solution)/shard_map/squeeze | solution.py:210
  (7 shorter events, 0.1 us)
Async XLA Ops:
  11.2 9.1 %collective-permute-start = (f32[24,8,128]{2,1,0:T(8,128)}, f32[24,8,128]{2,1,0:T(8,128)S(1)}, u32[]{:S(2)}, u32[]{:S(2)}) collective-permute-start(f32[24,8,128]{2,1,0:T(8,128)} %shard_map.95), channel_id=1, source_target_pairs={{0,16},{2,18},{4,20},{6,22},{8,24},{10,26},{12,28},{14,30},{16,0},... | collective-permute-start | bytes 294920 | tf_op jit(solution)/shard_map/ppermute | solution.py:182
  21.3 6.2 %collective-permute-start.1 = (f32[2,24,8,128]{3,2,1,0:T(8,128)S(1)}, f32[2,24,8,128]{3,2,1,0:T(8,128)S(1)}, u32[]{:S(2)}, u32[]{:S(2)}) collective-permute-start(f32[2,24,8,128]{3,2,1,0:T(8,128)S(1)} %get-tuple-element.11), channel_id=1, source_target_pairs={{0,8},{2,10},{4,12},{6,14},{8,0},{10,2},{12,4},{14,6},{16,24},{18,... | collective-permute-start | bytes 589832 | tf_op jit(solution)/shard_map/ppermute | solution.py:182
  27.5 9.8 %copy-start = (s32[4]{0:T(128)S(1)}, s32[4]{0:T(128)}, u32[]{:S(2)}) copy-start(s32[4]{0:T(128)} %param.13) | copy-start | bytes 52
  27.5 9.4 %collective-permute-start.2 = (f32[2,2,24,8,128]{4,3,2,0,1:T(8,128)S(1)}, f32[2,2,24,8,128]{4,3,2,0,1:T(8,128)S(1)}, u32[]{:S(2)}, u32[]{:S(2)}) collective-permute-start(f32[2,2,24,8,128]{4,3,2,0,1:T(8,128)S(1)} %get-tuple-element.9), channel_id=1, source_target_pairs={{0,4},{2,6},{4,0},{6,2},{8,12},{10,14},{12,8},{14,10},{16,20},{18,... | collective-permute-start | bytes 1179656 | tf_op jit(solution)/shard_map/ppermute | solution.py:182
  37.1 2.4 %collective-permute-start.3 = (f32[2,2,2,24,8,128]{5,4,3,0,1,2:T(8,128)S(1)}, f32[2,2,2,24,8,128]{5,4,3,0,1,2:T(8,128)S(1)}, u32[]{:S(2)}, u32[]{:S(2)}) collective-permute-start(f32[2,2,2,24,8,128]{5,4,3,0,1,2:T(8,128)S(1)} %get-tuple-element.7), channel_id=1, source_target_pairs={{0,2},{2,0},{4,6},{6,4},{8,10},{10,8},{12,14},{14,12},{16,18},{18,... | collective-permute-start | bytes 2359304 | tf_op jit(solution)/shard_map/ppermute | solution.py:182
  46.6 4.3 %collective-permute-start.4 = (f32[2,16,512]{2,1,0:T(8,128)S(1)}, f32[2,16,512]{2,1,0:T(8,128)S(1)}, u32[]{:S(2)}, u32[]{:S(2)}) collective-permute-start(f32[2,16,512]{2,1,0:T(8,128)S(1)} %select_bitcast_fusion), channel_id=1, source_target_pairs={{0,1},{1,0},{2,3},{3,2},{4,5},{5,4},{6,7},{7,6},{8,9},{9,8},{10,11... | collective-permute-start | bytes 196616 | tf_op jit(solution)/shard_map/ppermute | solution.py:207

commit v6 on v5

--- a/solution.py
+++ b/solution.py
@@ -48,18 +48,43 @@
     )
 
 
-def summary_kernel(count_ref, are_ref, aim_ref, hop_ref, out_ref):
-    points = are_ref.shape[1]
+def onsite_terms(table_ref, energy_ref, here, count, devices, slots, points, slot):
+    rows = 2 * slots
+    levels = table_ref[slot]
+    first_on = jnp.logical_and(here == 0, slot == 0).astype(jnp.float32)
+    last_on = jnp.logical_and(here == devices - 1, slot == count - 1).astype(jnp.float32)
+    onsite_re, onsite_im = [], []
+    for point in range(points):
+        energy = e_low + e_step * energy_ref[point].astype(jnp.float32)
+        onsite_re.append(
+            energy - levels
+            - first_on * table_ref[rows + 2 * point]
+            - last_on * table_ref[rows + 2 * point + 1]
+        )
+        onsite_im.append(
+            broaden
+            + first_on * table_ref[rows + 2 * points + 2 * point]
+            + last_on * table_ref[rows + 2 * points + 2 * point + 1]
+        )
+    return jnp.stack(onsite_re), jnp.stack(onsite_im)
+
+
+def summary_kernel(here_ref, length_ref, energy_ref, table_ref, out_ref, *, slots, points, devices):
+    here = here_ref[0]
+    count = length_ref[here]
 
     def single(slot):
-        g_re, g_im = reciprocal(are_ref[slot], aim_ref[slot])
-        return (g_re, g_im, g_re, g_im, g_re, g_im, hop_ref[slot])
+        onsite_re, onsite_im = onsite_terms(
+            table_ref, energy_ref, here, count, devices, slots, points, slot
+        )
+        g_re, g_im = reciprocal(onsite_re, onsite_im)
+        return (g_re, g_im, g_re, g_im, g_re, g_im, table_ref[slots + slot])
 
     def body(slot, summary):
         return join_segments(summary, single(slot))
 
     first_re, first_im, cross_re, cross_im, final_re, final_im, coupling = lax.fori_loop(
-        1, count_ref[0], body, single(0)
+        1, count, body, single(0)
     )
     square = coupling * coupling
     sq_re, sq_im = complex_mul(cross_re, cross_im, cross_re, cross_im)
@@ -68,12 +93,12 @@
         out_ref[index * points:(index + 1) * points] = value
 
 
-def final_kernel(here_ref, count_ref, weight_ref, every_ref, are_ref, aim_ref, hop_ref,
-                 dens_ref, bond_ref, left_re_ref, left_im_ref, *, mixed):
-    points = are_ref.shape[1]
+def final_kernel(here_ref, length_ref, energy_ref, code_ref, every_ref, table_ref,
+                 low_ref, high_ref, left_re_ref, left_im_ref, dens_ref, bond_ref, *, slots, points, mixed, scale):
     devices = every_ref.shape[0]
     here = here_ref[0]
-    count = count_ref[0]
+    count = length_ref[here]
+    rows = table_ref.shape[1]
 
     def field(device, index):
         block = jnp.bitwise_xor(device, here) if mixed else device
@@ -96,42 +121,57 @@
         h_re, h_im = complex_mul(h_re, h_im, inv_re, inv_im)
         return (field(device, 0) + h_re, field(device, 1) + h_im)
 
-    zero = jnp.zeros(are_ref.shape[1:], jnp.float32)
+    zero = jnp.zeros((points,) + table_ref.shape[1:], jnp.float32)
     into_re, into_im = lax.fori_loop(0, here, into_body, (zero, zero))
     from_re, from_im = lax.fori_loop(0, devices - 1 - here, from_body, (zero, zero))
 
+    def onsite(slot):
+        return onsite_terms(table_ref, energy_ref, here, count, devices, slots, points, slot)
+
     def forward_body(slot, carry):
         prev_re, prev_im, prev_coupling = carry
+        onsite_re, onsite_im = onsite(slot)
         square = prev_coupling * prev_coupling
-        g_re, g_im = reciprocal(are_ref[slot] - square * prev_re, aim_ref[slot] - square * prev_im)
+        g_re, g_im = reciprocal(onsite_re - square * prev_re, onsite_im - square * prev_im)
         left_re_ref[slot] = g_re
         left_im_ref[slot] = g_im
-        return (g_re, g_im, hop_ref[slot])
-
-    ones = jnp.ones(hop_ref.shape[1:], jnp.float32)
+        return (g_re, g_im, table_ref[slots + slot])
+
+    ones = jnp.ones(table_ref.shape[1:], jnp.float32)
     lax.fori_loop(0, count, forward_body, (into_re, into_im, ones))
     dens_ref[...] = jnp.zeros(dens_ref.shape, jnp.float32)
     bond_ref[...] = jnp.zeros(bond_ref.shape, jnp.float32)
+    weights = [code_ref[point].astype(jnp.float32) * scale for point in range(points)]
 
     def backward_body(step, carry):
         next_re, next_im = carry
         slot = count - 1 - step
+        onsite_re, onsite_im = onsite(slot)
         left_re, left_im = left_re_ref[slot], left_im_ref[slot]
-        square = hop_ref[slot] * hop_ref[slot]
+        coupling = table_ref[slots + slot]
+        square = coupling * coupling
         mix_re, mix_im = complex_mul(left_re, left_im, next_re, next_im)
         inv_re, inv_im = reciprocal(1.0 - square * mix_re, -square * mix_im)
         diag_re, diag_im = complex_mul(left_re, left_im, inv_re, inv_im)
         _, bond_im = complex_mul(diag_re, diag_im, next_re, next_im)
-        dens = weight_ref[0] * diag_im[0]
-        bond = weight_ref[0] * (square * bond_im[0])
+        dens = weights[0] * diag_im[0]
+        bond = weights[0] * (square * bond_im[0])
         for point in range(1, points):
-            dens = dens + weight_ref[point] * diag_im[point]
-            bond = bond + weight_ref[point] * (square * bond_im[point])
+            dens = dens + weights[point] * diag_im[point]
+            bond = bond + weights[point] * (square * bond_im[point])
         dens_ref[slot] = -inv_pi * dens
         bond_ref[slot] = -2.0 * inv_pi * bond
-        return reciprocal(are_ref[slot] - square * next_re, aim_ref[slot] - square * next_im)
+        return reciprocal(onsite_re - square * next_re, onsite_im - square * next_im)
 
     lax.fori_loop(0, count, backward_body, (from_re, from_im))
+    for slot in range(slots):
+        dens = dens_ref[slot]
+        bond = bond_ref[slot]
+        for row in range(rows):
+            target = low_ref if row < rows // 2 else high_ref
+            lane = (row % (rows // 2)) * 128
+            target[0, slot:slot + 1, lane:lane + 128] = dens[row:row + 1]
+            target[1, slot:slot + 1, lane:lane + 128] = bond[row:row + 1]
 
 
 def shards(
@@ -143,35 +183,26 @@
     rows = modes // 128
     here = lax.axis_index("slab")
     devices = lax.axis_size("slab")
-    count = lengths[here]
-    place = jnp.arange(slots, dtype=jnp.int32)
-    first_on = ((here == 0) & (place == 0)).astype(jnp.float32)[:, None, None, None]
-    last_on = ((here == devices - 1) & (place == count - 1)).astype(jnp.float32)[:, None, None, None]
-    energies = e_low + e_step * energy_index.astype(jnp.float32)
-    weights = weight_code.astype(jnp.float32) / (32.0 * points * lax.axis_size("energy"))
-    levels = (mode_floor[None, :] + onsite_noise).reshape(slots, 1, rows, 128)
-    shift = lead_shift.reshape(1, points, 2, rows, 128)
-    width = lead_width.reshape(1, points, 2, rows, 128)
-    onsite_re = (
-        energies[None, :, None, None]
-        - levels
-        - first_on * shift[:, :, 0]
-        - last_on * shift[:, :, 1]
-    )
-    onsite_im = broaden + first_on * width[:, :, 0] + last_on * width[:, :, 1]
-    onsite_im = onsite_im + jnp.zeros_like(onsite_re)
-    coupling_rows = hopping.reshape(slots, rows, 128)
-    count_arr = count.reshape(1)
+    groups = lax.axis_size("energy")
+    table = jnp.concatenate(
+        [
+            mode_floor[None, :] + onsite_noise,
+            hopping,
+            lead_shift.reshape(2 * points, modes),
+            lead_width.reshape(2 * points, modes),
+        ],
+        axis=0,
+    ).reshape(2 * slots + 4 * points, rows, 128)
     here_arr = here.astype(jnp.int32).reshape(1)
     smem = pl.BlockSpec(memory_space=pltpu.SMEM)
     vmem = pl.BlockSpec(memory_space=pltpu.VMEM)
 
     packed = pl.pallas_call(
-        summary_kernel,
+        functools.partial(summary_kernel, slots=slots, points=points, devices=devices),
         out_shape=jax.ShapeDtypeStruct((6 * points, rows, 128), jnp.float32),
-        in_specs=[smem, vmem, vmem, vmem],
+        in_specs=[smem, smem, smem, vmem],
         out_specs=vmem,
-    )(count_arr, onsite_re, onsite_im, coupling_rows)
+    )(here_arr, lengths, energy_index, table)
     mixed = devices & (devices - 1) == 0
     if mixed:
         every = packed
@@ -185,28 +216,31 @@
         every = every.reshape((devices,) + packed.shape)
     else:
         every = lax.all_gather(packed, "slab")
-    density, bond_density = pl.pallas_call(
-        functools.partial(final_kernel, mixed=mixed),
-        out_shape=(
-            jax.ShapeDtypeStruct((slots, rows, 128), jnp.float32),
-            jax.ShapeDtypeStruct((slots, rows, 128), jnp.float32),
+    half = jax.ShapeDtypeStruct((2, slots, modes // 2), jnp.float32)
+    low, high = pl.pallas_call(
+        functools.partial(
+            final_kernel, slots=slots, points=points, mixed=mixed,
+            scale=1.0 / (32.0 * points * groups),
         ),
-        in_specs=[smem, smem, smem, vmem, vmem, vmem, vmem],
+        out_shape=(half, half),
+        in_specs=[smem, smem, smem, smem, vmem, vmem],
         out_specs=(vmem, vmem),
         scratch_shapes=[
             pltpu.VMEM((slots, points, rows, 128), jnp.float32),
             pltpu.VMEM((slots, points, rows, 128), jnp.float32),
+            pltpu.VMEM((slots, rows, 128), jnp.float32),
+            pltpu.VMEM((slots, rows, 128), jnp.float32),
         ],
-    )(here_arr, count_arr, weights, every, onsite_re, onsite_im, coupling_rows)
-    both = jnp.stack([density.reshape(slots, modes), bond_density.reshape(slots, modes)])
-    if lax.axis_size("energy") == 2:
-        halves = both.reshape(2, slots, 2, modes // 2)
+    )(here_arr, lengths, energy_index, weight_code, every, table)
+    if groups == 2:
         lower = lax.axis_index("energy") == 0
-        mine = jnp.where(lower, halves[:, :, 0], halves[:, :, 1])
-        theirs = jnp.where(lower, halves[:, :, 1], halves[:, :, 0])
+        mine = jnp.where(lower, low, high)
+        theirs = jnp.where(lower, high, low)
         both = mine + lax.ppermute(theirs, "energy", [(0, 1), (1, 0)])
     else:
-        both = lax.psum_scatter(both, "energy", scatter_dimension=2, tiled=True)
+        both = lax.psum_scatter(
+            jnp.concatenate([low, high], axis=2), "energy", scatter_dimension=2, tiled=True
+        )
     return (both[0], both[1])
 
 

time: 52.2 us -> 48.5 us (0.929)
  local copies, waits for them, and re-layouts: 7.99 us -> 5.02 us
  waiting for transfers between devices: 23.8 us -> 26.7 us
  Pallas kernels: 6.99 us -> 4.54 us
  between operations: 1.4 us -> 0.74 us
    pallas_call x2, Pallas kernels: 6.99 us -> 4.54 us  [the longest x1 2.75 us: shards(): pl.pallas_call(functools.partial(final_kernel, slots=slots, points=points...]
    ppermute x4, waiting for transfers between devices: 20.9 us -> 23.2 us  [shards(): every = jnp.stack([every, lax.ppermute(every, 'slab', pairs)], axis=level)]
    another operation x3 -> x0, local copies, waits for them, and re-layouts: 1.76 us -> none  [shards(): jnp.stack([density.reshape(slots, modes), bond_density.reshape(slots, mod...]
    add x2 -> x0, other arithmetic: 1.63 us -> none  [the longest x1 0.97 us: shards(): onsite_im = broaden + first_on * width[:, :, 0] + last_on * width[:, :, 1]]
    concatenate x0 -> x3, local copies, waits for them, and re-layouts: none -> 1.58 us  [shards(): jnp.concatenate([mode_floor[None, :] + onsite_noise, hopping, lead_shift....]
    reshape x2 -> x0, local copies, waits for them, and re-layouts: 1.57 us -> none  [the longest x1 0.79 us: shards(): width = lead_width.reshape(1, points, 2, rows, 128)]
    dynamic_slice x1 -> x0, local copies, waits for them, and re-layouts: 1.24 us -> none  [shards(): count = lengths[here]]
    add x1, other arithmetic: 0.01 us -> 0.86 us  [shards(): both = mine + lax.ppermute(theirs, 'energy', [(0, 1), (1, 0)])]
  transfers between devices with their start and end apart: 5 -> 5, of which waited for: 5 -> 5; matrix products, arithmetic and copies ran while one was open for 1% -> 0% of each run, Pallas kernels for 0% -> 0%
where the time goes in v6:
time: 48.5 us; the launch traced here: 48.1 us
  waiting for transfers between devices  26.7 us (55%)
  starting transfers between devices  7.28 us (15%)
  local copies, waits for them, and re-layouts  5.02 us (10%)
  Pallas kernels  4.54 us (9%)
  other arithmetic  3.83 us (8%)
  between operations  0.74 us (2%)
    ppermute x4, waiting for transfers between devices, shards(): every = jnp.stack([every, lax.ppermute(every, 'slab', pairs)], axis=level)  23.2 us
    ppermute x4, starting transfers between devices, shards(): every = jnp.stack([every, lax.ppermute(every, 'slab', pairs)], axis=level)  5.81 us
    ppermute x1, waiting for transfers between devices, shards(): both = mine + lax.ppermute(theirs, 'energy', [(0, 1), (1, 0)])  3.48 us
    pallas_call x1, Pallas kernels, shards(): pl.pallas_call(functools.partial(final_kernel, slots=slots, points=points...  2.75 us
    pallas_call x1, Pallas kernels, shards(): pl.pallas_call(functools.partial(summary_kernel, slots=slots, points=poin...  1.79 us
    concatenate x3, local copies, waits for them, and re-layouts, shards(): jnp.concatenate([mode_floor[None, :] + onsite_noise, hopping, lead_shift....  1.58 us
    unnamed x7, local copies, waits for them, and re-layouts  1.55 us
    ppermute x1, starting transfers between devices, shards(): both = mine + lax.ppermute(theirs, 'energy', [(0, 1), (1, 0)])  1.47 us
  transfers between devices with their start and end apart: 5, of which 5 were waited for; matrix products, arithmetic and copies ran while one was open for 0% of the time, Pallas kernels for 0%

profile of v6, /device:TPU:0, one launch (start us, length us, event | category | flops | bytes accessed | tf_op | source)
XLA Modules:
  0.0 48.1 jit_solution(5852010837973225884)
XLA Ops:
  0.6 0.8 %concatenate.14 = f32[8,8,128]{2,1,0:T(8,128)S(1)} reshape(f32[4,2,1024]{2,1,0:T(2,128)} %param.14) | data formatting | bytes 65536 | tf_op jit(solution)/shard_map/concatenate | solution.py:187
  1.4 0.8 %concatenate.15 = f32[8,8,128]{2,1,0:T(8,128)S(1)} reshape(f32[4,2,1024]{2,1,0:T(2,128)} %param.15) | data formatting | bytes 65536 | tf_op jit(solution)/shard_map/concatenate | solution.py:187
  2.2 0.9 %add_bitcast_fusion = f32[2,8,8,128]{3,1,2,0:T(8,128)S(1)} fusion(f32[16,1024]{1,0:T(8,128)} %param.9, f32[1024]{0:T(1024)} %param.8), kind=kLoop, calls=%fused_computation.5 | loop fusion | flops 16384 | bytes 135168
  3.1 0.9 %copy.12 = f32[2,8,8,128]{3,2,1,0:T(8,128)S(1)} copy(f32[2,8,8,128]{3,1,2,0:T(8,128)} %bitcast.30) | data formatting | bytes 131072
  4.0 0.0 copy-start
  4.0 0.7 %copy-done = f32[48,8,128]{2,1,0:T(8,128)} copy-done((f32[48,8,128]{2,1,0:T(8,128)}, f32[48,8,128]{2,1,0:T(8,128)S(1)}, u32[]{:S(2)}) %copy-start) | copy-done | bytes 196632
  4.7 1.8 %shard_map.95 = f32[24,8,128]{2,1,0:T(8,128)} custom-call(s32[1]{0:T(128)} %bitcast.here_ref, s32[16]{0:T(128)} %length_ref.3, s32[4]{0:T(128)} %energy_ref.3, f32[48,8,128]{2,1,0:T(8,128)} %copy-done), custom_call_target="tpu_custom_call" | custom-call | tf_op jit(solution)/shard_map/pallas_call | solution.py:200
  6.5 4.2 %collective-permute-start = (f32[24,8,128]{2,1,0:T(8,128)}, f32[24,8,128]{2,1,0:T(8,128)S(1)}, u32[]{:S(2)}, u32[]{:S(2)}) collective-permute-start(f32[24,8,128]{2,1,0:T(8,128)} %shard_map.95), channel_id=1, source_target_pairs={{0,16},{2,18},{4,20},{6,22},{8,24},{10,26},{12,28},{14,30},{16,0},... | collective-permute-start | bytes 294920 | tf_op jit(solution)/shard_map/ppermute | solution.py:213
  10.6 5.7 %collective-permute-done = f32[24,8,128]{2,1,0:T(8,128)S(1)} collective-permute-done((f32[24,8,128]{2,1,0:T(8,128)}, f32[24,8,128]{2,1,0:T(8,128)S(1)}, u32[]{:S(2)}, u32[]{:S(2)}) %collective-permute-start) | collective-permute-done | bytes 98336 | tf_op jit(solution)/shard_map/ppermute | solution.py:213
  16.3 0.9 %fusion = (f32[2,1,24,8,128]{4,3,2,0,1:T(8,128)S(1)}, f32[2,24,8,128]{3,2,1,0:T(8,128)S(1)}) fusion(f32[1,24,8,128]{3,2,1,0:T(8,128)S(1)} %bitcast.29, f32[1,24,8,128]{3,2,1,0:T(8,128)} %bitcast.25), kind=kLoop, calls=%fused_computation.13 | loop fusion | flops 49152 | bytes 589824 | tf_op jit(solution)/shard_map/stack | solution.py:213
  17.2 0.1 collective-permute-start.1
  17.3 6.6 %collective-permute-done.1 = f32[2,24,8,128]{3,2,1,0:T(8,128)S(1)} collective-permute-done((f32[2,24,8,128]{3,2,1,0:T(8,128)S(1)}, f32[2,24,8,128]{3,2,1,0:T(8,128)S(1)}, u32[]{:S(2)}, u32[]{:S(2)}) %collective-permute-start.1) | collective-permute-done | bytes 196640 | tf_op jit(solution)/shard_map/ppermute | solution.py:213
  24.0 0.1 fusion.1
  24.0 1.5 %collective-permute-start.2 = (f32[2,2,24,8,128]{4,3,2,0,1:T(8,128)S(1)}, f32[2,2,24,8,128]{4,3,2,0,1:T(8,128)S(1)}, u32[]{:S(2)}, u32[]{:S(2)}) collective-permute-start(f32[2,2,24,8,128]{4,3,2,0,1:T(8,128)S(1)} %get-tuple-element.9), channel_id=1, source_target_pairs={{0,4},{2,6},{4,0},{6,2},{8,12},{10,14},{12,8},{14,10},{16,20},{18,... | collective-permute-start | bytes 1179656 | tf_op jit(solution)/shard_map/ppermute | solution.py:213
  25.5 8.6 %collective-permute-done.2 = f32[2,2,24,8,128]{4,3,2,0,1:T(8,128)S(1)} collective-permute-done((f32[2,2,24,8,128]{4,3,2,0,1:T(8,128)S(1)}, f32[2,2,24,8,128]{4,3,2,0,1:T(8,128)S(1)}, u32[]{:S(2)}, u32[]{:S(2)}) %collective-permute-start.2) | collective-permute-done | bytes 393248 | tf_op jit(solution)/shard_map/ppermute | solution.py:213
  34.1 0.2 fusion.2
  34.3 0.1 collective-permute-start.3
  34.4 2.3 %collective-permute-done.3 = f32[2,2,2,24,8,128]{5,4,3,0,1,2:T(8,128)S(1)} collective-permute-done((f32[2,2,2,24,8,128]{5,4,3,0,1,2:T(8,128)S(1)}, f32[2,2,2,24,8,128]{5,4,3,0,1,2:T(8,128)S(1)}, u32[]{:S(2)}, u32[]{:S(2)}) %collective-permute-start.3) | collective-permute-done | bytes 786464 | tf_op jit(solution)/shard_map/ppermute | solution.py:213
  36.6 0.1 pad_maximum_fusion
  36.8 1.3 %copy.10 = f32[2,2,2,2,24,8,128]{6,5,4,3,2,1,0:T(8,128)} copy(f32[2,2,2,2,24,8,128]{6,5,4,0,1,2,3:T(8,128)S(1)} %pad_maximum_fusion) | data formatting | bytes 3145728 | tf_op jit(solution)/shard_map/stack | solution.py:213
  38.0 2.7 %shard_map.96 = (f32[2,16,512]{2,1,0:T(8,128)}, f32[2,16,512]{2,1,0:T(8,128)}) custom-call(s32[1]{0:T(128)} %bitcast.here_ref, s32[16]{0:T(128)} %length_ref.3, s32[4]{0:T(128)} %energy_ref.3, s32[4]{0:T(128)} %code_ref.1, f32[16,24,8,128]{3,2,1,0:T(8,128)} %bitcast.22, f32[48,8,128]{2,1,0:T(8,128)} %copy-done), custom_call_target="tpu_custom_call" | custom-call | tf_op jit(solution)/shard_map/pallas_call | solution.py:220
  40.8 0.9 %broadcast_select_fusion = f32[2,16,512]{2,1,0:T(8,128)S(1)} fusion(f32[2,16,512]{2,1,0:T(8,128)} %get-tuple-element.5, f32[2,16,512]{2,1,0:T(8,128)} %get-tuple-element.4, pred[]{:T(512)S(6)} %eq.3), kind=kLoop, calls=%fused_computation.8 | loop fusion | flops 16384 | bytes 196609 | tf_op jit(solution)/shard_map/jit(_where)/select_n | solution.py:238
  41.7 1.5 %collective-permute-start.4 = (f32[2,16,512]{2,1,0:T(8,128)S(1)}, f32[2,16,512]{2,1,0:T(8,128)S(1)}, u32[]{:S(2)}, u32[]{:S(2)}) collective-permute-start(f32[2,16,512]{2,1,0:T(8,128)S(1)} %broadcast_select_fusion), channel_id=1, source_target_pairs={{0,1},{1,0},{2,3},{3,2},{4,5},{5,4},{6,7},{7,6},{8,9},{9,8},{10,11... | collective-permute-start | bytes 196616 | tf_op jit(solution)/shard_map/ppermute | solution.py:239
  43.1 3.5 %collective-permute-done.4 = f32[2,16,512]{2,1,0:T(8,128)S(1)} collective-permute-done((f32[2,16,512]{2,1,0:T(8,128)S(1)}, f32[2,16,512]{2,1,0:T(8,128)S(1)}, u32[]{:S(2)}, u32[]{:S(2)}) %collective-permute-start.4) | collective-permute-done | bytes 65568 | tf_op jit(solution)/shard_map/ppermute | solution.py:239
  46.6 0.9 %select_add_fusion = f32[2,16,512]{2,1,0:T(8,128)S(1)} fusion(f32[2,16,512]{2,1,0:T(8,128)S(1)} %collective-permute-done.4, f32[2,16,512]{2,1,0:T(8,128)} %get-tuple-element.4, f32[2,16,512]{2,1,0:T(8,128)} %get-tuple-element.5, pred[]{:T(512)S(6)} %eq.3), kind=kLoop, calls=%fused_computation.4 | loop fusion | flops 32768 | bytes 262145 | tf_op jit(solution)/shard_map/add | solution.py:239
  47.5 0.6 %slice_bitcast_fusion = (f32[16,512]{1,0:T(8,128)}, f32[16,512]{1,0:T(8,128)}) fusion(f32[2,16,512]{2,1,0:T(8,128)S(1)} %select_add_fusion), kind=kLoop, calls=%fused_computation.6 | loop fusion | bytes 131072 | tf_op jit(solution)/shard_map/squeeze | solution.py:244
  (5 shorter events, 0.0 us)
Async XLA Ops:
  4.0 0.7 %copy-start = (f32[48,8,128]{2,1,0:T(8,128)}, f32[48,8,128]{2,1,0:T(8,128)S(1)}, u32[]{:S(2)}) copy-start(f32[48,8,128]{2,1,0:T(8,128)S(1)} %constant_dynamic-update-slice_fusion.table_ref) | copy-start | bytes 589828
  6.5 9.9 %collective-permute-start = (f32[24,8,128]{2,1,0:T(8,128)}, f32[24,8,128]{2,1,0:T(8,128)S(1)}, u32[]{:S(2)}, u32[]{:S(2)}) collective-permute-start(f32[24,8,128]{2,1,0:T(8,128)} %shard_map.95), channel_id=1, source_target_pairs={{0,16},{2,18},{4,20},{6,22},{8,24},{10,26},{12,28},{14,30},{16,0},... | collective-permute-start | bytes 294920 | tf_op jit(solution)/shard_map/ppermute | solution.py:213
  17.2 6.7 %collective-permute-start.1 = (f32[2,24,8,128]{3,2,1,0:T(8,128)S(1)}, f32[2,24,8,128]{3,2,1,0:T(8,128)S(1)}, u32[]{:S(2)}, u32[]{:S(2)}) collective-permute-start(f32[2,24,8,128]{3,2,1,0:T(8,128)S(1)} %get-tuple-element.11), channel_id=1, source_target_pairs={{0,8},{2,10},{4,12},{6,14},{8,0},{10,2},{12,4},{14,6},{16,24},{18,... | collective-permute-start | bytes 589832 | tf_op jit(solution)/shard_map/ppermute | solution.py:213
  24.0 10.1 %collective-permute-start.2 = (f32[2,2,24,8,128]{4,3,2,0,1:T(8,128)S(1)}, f32[2,2,24,8,128]{4,3,2,0,1:T(8,128)S(1)}, u32[]{:S(2)}, u32[]{:S(2)}) collective-permute-start(f32[2,2,24,8,128]{4,3,2,0,1:T(8,128)S(1)} %get-tuple-element.9), channel_id=1, source_target_pairs={{0,4},{2,6},{4,0},{6,2},{8,12},{10,14},{12,8},{14,10},{16,20},{18,... | collective-permute-start | bytes 1179656 | tf_op jit(solution)/shard_map/ppermute | solution.py:213
  34.3 2.4 %collective-permute-start.3 = (f32[2,2,2,24,8,128]{5,4,3,0,1,2:T(8,128)S(1)}, f32[2,2,2,24,8,128]{5,4,3,0,1,2:T(8,128)S(1)}, u32[]{:S(2)}, u32[]{:S(2)}) collective-permute-start(f32[2,2,2,24,8,128]{5,4,3,0,1,2:T(8,128)S(1)} %get-tuple-element.7), channel_id=1, source_target_pairs={{0,2},{2,0},{4,6},{6,4},{8,10},{10,8},{12,14},{14,12},{16,18},{18,... | collective-permute-start | bytes 2359304 | tf_op jit(solution)/shard_map/ppermute | solution.py:213
  41.7 5.0 %collective-permute-start.4 = (f32[2,16,512]{2,1,0:T(8,128)S(1)}, f32[2,16,512]{2,1,0:T(8,128)S(1)}, u32[]{:S(2)}, u32[]{:S(2)}) collective-permute-start(f32[2,16,512]{2,1,0:T(8,128)S(1)} %broadcast_select_fusion), channel_id=1, source_target_pairs={{0,1},{1,0},{2,3},{3,2},{4,5},{5,4},{6,7},{7,6},{8,9},{9,8},{10,11... | collective-permute-start | bytes 196616 | tf_op jit(solution)/shard_map/ppermute | solution.py:239

commit v7 on v6

--- a/solution.py
+++ b/solution.py
@@ -93,15 +93,22 @@
         out_ref[index * points:(index + 1) * points] = value
 
 
-def final_kernel(here_ref, length_ref, energy_ref, code_ref, every_ref, table_ref,
-                 low_ref, high_ref, left_re_ref, left_im_ref, dens_ref, bond_ref, *, slots, points, mixed, scale):
+def final_kernel(here_ref, group_ref, length_ref, energy_ref, code_ref, every_ref, table_ref,
+                 dens_out_ref, bond_out_ref, theirs_ref, left_re_ref, left_im_ref, dens_ref, bond_ref, *, slots, points, mixed, scale):
     devices = every_ref.shape[0]
     here = here_ref[0]
     count = length_ref[here]
     rows = table_ref.shape[1]
 
+    bits = devices.bit_length() - 1
+
     def field(device, index):
-        block = jnp.bitwise_xor(device, here) if mixed else device
+        block = device
+        if mixed:
+            offset = jnp.bitwise_xor(device, here)
+            block = 0
+            for bit in range(bits):
+                block = block * 2 + jnp.bitwise_and(jnp.right_shift(offset, bit), 1)
         return every_ref[block, index * points:(index + 1) * points]
 
     def into_body(device, run):
@@ -164,14 +171,17 @@
         return reciprocal(onsite_re - square * next_re, onsite_im - square * next_im)
 
     lax.fori_loop(0, count, backward_body, (from_re, from_im))
+    lower = group_ref[0] == 0
+    half = rows // 2
     for slot in range(slots):
         dens = dens_ref[slot]
         bond = bond_ref[slot]
-        for row in range(rows):
-            target = low_ref if row < rows // 2 else high_ref
-            lane = (row % (rows // 2)) * 128
-            target[0, slot:slot + 1, lane:lane + 128] = dens[row:row + 1]
-            target[1, slot:slot + 1, lane:lane + 128] = bond[row:row + 1]
+        for row in range(half):
+            lane = row * 128
+            for kind, value, mine_ref in ((0, dens, dens_out_ref), (1, bond, bond_out_ref)):
+                low, high = value[row:row + 1], value[row + half:row + half + 1]
+                mine_ref[slot:slot + 1, lane:lane + 128] = jnp.where(lower, low, high)
+                theirs_ref[kind, slot:slot + 1, lane:lane + 128] = jnp.where(lower, high, low)
 
 
 def shards(
@@ -205,42 +215,40 @@
     )(here_arr, lengths, energy_index, table)
     mixed = devices & (devices - 1) == 0
     if mixed:
-        every = packed
+        every = packed[None]
         distance = devices // 2
-        level = 0
         while distance >= 1:
             pairs = [(device, device ^ distance) for device in range(devices)]
-            every = jnp.stack([every, lax.ppermute(every, "slab", pairs)], axis=level)
+            every = jnp.concatenate([every, lax.ppermute(every, "slab", pairs)], axis=0)
             distance //= 2
-            level += 1
-        every = every.reshape((devices,) + packed.shape)
     else:
         every = lax.all_gather(packed, "slab")
-    half = jax.ShapeDtypeStruct((2, slots, modes // 2), jnp.float32)
-    low, high = pl.pallas_call(
+    half = jax.ShapeDtypeStruct((slots, modes // 2), jnp.float32)
+    group_arr = lax.axis_index("energy").astype(jnp.int32).reshape(1)
+    density, bond_density, theirs = pl.pallas_call(
         functools.partial(
             final_kernel, slots=slots, points=points, mixed=mixed,
             scale=1.0 / (32.0 * points * groups),
         ),
-        out_shape=(half, half),
-        in_specs=[smem, smem, smem, smem, vmem, vmem],
-        out_specs=(vmem, vmem),
+        out_shape=(half, half, jax.ShapeDtypeStruct((2, slots, modes // 2), jnp.float32)),
+        in_specs=[smem, smem, smem, smem, smem, vmem, vmem],
+        out_specs=(vmem, vmem, vmem),
         scratch_shapes=[
             pltpu.VMEM((slots, points, rows, 128), jnp.float32),
             pltpu.VMEM((slots, points, rows, 128), jnp.float32),
             pltpu.VMEM((slots, rows, 128), jnp.float32),
             pltpu.VMEM((slots, rows, 128), jnp.float32),
         ],
-    )(here_arr, lengths, energy_index, weight_code, every, table)
+    )(here_arr, group_arr, lengths, energy_index, weight_code, every, table)
     if groups == 2:
-        lower = lax.axis_index("energy") == 0
-        mine = jnp.where(lower, low, high)
-        theirs = jnp.where(lower, high, low)
-        both = mine + lax.ppermute(theirs, "energy", [(0, 1), (1, 0)])
-    else:
-        both = lax.psum_scatter(
-            jnp.concatenate([low, high], axis=2), "energy", scatter_dimension=2, tiled=True
-        )
+        theirs = lax.ppermute(theirs, "energy", [(0, 1), (1, 0)])
+        return (density + theirs[0], bond_density + theirs[1])
+    lower = lax.axis_index("energy") == 0
+    both = jnp.stack([
+        jnp.where(lower, jnp.concatenate([density, theirs[0]], axis=1), jnp.concatenate([theirs[0], density], axis=1)),
+        jnp.where(lower, jnp.concatenate([bond_density, theirs[1]], axis=1), jnp.concatenate([theirs[1], bond_density], axis=1)),
+    ])
+    both = lax.psum_scatter(both, "energy", scatter_dimension=2, tiled=True)
     return (both[0], both[1])
 
 

time: 48.5 us -> 50.2 us (1.035)
  other arithmetic: 3.83 us -> 5.91 us
  waiting for transfers between devices: 26.7 us -> 28.1 us
  starting transfers between devices: 7.28 us -> 6.23 us
  local copies, waits for them, and re-layouts: 5.02 us -> 4.39 us
    concatenate x0 -> x3, other arithmetic: none -> 3.66 us  [shards(): every = jnp.concatenate([every, lax.ppermute(every, 'slab', pairs)], axis=0)]
    ppermute x5, waiting for transfers between devices: 26.7 us -> 28.1 us  [the longest x4 24.4 us: shards(): every = jnp.concatenate([every, lax.ppermute(every, 'slab', pairs)], axis=0)]
    another operation x4 -> x0, other arithmetic: 1.27 us -> none  [shards(): every = jnp.stack([every, lax.ppermute(every, 'slab', pairs)], axis=level)]
    another operation x1 -> x0, local copies, waits for them, and re-layouts: 1.26 us -> none  [shards(): every = jnp.stack([every, lax.ppermute(every, 'slab', pairs)], axis=level)]
    unnamed x7 -> x15, local copies, waits for them, and re-layouts: 1.55 us -> 2.76 us
    ppermute x5, starting transfers between devices: 7.28 us -> 6.23 us  [the longest x4 5.25 us: shards(): every = jnp.concatenate([every, lax.ppermute(every, 'slab', pairs)], axis=0)]
    select_n x1 -> x0, other arithmetic: 0.85 us -> none  [shards(): theirs = jnp.where(lower, high, low)]
    squeeze x1 -> x0, local copies, waits for them, and re-layouts: 0.63 us -> none  [shards(): return (both[0], both[1])]
where the time goes in v7:
time: 50.2 us; the launch traced here: 49.8 us
  waiting for transfers between devices  28.1 us (56%)
  starting transfers between devices  6.23 us (12%)
  other arithmetic  5.91 us (12%)
  Pallas kernels  4.45 us (9%)
  local copies, waits for them, and re-layouts  4.39 us (9%)
  between operations  0.74 us (1%)
    ppermute x4, waiting for transfers between devices, shards(): every = jnp.concatenate([every, lax.ppermute(every, 'slab', pairs)], axis=0)  24.4 us
    ppermute x4, starting transfers between devices, shards(): every = jnp.concatenate([every, lax.ppermute(every, 'slab', pairs)], axis=0)  5.25 us
    ppermute x1, waiting for transfers between devices, shards(): theirs = lax.ppermute(theirs, 'energy', [(0, 1), (1, 0)])  3.74 us
    concatenate x3, other arithmetic, shards(): every = jnp.concatenate([every, lax.ppermute(every, 'slab', pairs)], axis=0)  3.66 us
    unnamed x15, local copies, waits for them, and re-layouts  2.76 us
    pallas_call x1, Pallas kernels, shards(): pl.pallas_call(functools.partial(final_kernel, slots=slots, points=points...  2.71 us
    pallas_call x1, Pallas kernels, shards(): pl.pallas_call(functools.partial(summary_kernel, slots=slots, points=poin...  1.75 us
    concatenate x3, local copies, waits for them, and re-layouts, shards(): jnp.concatenate([mode_floor[None, :] + onsite_noise, hopping, lead_shift....  1.58 us
  transfers between devices with their start and end apart: 5, of which 5 were waited for; matrix products, arithmetic and copies ran while one was open for 0% of the time, Pallas kernels for 0%

profile of v7, /device:TPU:0, one launch (start us, length us, event | category | flops | bytes accessed | tf_op | source)
XLA Modules:
  0.0 49.8 jit_solution(9868913316175352426)
XLA Ops:
  0.6 0.8 %add_bitcast_fusion = f32[2,8,8,128]{3,1,2,0:T(8,128)S(1)} fusion(f32[16,1024]{1,0:T(8,128)} %param.9, f32[1024]{0:T(1024)} %param.8), kind=kLoop, calls=%fused_computation.3 | loop fusion | flops 16384 | bytes 135168
  1.5 0.9 %copy.11 = f32[2,8,8,128]{3,2,1,0:T(8,128)S(1)} copy(f32[2,8,8,128]{3,1,2,0:T(8,128)} %bitcast.23) | data formatting | bytes 131072
  2.4 0.8 %concatenate.29 = f32[8,8,128]{2,1,0:T(8,128)S(1)} reshape(f32[4,2,1024]{2,1,0:T(2,128)} %param.14) | data formatting | bytes 65536 | tf_op jit(solution)/shard_map/concatenate | solution.py:197
  3.2 0.8 %concatenate.30 = f32[8,8,128]{2,1,0:T(8,128)S(1)} reshape(f32[4,2,1024]{2,1,0:T(2,128)} %param.15) | data formatting | bytes 65536 | tf_op jit(solution)/shard_map/concatenate | solution.py:197
  4.0 0.0 copy-start.2
  4.0 0.7 %copy-done.2 = f32[48,8,128]{2,1,0:T(8,128)} copy-done((f32[48,8,128]{2,1,0:T(8,128)}, f32[48,8,128]{2,1,0:T(8,128)S(1)}, u32[]{:S(2)}) %copy-start.2) | copy-done | bytes 196632
  4.7 1.7 %shard_map.95 = f32[24,8,128]{2,1,0:T(8,128)} custom-call(s32[1]{0:T(128)} %bitcast.here_ref, s32[16]{0:T(128)} %length_ref.3, s32[4]{0:T(128)} %energy_ref.3, f32[48,8,128]{2,1,0:T(8,128)} %copy-done.2), custom_call_target="tpu_custom_call" | custom-call | tf_op jit(solution)/shard_map/pallas_call | solution.py:210
  6.4 0.0 copy-start
  6.4 4.0 %collective-permute-start = (f32[1,24,8,128]{3,2,1,0:T(8,128)}, f32[1,24,8,128]{3,2,1,0:T(8,128)S(1)}, u32[]{:S(2)}, u32[]{:S(2)}) collective-permute-start(f32[1,24,8,128]{3,2,1,0:T(8,128)} %bitcast.17), channel_id=1, source_target_pairs={{0,16},{2,18},{4,20},{6,22},{8,24},{10,26},{12,28},{14,30},{16,0},... | collective-permute-start | bytes 294920 | tf_op jit(solution)/shard_map/ppermute | solution.py:222
  10.5 6.0 %collective-permute-done = f32[1,24,8,128]{3,2,1,0:T(8,128)S(1)} collective-permute-done((f32[1,24,8,128]{3,2,1,0:T(8,128)}, f32[1,24,8,128]{3,2,1,0:T(8,128)S(1)}, u32[]{:S(2)}, u32[]{:S(2)}) %collective-permute-start) | collective-permute-done | bytes 98336 | tf_op jit(solution)/shard_map/ppermute | solution.py:222
  16.4 0.9 %pad_maximum_fusion.2 = f32[2,24,8,128]{3,2,1,0:T(8,128)S(1)} fusion(f32[1,24,8,128]{3,2,1,0:T(8,128)S(1)} %collective-permute-done, f32[1,24,8,128]{3,2,1,0:T(8,128)} %bitcast.18), kind=kLoop, calls=%fused_computation.2 | loop fusion | flops 49152 | bytes 393216 | tf_op jit(solution)/shard_map/concatenate | solution.py:222
  17.3 0.2 collective-permute-start.1
  17.5 6.8 %collective-permute-done.1 = f32[2,24,8,128]{3,2,1,0:T(8,128)S(1)} collective-permute-done((f32[2,24,8,128]{3,2,1,0:T(8,128)S(1)}, f32[2,24,8,128]{3,2,1,0:T(8,128)S(1)}, u32[]{:S(2)}, u32[]{:S(2)}) %collective-permute-start.1) | collective-permute-done | bytes 196640 | tf_op jit(solution)/shard_map/ppermute | solution.py:222
  24.2 0.9 %pad_maximum_fusion.1 = f32[4,24,8,128]{3,2,1,0:T(8,128)S(1)} fusion(f32[2,24,8,128]{3,2,1,0:T(8,128)S(1)} %collective-permute-done.1, f32[1,24,8,128]{3,2,1,0:T(8,128)S(1)} %collective-permute-done, f32[1,24,8,128]{3,2,1,0:T(8,128)} %bitcast.19), kind=kLoop, calls=%fused_computation.1 | loop fusion | flops 196608 | bytes 786432 | tf_op jit(solution)/shard_map/concatenate | solution.py:222
  25.2 1.1 %collective-permute-start.2 = (f32[4,24,8,128]{3,2,1,0:T(8,128)S(1)}, f32[4,24,8,128]{3,2,1,0:T(8,128)S(1)}, u32[]{:S(2)}, u32[]{:S(2)}) collective-permute-start(f32[4,24,8,128]{3,2,1,0:T(8,128)S(1)} %pad_maximum_fusion.1), channel_id=1, source_target_pairs={{0,4},{2,6},{4,0},{6,2},{8,12},{10,14},{12,8},{14,10},{16,20},{18,... | collective-permute-start | bytes 1179656 | tf_op jit(solution)/shard_map/ppermute | solution.py:222
  26.2 9.2 %collective-permute-done.2 = f32[4,24,8,128]{3,2,1,0:T(8,128)S(1)} collective-permute-done((f32[4,24,8,128]{3,2,1,0:T(8,128)S(1)}, f32[4,24,8,128]{3,2,1,0:T(8,128)S(1)}, u32[]{:S(2)}, u32[]{:S(2)}) %collective-permute-start.2) | collective-permute-done | bytes 393248 | tf_op jit(solution)/shard_map/ppermute | solution.py:222
  35.5 1.8 %pad_maximum_fusion = f32[8,24,8,128]{3,2,1,0:T(8,128)} fusion(f32[4,24,8,128]{3,2,1,0:T(8,128)S(1)} %collective-permute-done.2, f32[2,24,8,128]{3,2,1,0:T(8,128)S(1)} %collective-permute-done.1, f32[1,24,8,128]{3,2,1,0:T(8,128)S(1)} %collective-permute-done, f32[1,24,8,128]{3,2,1,0:T(8,128)} %bitcast.20), kind=kLoop, calls=%fused_computation | loop fusion | flops 589824 | bytes 1572864 | tf_op jit(solution)/shard_map/concatenate | solution.py:222
  37.3 0.0 collective-permute-start.3
  37.3 0.0 copy-done
  37.4 2.4 %collective-permute-done.3 = f32[8,24,8,128]{3,2,1,0:T(8,128)S(1)} collective-permute-done((f32[8,24,8,128]{3,2,1,0:T(8,128)}, f32[8,24,8,128]{3,2,1,0:T(8,128)S(1)}, u32[]{:S(2)}, u32[]{:S(2)}) %collective-permute-start.3) | collective-permute-done | bytes 786464 | tf_op jit(solution)/shard_map/ppermute | solution.py:222
  39.8 0.1 constant_dynamic-update-slice_fusion.4.every_ref
  39.8 0.0 copy-start.1
  39.9 1.1 %copy-done.1 = f32[16,24,8,128]{3,2,1,0:T(8,128)} copy-done((f32[16,24,8,128]{3,2,1,0:T(8,128)}, f32[16,24,8,128]{3,2,1,0:T(8,128)S(1)}, u32[]{:S(2)}) %copy-start.1) | copy-done | bytes 1572888
  41.0 2.7 %shard_map.96 = (f32[16,512]{1,0:T(8,128)}, f32[16,512]{1,0:T(8,128)}, f32[2,16,512]{2,1,0:T(8,128)}) custom-call(s32[1]{0:T(128)} %bitcast.here_ref, s32[1]{0:T(128)} %bitcast.1.group_ref, s32[16]{0:T(128)} %length_ref.3, s32[4]{0:T(128)} %energy_ref.3, s32[4]{0:T(128)} %code_ref.1, f32[16,24,8,128]{3,2,1,0:T(8,128)} %copy-done.1, f32[48,8,128]{2,1,0:T(8,128)} %copy-done.2), custom_call_target="tpu_custom_call" | custom-call | tf_op jit(solution)/shard_map/pallas_call | solution.py:228
  43.7 1.0 %collective-permute-start.4 = (f32[2,16,512]{2,1,0:T(8,128)}, f32[2,16,512]{2,1,0:T(8,128)S(1)}, u32[]{:S(2)}, u32[]{:S(2)}) collective-permute-start(f32[2,16,512]{2,1,0:T(8,128)} %get-tuple-element.6), channel_id=1, source_target_pairs={{0,1},{1,0},{2,3},{3,2},{4,5},{5,4},{6,7},{7,6},{8,9},{9,8},{10,11... | collective-permute-start | bytes 196616 | tf_op jit(solution)/shard_map/ppermute | solution.py:244
  44.7 3.7 %collective-permute-done.4 = f32[2,16,512]{2,1,0:T(8,128)S(1)} collective-permute-done((f32[2,16,512]{2,1,0:T(8,128)}, f32[2,16,512]{2,1,0:T(8,128)S(1)}, u32[]{:S(2)}, u32[]{:S(2)}) %collective-permute-start.4) | collective-permute-done | bytes 65568 | tf_op jit(solution)/shard_map/ppermute | solution.py:244
  48.4 1.4 %fusion = (f32[16,512]{1,0:T(8,128)}, f32[16,512]{1,0:T(8,128)}) fusion(f32[16,512]{1,0:T(8,128)} %get-tuple-element.7, f32[2,16,512]{2,1,0:T(8,128)S(1)} %collective-permute-done.4, f32[16,512]{1,0:T(8,128)} %get-tuple-element.5), kind=kLoop, calls=%fused_computation.5 | loop fusion | flops 16384 | bytes 196608 | tf_op jit(solution)/shard_map/add | solution.py:245
  (9 shorter events, 0.1 us)
Async XLA Ops:
  4.0 0.7 %copy-start.2 = (f32[48,8,128]{2,1,0:T(8,128)}, f32[48,8,128]{2,1,0:T(8,128)S(1)}, u32[]{:S(2)}) copy-start(f32[48,8,128]{2,1,0:T(8,128)S(1)} %constant_dynamic-update-slice_fusion.table_ref) | copy-start | bytes 589828
  6.4 30.9 %copy-start = (f32[24,8,128]{2,1,0:T(8,128)S(1)}, f32[24,8,128]{2,1,0:T(8,128)}, u32[]{:S(2)}) copy-start(f32[24,8,128]{2,1,0:T(8,128)} %shard_map.95) | copy-start | bytes 294916
  6.4 10.0 %collective-permute-start = (f32[1,24,8,128]{3,2,1,0:T(8,128)}, f32[1,24,8,128]{3,2,1,0:T(8,128)S(1)}, u32[]{:S(2)}, u32[]{:S(2)}) collective-permute-start(f32[1,24,8,128]{3,2,1,0:T(8,128)} %bitcast.17), channel_id=1, source_target_pairs={{0,16},{2,18},{4,20},{6,22},{8,24},{10,26},{12,28},{14,30},{16,0},... | collective-permute-start | bytes 294920 | tf_op jit(solution)/shard_map/ppermute | solution.py:222
  17.3 6.9 %collective-permute-start.1 = (f32[2,24,8,128]{3,2,1,0:T(8,128)S(1)}, f32[2,24,8,128]{3,2,1,0:T(8,128)S(1)}, u32[]{:S(2)}, u32[]{:S(2)}) collective-permute-start(f32[2,24,8,128]{3,2,1,0:T(8,128)S(1)} %pad_maximum_fusion.2), channel_id=1, source_target_pairs={{0,8},{2,10},{4,12},{6,14},{8,0},{10,2},{12,4},{14,6},{16,24},{18,... | collective-permute-start | bytes 589832 | tf_op jit(solution)/shard_map/ppermute | solution.py:222
  25.2 10.3 %collective-permute-start.2 = (f32[4,24,8,128]{3,2,1,0:T(8,128)S(1)}, f32[4,24,8,128]{3,2,1,0:T(8,128)S(1)}, u32[]{:S(2)}, u32[]{:S(2)}) collective-permute-start(f32[4,24,8,128]{3,2,1,0:T(8,128)S(1)} %pad_maximum_fusion.1), channel_id=1, source_target_pairs={{0,4},{2,6},{4,0},{6,2},{8,12},{10,14},{12,8},{14,10},{16,20},{18,... | collective-permute-start | bytes 1179656 | tf_op jit(solution)/shard_map/ppermute | solution.py:222
  37.3 2.5 %collective-permute-start.3 = (f32[8,24,8,128]{3,2,1,0:T(8,128)}, f32[8,24,8,128]{3,2,1,0:T(8,128)S(1)}, u32[]{:S(2)}, u32[]{:S(2)}) collective-permute-start(f32[8,24,8,128]{3,2,1,0:T(8,128)} %pad_maximum_fusion), channel_id=1, source_target_pairs={{0,2},{2,0},{4,6},{6,4},{8,10},{10,8},{12,14},{14,12},{16,18},{18,... | collective-permute-start | bytes 2359304 | tf_op jit(solution)/shard_map/ppermute | solution.py:222
  39.8 1.1 %copy-start.1 = (f32[16,24,8,128]{3,2,1,0:T(8,128)}, f32[16,24,8,128]{3,2,1,0:T(8,128)S(1)}, u32[]{:S(2)}) copy-start(f32[16,24,8,128]{3,2,1,0:T(8,128)S(1)} %constant_dynamic-update-slice_fusion.4.every_ref) | copy-start | bytes 4718596
  43.7 4.7 %collective-permute-start.4 = (f32[2,16,512]{2,1,0:T(8,128)}, f32[2,16,512]{2,1,0:T(8,128)S(1)}, u32[]{:S(2)}, u32[]{:S(2)}) collective-permute-start(f32[2,16,512]{2,1,0:T(8,128)} %get-tuple-element.6), channel_id=1, source_target_pairs={{0,1},{1,0},{2,3},{3,2},{4,5},{5,4},{6,7},{7,6},{8,9},{9,8},{10,11... | collective-permute-start | bytes 196616 | tf_op jit(solution)/shard_map/ppermute | solution.py:244

commit v8 on v6

--- a/solution.py
+++ b/solution.py
@@ -93,37 +93,84 @@
         out_ref[index * points:(index + 1) * points] = value
 
 
-def final_kernel(here_ref, length_ref, energy_ref, code_ref, every_ref, table_ref,
-                 low_ref, high_ref, left_re_ref, left_im_ref, dens_ref, bond_ref, *, slots, points, mixed, scale):
-    devices = every_ref.shape[0]
+def join_coupled(left, right):
+    d_re, d_im = complex_mul(left[2], left[3], right[0], right[1])
+    inv_re, inv_im = reciprocal(1.0 - d_re, -d_im)
+    f_re, f_im = complex_mul(left[4], left[5], right[0], right[1])
+    f_re, f_im = complex_mul(f_re, f_im, inv_re, inv_im)
+    g_re, g_im = complex_mul(right[4], right[5], left[2], left[3])
+    g_re, g_im = complex_mul(g_re, g_im, inv_re, inv_im)
+    x_re, x_im = complex_mul(left[4], left[5], right[4], right[5])
+    x_re, x_im = complex_mul(x_re, x_im, inv_re, inv_im)
+    x_re, x_im = complex_mul(x_re, x_im, inv_re, inv_im)
+    return (left[0] + f_re, left[1] + f_im, right[2] + g_re, right[3] + g_im, x_re, x_im)
+
+
+def group_kernel(here_ref, local_ref, out_ref):
+    points = local_ref.shape[1] // 6
+    size = local_ref.shape[0]
+    here = here_ref[0]
+
+    def block(member):
+        index = jnp.bitwise_xor(member, jnp.bitwise_and(here, size - 1))
+        return tuple(local_ref[index, f * points:(f + 1) * points] for f in range(6))
+
+    def body(member, summary):
+        return join_coupled(summary, block(member))
+
+    summary = lax.fori_loop(1, size, body, block(0))
+    for index, value in enumerate(summary):
+        out_ref[index * points:(index + 1) * points] = value
+
+
+def final_kernel(here_ref, length_ref, energy_ref, code_ref, local_ref, group_ref, table_ref,
+                 low_ref, high_ref, left_re_ref, left_im_ref, dens_ref, bond_ref, *,
+                 slots, points, devices, mixed, scale):
+    size = local_ref.shape[0]
+    groups = group_ref.shape[0]
     here = here_ref[0]
     count = length_ref[here]
     rows = table_ref.shape[1]
-
-    def field(device, index):
-        block = jnp.bitwise_xor(device, here) if mixed else device
-        return every_ref[block, index * points:(index + 1) * points]
-
-    def into_body(device, run):
-        run_re, run_im = run
-        m_re, m_im = complex_mul(run_re, run_im, field(device, 0), field(device, 1))
-        inv_re, inv_im = reciprocal(1.0 - m_re, -m_im)
-        t_re, t_im = complex_mul(field(device, 4), field(device, 5), run_re, run_im)
-        t_re, t_im = complex_mul(t_re, t_im, inv_re, inv_im)
-        return (field(device, 2) + t_re, field(device, 3) + t_im)
-
-    def from_body(step, run):
-        run_re, run_im = run
-        device = devices - 1 - step
-        m_re, m_im = complex_mul(field(device, 2), field(device, 3), run_re, run_im)
-        inv_re, inv_im = reciprocal(1.0 - m_re, -m_im)
-        h_re, h_im = complex_mul(field(device, 4), field(device, 5), run_re, run_im)
-        h_re, h_im = complex_mul(h_re, h_im, inv_re, inv_im)
-        return (field(device, 0) + h_re, field(device, 1) + h_im)
+    member_here = here % size
+    group_here = here // size
+
+    def field(ref, index_of, position, index):
+        return ref[index_of(position), index * points:(index + 1) * points]
+
+    def local_index(member):
+        return jnp.bitwise_xor(member, member_here) if mixed else member
+
+    def group_index(group):
+        return jnp.bitwise_xor(group, group_here) if mixed else group
+
+    def into_step(ref, index_of):
+        def body(position, run):
+            run_re, run_im = run
+            m_re, m_im = complex_mul(run_re, run_im, field(ref, index_of, position, 0), field(ref, index_of, position, 1))
+            inv_re, inv_im = reciprocal(1.0 - m_re, -m_im)
+            t_re, t_im = complex_mul(field(ref, index_of, position, 4), field(ref, index_of, position, 5), run_re, run_im)
+            t_re, t_im = complex_mul(t_re, t_im, inv_re, inv_im)
+            return (field(ref, index_of, position, 2) + t_re, field(ref, index_of, position, 3) + t_im)
+        return body
+
+    def from_step(ref, index_of, last):
+        def body(step, run):
+            run_re, run_im = run
+            position = last - step
+            m_re, m_im = complex_mul(field(ref, index_of, position, 2), field(ref, index_of, position, 3), run_re, run_im)
+            inv_re, inv_im = reciprocal(1.0 - m_re, -m_im)
+            h_re, h_im = complex_mul(field(ref, index_of, position, 4), field(ref, index_of, position, 5), run_re, run_im)
+            h_re, h_im = complex_mul(h_re, h_im, inv_re, inv_im)
+            return (field(ref, index_of, position, 0) + h_re, field(ref, index_of, position, 1) + h_im)
+        return body
 
     zero = jnp.zeros((points,) + table_ref.shape[1:], jnp.float32)
-    into_re, into_im = lax.fori_loop(0, here, into_body, (zero, zero))
-    from_re, from_im = lax.fori_loop(0, devices - 1 - here, from_body, (zero, zero))
+    into = lax.fori_loop(0, group_here, into_step(group_ref, group_index), (zero, zero))
+    into_re, into_im = lax.fori_loop(0, member_here, into_step(local_ref, local_index), into)
+    outof = lax.fori_loop(0, groups - 1 - group_here, from_step(group_ref, group_index, groups - 1), (zero, zero))
+    from_re, from_im = lax.fori_loop(
+        0, size - 1 - member_here, from_step(local_ref, local_index, size - 1), outof
+    )
 
     def onsite(slot):
         return onsite_terms(table_ref, energy_ref, here, count, devices, slots, points, slot)
@@ -203,27 +250,37 @@
         in_specs=[smem, smem, smem, vmem],
         out_specs=vmem,
     )(here_arr, lengths, energy_index, table)
-    mixed = devices & (devices - 1) == 0
+    mixed = devices & (devices - 1) == 0 and devices >= 4
     if mixed:
-        every = packed
-        distance = devices // 2
-        level = 0
-        while distance >= 1:
+        size = 4
+        local = packed[None]
+        for distance in (1, 2):
             pairs = [(device, device ^ distance) for device in range(devices)]
-            every = jnp.stack([every, lax.ppermute(every, "slab", pairs)], axis=level)
-            distance //= 2
-            level += 1
-        every = every.reshape((devices,) + packed.shape)
+            local = jnp.concatenate([local, lax.ppermute(local, "slab", pairs)], axis=0)
+        summary = pl.pallas_call(
+            group_kernel,
+            out_shape=jax.ShapeDtypeStruct(packed.shape, jnp.float32),
+            in_specs=[smem, vmem],
+            out_specs=vmem,
+        )(here_arr, local)
+        every = summary[None]
+        distance = size
+        while distance < devices:
+            pairs = [(device, device ^ distance) for device in range(devices)]
+            every = jnp.concatenate([every, lax.ppermute(every, "slab", pairs)], axis=0)
+            distance *= 2
     else:
-        every = lax.all_gather(packed, "slab")
+        size = devices
+        local = lax.all_gather(packed, "slab")
+        every = jnp.zeros((1,) + packed.shape, jnp.float32)
     half = jax.ShapeDtypeStruct((2, slots, modes // 2), jnp.float32)
     low, high = pl.pallas_call(
         functools.partial(
-            final_kernel, slots=slots, points=points, mixed=mixed,
+            final_kernel, slots=slots, points=points, devices=devices, mixed=mixed,
             scale=1.0 / (32.0 * points * groups),
         ),
         out_shape=(half, half),
-        in_specs=[smem, smem, smem, smem, vmem, vmem],
+        in_specs=[smem, smem, smem, smem, vmem, vmem, vmem],
         out_specs=(vmem, vmem),
         scratch_shapes=[
             pltpu.VMEM((slots, points, rows, 128), jnp.float32),
@@ -231,7 +288,7 @@
             pltpu.VMEM((slots, rows, 128), jnp.float32),
             pltpu.VMEM((slots, rows, 128), jnp.float32),
         ],
-    )(here_arr, lengths, energy_index, weight_code, every, table)
+    )(here_arr, lengths, energy_index, weight_code, local, every, table)
     if groups == 2:
         lower = lax.axis_index("energy") == 0
         mine = jnp.where(lower, low, high)

time: 48.5 us -> 45.4 us (0.936)
  waiting for transfers between devices: 26.7 us -> 19.7 us
  starting transfers between devices: 7.28 us -> 9.96 us
  Pallas kernels: 4.54 us -> 6.21 us
  local copies, waits for them, and re-layouts: 5.02 us -> 3.68 us
  other arithmetic: 3.83 us -> 4.32 us
    ppermute x4, waiting for transfers between devices: 23.2 us -> 17 us  [the longest x2 10.6 us: shards(): every = jnp.concatenate([every, lax.ppermute(every, 'slab', pairs)], axis=0)]
    concatenate x0 -> x4, other arithmetic: none -> 3.38 us  [the longest x2 1.69 us: shards(): every = jnp.concatenate([every, lax.ppermute(every, 'slab', pairs)], axis=0)]
    ppermute x4, starting transfers between devices: 5.81 us -> 8.38 us  [the longest x2 5.2 us: shards(): every = jnp.concatenate([every, lax.ppermute(every, 'slab', pairs)], axis=0)]
    pallas_call x0 -> x1, Pallas kernels: none -> 1.75 us  [shards(): pl.pallas_call(group_kernel, out_shape=jax.ShapeDtypeStruct(packed.shape,...]
    another operation x4 -> x0, other arithmetic: 1.27 us -> none  [shards(): every = jnp.stack([every, lax.ppermute(every, 'slab', pairs)], axis=level)]
    another operation x1 -> x0, local copies, waits for them, and re-layouts: 1.26 us -> none  [shards(): every = jnp.stack([every, lax.ppermute(every, 'slab', pairs)], axis=level)]
    add x1, other arithmetic: 0.86 us -> 0.01 us  [shards(): both = mine + lax.ppermute(theirs, 'energy', [(0, 1), (1, 0)])]
    unnamed x1, other arithmetic: 0.85 us -> 0.01 us
where the time goes in v8:
time: 45.4 us; the launch traced here: 44.7 us
  waiting for transfers between devices  19.7 us (43%)
  starting transfers between devices  9.96 us (22%)
  Pallas kernels  6.21 us (14%)
  other arithmetic  4.32 us (10%)
  local copies, waits for them, and re-layouts  3.68 us (8%)
  between operations  0.77 us (2%)
    ppermute x2, waiting for transfers between devices, shards(): every = jnp.concatenate([every, lax.ppermute(every, 'slab', pairs)], axis=0)  10.6 us
    ppermute x2, waiting for transfers between devices, shards(): local = jnp.concatenate([local, lax.ppermute(local, 'slab', pairs)], axis=0)  6.37 us
    ppermute x2, starting transfers between devices, shards(): every = jnp.concatenate([every, lax.ppermute(every, 'slab', pairs)], axis=0)  5.2 us
    ppermute x2, starting transfers between devices, shards(): local = jnp.concatenate([local, lax.ppermute(local, 'slab', pairs)], axis=0)  3.18 us
    ppermute x1, waiting for transfers between devices, shards(): both = mine + lax.ppermute(theirs, 'energy', [(0, 1), (1, 0)])  2.75 us
    pallas_call x1, Pallas kernels, shards(): pl.pallas_call(functools.partial(final_kernel, slots=slots, points=points...  2.48 us
    unnamed x23, local copies, waits for them, and re-layouts  2.19 us
    pallas_call x1, Pallas kernels, shards(): pl.pallas_call(functools.partial(summary_kernel, slots=slots, points=poin...  1.98 us
  transfers between devices with their start and end apart: 5, of which 5 were waited for; matrix products, arithmetic and copies ran while one was open for 0% of the time, Pallas kernels for 0%

profile of v8, /device:TPU:0, one launch (start us, length us, event | category | flops | bytes accessed | tf_op | source)
XLA Modules:
  0.0 44.7 jit_solution(1017953024718003076)
XLA Ops:
  0.6 0.0 copy-start.7
  0.6 0.0 copy-start.5
  0.7 0.8 %concatenate.28 = f32[8,8,128]{2,1,0:T(8,128)S(1)} reshape(f32[4,2,1024]{2,1,0:T(2,128)} %param.14) | data formatting | bytes 65536 | tf_op jit(solution)/shard_map/concatenate | solution.py:234
  1.5 0.0 copy-done.7
  1.5 0.0 copy-start.8
  1.5 0.0 copy-done.5
  1.5 0.6 %copy-done.8 = f32[1024]{0:T(1024)S(1)} copy-done((f32[1024]{0:T(1024)S(1)}, f32[1024]{0:T(1024)}, u32[]{:S(2)}) %copy-start.8) | copy-done | bytes 4120
  2.2 0.8 %copy-done.6 = f32[16,1024]{1,0:T(8,128)S(1)} copy-done((f32[16,1024]{1,0:T(8,128)S(1)}, f32[16,1024]{1,0:T(8,128)}, u32[]{:S(2)}) %copy-start.6) | copy-done | bytes 65560
  3.1 0.0 copy-start
  3.1 0.7 %copy-done = f32[48,8,128]{2,1,0:T(8,128)} copy-done((f32[48,8,128]{2,1,0:T(8,128)}, f32[48,8,128]{2,1,0:T(8,128)S(1)}, u32[]{:S(2)}) %copy-start) | copy-done | bytes 196632
  3.8 2.0 %shard_map.95 = f32[24,8,128]{2,1,0:T(8,128)} custom-call(s32[1]{0:T(128)} %bitcast.here_ref, s32[16]{0:T(128)} %length_ref.3, s32[4]{0:T(128)} %energy_ref.3, f32[48,8,128]{2,1,0:T(8,128)} %copy-done), custom_call_target="tpu_custom_call" | custom-call | tf_op jit(solution)/shard_map/pallas_call | solution.py:247
  5.8 0.8 %collective-permute-start = (f32[1,24,8,128]{3,2,1,0:T(8,128)}, f32[1,24,8,128]{3,2,1,0:T(8,128)S(1)}, u32[]{:S(2)}, u32[]{:S(2)}) collective-permute-start(f32[1,24,8,128]{3,2,1,0:T(8,128)} %bitcast.15), channel_id=1, source_target_pairs={{0,2},{2,0},{4,6},{6,4},{8,10},{10,8},{12,14},{14,12},{16,18},{18,... | collective-permute-start | bytes 294920 | tf_op jit(solution)/shard_map/ppermute | solution.py:259
  6.5 1.2 %collective-permute-done = f32[1,24,8,128]{3,2,1,0:T(8,128)S(1)} collective-permute-done((f32[1,24,8,128]{3,2,1,0:T(8,128)}, f32[1,24,8,128]{3,2,1,0:T(8,128)S(1)}, u32[]{:S(2)}, u32[]{:S(2)}) %collective-permute-start) | collective-permute-done | bytes 98336 | tf_op jit(solution)/shard_map/ppermute | solution.py:259
  7.7 0.9 %pad_maximum_fusion.2 = f32[2,24,8,128]{3,2,1,0:T(8,128)S(1)} fusion(f32[1,24,8,128]{3,2,1,0:T(8,128)S(1)} %collective-permute-done, f32[1,24,8,128]{3,2,1,0:T(8,128)} %bitcast.16), kind=kLoop, calls=%fused_computation.2 | loop fusion | flops 49152 | bytes 393216 | tf_op jit(solution)/shard_map/concatenate | solution.py:259
  8.6 2.4 %collective-permute-start.1 = (f32[2,24,8,128]{3,2,1,0:T(8,128)S(1)}, f32[2,24,8,128]{3,2,1,0:T(8,128)S(1)}, u32[]{:S(2)}, u32[]{:S(2)}) collective-permute-start(f32[2,24,8,128]{3,2,1,0:T(8,128)S(1)} %pad_maximum_fusion.2), channel_id=1, source_target_pairs={{0,4},{2,6},{4,0},{6,2},{8,12},{10,14},{12,8},{14,10},{16,20},{18,... | collective-permute-start | bytes 589832 | tf_op jit(solution)/shard_map/ppermute | solution.py:259
  11.0 5.2 %collective-permute-done.1 = f32[2,24,8,128]{3,2,1,0:T(8,128)S(1)} collective-permute-done((f32[2,24,8,128]{3,2,1,0:T(8,128)S(1)}, f32[2,24,8,128]{3,2,1,0:T(8,128)S(1)}, u32[]{:S(2)}, u32[]{:S(2)}) %collective-permute-start.1) | collective-permute-done | bytes 196640 | tf_op jit(solution)/shard_map/ppermute | solution.py:259
  16.2 0.0 copy-done.2
  16.2 0.8 %pad_maximum_fusion.local_ref = f32[4,24,8,128]{3,2,1,0:T(8,128)} fusion(f32[2,24,8,128]{3,2,1,0:T(8,128)S(1)} %collective-permute-done.1, f32[1,24,8,128]{3,2,1,0:T(8,128)S(1)} %collective-permute-done, f32[1,24,8,128]{3,2,1,0:T(8,128)S(1)} %bitcast.17), kind=kLoop, calls=%fused_computation | loop fusion | flops 196608 | bytes 786432 | tf_op jit(solution)/shard_map/concatenate | solution.py:259
  17.0 1.8 %shard_map.96 = f32[24,8,128]{2,1,0:T(8,128)} custom-call(s32[1]{0:T(128)} %bitcast.here_ref, f32[4,24,8,128]{3,2,1,0:T(8,128)} %pad_maximum_fusion.local_ref), custom_call_target="tpu_custom_call" | custom-call | tf_op jit(solution)/shard_map/pallas_call | solution.py:260
  18.8 2.2 %collective-permute-start.2 = (f32[1,24,8,128]{3,2,1,0:T(8,128)}, f32[1,24,8,128]{3,2,1,0:T(8,128)S(1)}, u32[]{:S(2)}, u32[]{:S(2)}) collective-permute-start(f32[1,24,8,128]{3,2,1,0:T(8,128)} %bitcast.12), channel_id=1, source_target_pairs={{0,8},{2,10},{4,12},{6,14},{8,0},{10,2},{12,4},{14,6},{16,24},{18,... | collective-permute-start | bytes 294920 | tf_op jit(solution)/shard_map/ppermute | solution.py:270
  20.9 2.9 %collective-permute-done.2 = f32[1,24,8,128]{3,2,1,0:T(8,128)S(1)} collective-permute-done((f32[1,24,8,128]{3,2,1,0:T(8,128)}, f32[1,24,8,128]{3,2,1,0:T(8,128)S(1)}, u32[]{:S(2)}, u32[]{:S(2)}) %collective-permute-start.2) | collective-permute-done | bytes 98336 | tf_op jit(solution)/shard_map/ppermute | solution.py:270
  23.8 0.9 %pad_maximum_fusion.3 = f32[2,24,8,128]{3,2,1,0:T(8,128)S(1)} fusion(f32[1,24,8,128]{3,2,1,0:T(8,128)S(1)} %collective-permute-done.2, f32[1,24,8,128]{3,2,1,0:T(8,128)} %bitcast.13), kind=kLoop, calls=%fused_computation.3 | loop fusion | flops 49152 | bytes 393216 | tf_op jit(solution)/shard_map/concatenate | solution.py:270
  24.7 3.0 %collective-permute-start.3 = (f32[2,24,8,128]{3,2,1,0:T(8,128)S(1)}, f32[2,24,8,128]{3,2,1,0:T(8,128)S(1)}, u32[]{:S(2)}, u32[]{:S(2)}) collective-permute-start(f32[2,24,8,128]{3,2,1,0:T(8,128)S(1)} %pad_maximum_fusion.3), channel_id=1, source_target_pairs={{0,16},{2,18},{4,20},{6,22},{8,24},{10,26},{12,28},{14,30},{16,0},... | collective-permute-start | bytes 589832 | tf_op jit(solution)/shard_map/ppermute | solution.py:270
  27.7 7.7 %collective-permute-done.3 = f32[2,24,8,128]{3,2,1,0:T(8,128)S(1)} collective-permute-done((f32[2,24,8,128]{3,2,1,0:T(8,128)S(1)}, f32[2,24,8,128]{3,2,1,0:T(8,128)S(1)}, u32[]{:S(2)}, u32[]{:S(2)}) %collective-permute-start.3) | collective-permute-done | bytes 196640 | tf_op jit(solution)/shard_map/ppermute | solution.py:270
  35.5 0.0 copy-done.1
  35.5 0.8 %pad_maximum_fusion.1.group_ref = f32[4,24,8,128]{3,2,1,0:T(8,128)} fusion(f32[2,24,8,128]{3,2,1,0:T(8,128)S(1)} %collective-permute-done.3, f32[1,24,8,128]{3,2,1,0:T(8,128)S(1)} %collective-permute-done.2, f32[1,24,8,128]{3,2,1,0:T(8,128)S(1)} %bitcast.14), kind=kLoop, calls=%fused_computation.1 | loop fusion | flops 196608 | bytes 786432 | tf_op jit(solution)/shard_map/concatenate | solution.py:270
  36.3 2.5 %shard_map.97 = (f32[2,16,512]{2,1,0:T(8,128)}, f32[2,16,512]{2,1,0:T(8,128)}) custom-call(s32[1]{0:T(128)} %bitcast.here_ref, s32[16]{0:T(128)} %length_ref.3, s32[4]{0:T(128)} %energy_ref.3, s32[4]{0:T(128)} %code_ref.1, f32[4,24,8,128]{3,2,1,0:T(8,128)} %pad_maximum_fusion.local_ref, f32[4,24,8,128]{3,2,1,0:T(8,128)} %pad_maximum_fusion.1.group_ref, ...), custom_call_target="tpu_custom_call" | custom-call | tf_op jit(solution)/shard_map/pallas_call | solution.py:277
  38.8 0.9 %broadcast_select_fusion = f32[2,16,512]{2,1,0:T(8,128)S(1)} fusion(f32[2,16,512]{2,1,0:T(8,128)} %get-tuple-element.5, f32[2,16,512]{2,1,0:T(8,128)} %get-tuple-element.4, pred[]{:T(512)S(6)} %eq.3), kind=kLoop, calls=%fused_computation.8 | loop fusion | flops 16384 | bytes 196609 | tf_op jit(solution)/shard_map/jit(_where)/select_n | solution.py:295
  39.7 1.6 %collective-permute-start.4 = (f32[2,16,512]{2,1,0:T(8,128)S(1)}, f32[2,16,512]{2,1,0:T(8,128)S(1)}, u32[]{:S(2)}, u32[]{:S(2)}) collective-permute-start(f32[2,16,512]{2,1,0:T(8,128)S(1)} %broadcast_select_fusion), channel_id=1, source_target_pairs={{0,1},{1,0},{2,3},{3,2},{4,5},{5,4},{6,7},{7,6},{8,9},{9,8},{10,11... | collective-permute-start | bytes 196616 | tf_op jit(solution)/shard_map/ppermute | solution.py:296
  41.3 2.7 %collective-permute-done.4 = f32[2,16,512]{2,1,0:T(8,128)S(1)} collective-permute-done((f32[2,16,512]{2,1,0:T(8,128)S(1)}, f32[2,16,512]{2,1,0:T(8,128)S(1)}, u32[]{:S(2)}, u32[]{:S(2)}) %collective-permute-start.4) | collective-permute-done | bytes 65568 | tf_op jit(solution)/shard_map/ppermute | solution.py:296
  44.0 0.0 copy-done.3
  44.0 0.6 %slice_bitcast_fusion = (f32[16,512]{1,0:T(8,128)}, f32[16,512]{1,0:T(8,128)}) fusion(f32[2,16,512]{2,1,0:T(8,128)S(1)} %select_add_fusion), kind=kLoop, calls=%fused_computation.6 | loop fusion | bytes 131072 | tf_op jit(solution)/shard_map/squeeze | solution.py:301
  (15 shorter events, 0.1 us)
Async XLA Ops:
  0.6 0.8 %copy-start.7 = (f32[4,2,1024]{2,1,0:T(2,128)S(1)}, f32[4,2,1024]{2,1,0:T(2,128)}, u32[]{:S(2)}) copy-start(f32[4,2,1024]{2,1,0:T(2,128)} %param.15) | copy-start | bytes 98308
  0.6 0.9 %copy-start.5 = (f32[16,1024]{1,0:T(8,128)S(1)}, f32[16,1024]{1,0:T(8,128)}, u32[]{:S(2)}) copy-start(f32[16,1024]{1,0:T(8,128)} %param.9) | copy-start | bytes 196612
  1.5 0.7 %copy-start.8 = (f32[1024]{0:T(1024)S(1)}, f32[1024]{0:T(1024)}, u32[]{:S(2)}) copy-start(f32[1024]{0:T(1024)} %param.8) | copy-start | bytes 12292
  2.2 0.8 %copy-start.6 = (f32[16,1024]{1,0:T(8,128)S(1)}, f32[16,1024]{1,0:T(8,128)}, u32[]{:S(2)}) copy-start(f32[16,1024]{1,0:T(8,128)} %param.10) | copy-start | bytes 196612
  3.1 0.7 %copy-start = (f32[48,8,128]{2,1,0:T(8,128)}, f32[48,8,128]{2,1,0:T(8,128)S(1)}, u32[]{:S(2)}) copy-start(f32[48,8,128]{2,1,0:T(8,128)S(1)} %constant_dynamic-update-slice_fusion.table_ref) | copy-start | bytes 589828
  5.8 10.5 %copy-start.2 = (f32[24,8,128]{2,1,0:T(8,128)S(1)}, f32[24,8,128]{2,1,0:T(8,128)}, u32[]{:S(2)}) copy-start(f32[24,8,128]{2,1,0:T(8,128)} %shard_map.95) | copy-start | bytes 294916
  5.8 1.9 %collective-permute-start = (f32[1,24,8,128]{3,2,1,0:T(8,128)}, f32[1,24,8,128]{3,2,1,0:T(8,128)S(1)}, u32[]{:S(2)}, u32[]{:S(2)}) collective-permute-start(f32[1,24,8,128]{3,2,1,0:T(8,128)} %bitcast.15), channel_id=1, source_target_pairs={{0,2},{2,0},{4,6},{6,4},{8,10},{10,8},{12,14},{14,12},{16,18},{18,... | collective-permute-start | bytes 294920 | tf_op jit(solution)/shard_map/ppermute | solution.py:259
  8.6 7.6 %collective-permute-start.1 = (f32[2,24,8,128]{3,2,1,0:T(8,128)S(1)}, f32[2,24,8,128]{3,2,1,0:T(8,128)S(1)}, u32[]{:S(2)}, u32[]{:S(2)}) collective-permute-start(f32[2,24,8,128]{3,2,1,0:T(8,128)S(1)} %pad_maximum_fusion.2), channel_id=1, source_target_pairs={{0,4},{2,6},{4,0},{6,2},{8,12},{10,14},{12,8},{14,10},{16,20},{18,... | collective-permute-start | bytes 589832 | tf_op jit(solution)/shard_map/ppermute | solution.py:259
  18.8 16.7 %copy-start.1 = (f32[24,8,128]{2,1,0:T(8,128)S(1)}, f32[24,8,128]{2,1,0:T(8,128)}, u32[]{:S(2)}) copy-start(f32[24,8,128]{2,1,0:T(8,128)} %shard_map.96) | copy-start | bytes 294916
  18.8 5.0 %collective-permute-start.2 = (f32[1,24,8,128]{3,2,1,0:T(8,128)}, f32[1,24,8,128]{3,2,1,0:T(8,128)S(1)}, u32[]{:S(2)}, u32[]{:S(2)}) collective-permute-start(f32[1,24,8,128]{3,2,1,0:T(8,128)} %bitcast.12), channel_id=1, source_target_pairs={{0,8},{2,10},{4,12},{6,14},{8,0},{10,2},{12,4},{14,6},{16,24},{18,... | collective-permute-start | bytes 294920 | tf_op jit(solution)/shard_map/ppermute | solution.py:270
  24.7 10.8 %collective-permute-start.3 = (f32[2,24,8,128]{3,2,1,0:T(8,128)S(1)}, f32[2,24,8,128]{3,2,1,0:T(8,128)S(1)}, u32[]{:S(2)}, u32[]{:S(2)}) collective-permute-start(f32[2,24,8,128]{3,2,1,0:T(8,128)S(1)} %pad_maximum_fusion.3), channel_id=1, source_target_pairs={{0,16},{2,18},{4,20},{6,22},{8,24},{10,26},{12,28},{14,30},{16,0},... | collective-permute-start | bytes 589832 | tf_op jit(solution)/shard_map/ppermute | solution.py:270
  38.7 5.3 %copy-start.3 = (f32[2,16,512]{2,1,0:T(8,128)S(1)}, f32[2,16,512]{2,1,0:T(8,128)}, u32[]{:S(2)}) copy-start(f32[2,16,512]{2,1,0:T(8,128)} %get-tuple-element.4) | copy-start | bytes 196612
  38.8 5.3 %copy-start.4 = (f32[2,16,512]{2,1,0:T(8,128)S(1)}, f32[2,16,512]{2,1,0:T(8,128)}, u32[]{:S(2)}) copy-start(f32[2,16,512]{2,1,0:T(8,128)} %get-tuple-element.5) | copy-start | bytes 196612
  39.7 4.3 %collective-permute-start.4 = (f32[2,16,512]{2,1,0:T(8,128)S(1)}, f32[2,16,512]{2,1,0:T(8,128)S(1)}, u32[]{:S(2)}, u32[]{:S(2)}) collective-permute-start(f32[2,16,512]{2,1,0:T(8,128)S(1)} %broadcast_select_fusion), channel_id=1, source_target_pairs={{0,1},{1,0},{2,3},{3,2},{4,5},{5,4},{6,7},{7,6},{8,9},{9,8},{10,11... | collective-permute-start | bytes 196616 | tf_op jit(solution)/shard_map/ppermute | solution.py:296

commit v9 on v8

--- a/solution.py
+++ b/solution.py
@@ -253,22 +253,28 @@
     mixed = devices & (devices - 1) == 0 and devices >= 4
     if mixed:
         size = 4
-        local = packed[None]
-        for distance in (1, 2):
-            pairs = [(device, device ^ distance) for device in range(devices)]
-            local = jnp.concatenate([local, lax.ppermute(local, "slab", pairs)], axis=0)
+        local = jnp.stack([packed] + [
+            lax.ppermute(packed, "slab", [(device, device ^ offset) for device in range(devices)])
+            for offset in range(1, size)
+        ])
         summary = pl.pallas_call(
             group_kernel,
             out_shape=jax.ShapeDtypeStruct(packed.shape, jnp.float32),
             in_specs=[smem, vmem],
             out_specs=vmem,
         )(here_arr, local)
-        every = summary[None]
-        distance = size
-        while distance < devices:
-            pairs = [(device, device ^ distance) for device in range(devices)]
-            every = jnp.concatenate([every, lax.ppermute(every, "slab", pairs)], axis=0)
-            distance *= 2
+        if devices == size * size:
+            every = jnp.stack([summary] + [
+                lax.ppermute(summary, "slab", [(device, device ^ (offset * size)) for device in range(devices)])
+                for offset in range(1, size)
+            ])
+        else:
+            every = summary[None]
+            distance = size
+            while distance < devices:
+                pairs = [(device, device ^ distance) for device in range(devices)]
+                every = jnp.concatenate([every, lax.ppermute(every, "slab", pairs)], axis=0)
+                distance *= 2
     else:
         size = devices
         local = lax.all_gather(packed, "slab")

time: 45.4 us -> 40.7 us (0.90)
  waiting for transfers between devices: 19.7 us -> 15.1 us
  starting transfers between devices: 9.96 us -> 10.6 us
  Pallas kernels: 6.21 us -> 5.71 us
    ppermute x4 -> x6, waiting for transfers between devices: 17 us -> 12.3 us  [the longest x3 7.57 us: shards(): lax.ppermute(summary, 'slab', [(device, device ^ offset * size) for devic...]
    concatenate x4 -> x0, other arithmetic: 3.38 us -> none  [the longest x2 1.69 us: shards(): every = jnp.concatenate([every, lax.ppermute(every, 'slab', pairs)], axis=0)]
    another operation x0 -> x2, other arithmetic: none -> 3.35 us  [the longest x1 1.68 us: shards(): jnp.stack([summary] + [lax.ppermute(summary, 'slab', [(device, device ^ o...]
    ppermute x4 -> x6, starting transfers between devices: 8.38 us -> 8.99 us  [the longest x3 5.7 us: shards(): lax.ppermute(summary, 'slab', [(device, device ^ offset * size) for devic...]
    unnamed x23 -> x19, local copies, waits for them, and re-layouts: 2.19 us -> 2.19 us
  transfers between devices with their start and end apart: 5 -> 7, of which waited for: 5 -> 5; matrix products, arithmetic and copies ran while one was open for 0% -> 0% of each run, Pallas kernels for 0% -> 0%
where the time goes in v9:
time: 40.7 us; the launch traced here: 40.1 us
  waiting for transfers between devices  15.1 us (37%)
  starting transfers between devices  10.6 us (26%)
  Pallas kernels  5.71 us (14%)
  other arithmetic  4.3 us (11%)
  local copies, waits for them, and re-layouts  3.67 us (9%)
  between operations  0.76 us (2%)
    ppermute x3, waiting for transfers between devices, shards(): lax.ppermute(summary, 'slab', [(device, device ^ offset * size) for devic...  7.57 us
    ppermute x3, starting transfers between devices, shards(): lax.ppermute(summary, 'slab', [(device, device ^ offset * size) for devic...  5.7 us
    ppermute x3, waiting for transfers between devices, shards(): lax.ppermute(packed, 'slab', [(device, device ^ offset) for device in ran...  4.76 us
    ppermute x3, starting transfers between devices, shards(): lax.ppermute(packed, 'slab', [(device, device ^ offset) for device in ran...  3.3 us
    ppermute x1, waiting for transfers between devices, shards(): both = mine + lax.ppermute(theirs, 'energy', [(0, 1), (1, 0)])  2.75 us
    pallas_call x1, Pallas kernels, shards(): pl.pallas_call(functools.partial(final_kernel, slots=slots, points=points...  2.23 us
    unnamed x19, local copies, waits for them, and re-layouts  2.19 us
    pallas_call x1, Pallas kernels, shards(): pl.pallas_call(group_kernel, out_shape=jax.ShapeDtypeStruct(packed.shape,...  1.75 us
  transfers between devices with their start and end apart: 7, of which 5 were waited for; matrix products, arithmetic and copies ran while one was open for 0% of the time, Pallas kernels for 0%

profile of v9, /device:TPU:0, one launch (start us, length us, event | category | flops | bytes accessed | tf_op | source)
XLA Modules:
  0.0 40.1 jit_solution(2567233185178330883)
XLA Ops:
  0.6 0.0 copy-start.5
  0.6 0.0 copy-start.3
  0.7 0.8 %concatenate.14 = f32[8,8,128]{2,1,0:T(8,128)S(1)} reshape(f32[4,2,1024]{2,1,0:T(2,128)} %param.14) | data formatting | bytes 65536 | tf_op jit(solution)/shard_map/concatenate | solution.py:234
  1.5 0.0 copy-done.5
  1.5 0.0 copy-start.6
  1.5 0.0 copy-done.3
  1.5 0.6 %copy-done.6 = f32[1024]{0:T(1024)S(1)} copy-done((f32[1024]{0:T(1024)S(1)}, f32[1024]{0:T(1024)}, u32[]{:S(2)}) %copy-start.6) | copy-done | bytes 4120
  2.2 0.8 %copy-done.4 = f32[16,1024]{1,0:T(8,128)S(1)} copy-done((f32[16,1024]{1,0:T(8,128)S(1)}, f32[16,1024]{1,0:T(8,128)}, u32[]{:S(2)}) %copy-start.4) | copy-done | bytes 65560
  3.1 0.0 copy-start
  3.1 0.7 %copy-done = f32[48,8,128]{2,1,0:T(8,128)} copy-done((f32[48,8,128]{2,1,0:T(8,128)}, f32[48,8,128]{2,1,0:T(8,128)S(1)}, u32[]{:S(2)}) %copy-start) | copy-done | bytes 196632
  3.8 1.7 %shard_map.95 = f32[24,8,128]{2,1,0:T(8,128)} custom-call(s32[1]{0:T(128)} %bitcast.here_ref, s32[16]{0:T(128)} %length_ref.3, s32[4]{0:T(128)} %energy_ref.3, f32[48,8,128]{2,1,0:T(8,128)} %copy-done), custom_call_target="tpu_custom_call" | custom-call | tf_op jit(solution)/shard_map/pallas_call | solution.py:247
  5.5 2.3 %collective-permute-start.2 = (f32[24,8,128]{2,1,0:T(8,128)}, f32[24,8,128]{2,1,0:T(8,128)S(1)}, u32[]{:S(2)}, u32[]{:S(2)}) collective-permute-start(f32[24,8,128]{2,1,0:T(8,128)} %shard_map.95), channel_id=1, source_target_pairs={{0,6},{2,4},{4,2},{6,0},{8,14},{10,12},{12,10},{14,8},{16,22},{18,... | collective-permute-start | bytes 294920 | tf_op jit(solution)/shard_map/ppermute | solution.py:257
  7.8 1.0 %collective-permute-start.1 = (f32[24,8,128]{2,1,0:T(8,128)}, f32[24,8,128]{2,1,0:T(8,128)S(1)}, u32[]{:S(2)}, u32[]{:S(2)}) collective-permute-start(f32[24,8,128]{2,1,0:T(8,128)} %shard_map.95), channel_id=1, source_target_pairs={{0,4},{2,6},{4,0},{6,2},{8,12},{10,14},{12,8},{14,10},{16,20},{18,... | collective-permute-start | bytes 294920 | tf_op jit(solution)/shard_map/ppermute | solution.py:257
  8.7 0.1 collective-permute-start
  8.8 2.2 %collective-permute-done.2 = f32[24,8,128]{2,1,0:T(8,128)S(1)} collective-permute-done((f32[24,8,128]{2,1,0:T(8,128)}, f32[24,8,128]{2,1,0:T(8,128)S(1)}, u32[]{:S(2)}, u32[]{:S(2)}) %collective-permute-start.2) | collective-permute-done | bytes 98336 | tf_op jit(solution)/shard_map/ppermute | solution.py:257
  11.0 2.6 %collective-permute-done.1 = f32[24,8,128]{2,1,0:T(8,128)S(1)} collective-permute-done((f32[24,8,128]{2,1,0:T(8,128)}, f32[24,8,128]{2,1,0:T(8,128)S(1)}, u32[]{:S(2)}, u32[]{:S(2)}) %collective-permute-start.1) | collective-permute-done | bytes 98336 | tf_op jit(solution)/shard_map/ppermute | solution.py:257
  13.6 0.0 collective-permute-done
  13.6 1.7 %pad_maximum_fusion.local_ref = f32[4,24,8,128]{3,2,1,0:T(8,128)} fusion(f32[1,24,8,128]{3,2,1,0:T(8,128)S(1)} %bitcast.25, f32[1,24,8,128]{3,2,1,0:T(8,128)S(1)} %bitcast.26, f32[1,24,8,128]{3,2,1,0:T(8,128)S(1)} %bitcast.27, f32[1,24,8,128]{3,2,1,0:T(8,128)} %bitcast.19), kind=kLoop, calls=%fused_computation | loop fusion | flops 294912 | bytes 786432 | tf_op jit(solution)/shard_map/stack | solution.py:256
  15.2 1.8 %shard_map.96 = f32[24,8,128]{2,1,0:T(8,128)} custom-call(s32[1]{0:T(128)} %bitcast.here_ref, f32[4,24,8,128]{3,2,1,0:T(8,128)} %pad_maximum_fusion.local_ref), custom_call_target="tpu_custom_call" | custom-call | tf_op jit(solution)/shard_map/pallas_call | solution.py:260
  17.0 5.1 %collective-permute-start.5 = (f32[24,8,128]{2,1,0:T(8,128)}, f32[24,8,128]{2,1,0:T(8,128)S(1)}, u32[]{:S(2)}, u32[]{:S(2)}) collective-permute-start(f32[24,8,128]{2,1,0:T(8,128)} %shard_map.96), channel_id=1, source_target_pairs={{0,24},{2,26},{4,28},{6,30},{8,16},{10,18},{12,20},{14,22},{16,8},... | collective-permute-start | bytes 294920 | tf_op jit(solution)/shard_map/ppermute | solution.py:268
  22.1 0.0 collective-permute-start.4
  22.1 0.6 %collective-permute-start.3 = (f32[24,8,128]{2,1,0:T(8,128)}, f32[24,8,128]{2,1,0:T(8,128)S(1)}, u32[]{:S(2)}, u32[]{:S(2)}) collective-permute-start(f32[24,8,128]{2,1,0:T(8,128)} %shard_map.96), channel_id=1, source_target_pairs={{0,8},{2,10},{4,12},{6,14},{8,0},{10,2},{12,4},{14,6},{16,24},{18,... | collective-permute-start | bytes 294920 | tf_op jit(solution)/shard_map/ppermute | solution.py:268
  22.7 3.3 %collective-permute-done.5 = f32[24,8,128]{2,1,0:T(8,128)S(1)} collective-permute-done((f32[24,8,128]{2,1,0:T(8,128)}, f32[24,8,128]{2,1,0:T(8,128)S(1)}, u32[]{:S(2)}, u32[]{:S(2)}) %collective-permute-start.5) | collective-permute-done | bytes 98336 | tf_op jit(solution)/shard_map/ppermute | solution.py:268
  26.0 4.2 %collective-permute-done.4 = f32[24,8,128]{2,1,0:T(8,128)S(1)} collective-permute-done((f32[24,8,128]{2,1,0:T(8,128)}, f32[24,8,128]{2,1,0:T(8,128)S(1)}, u32[]{:S(2)}, u32[]{:S(2)}) %collective-permute-start.4) | collective-permute-done | bytes 98336 | tf_op jit(solution)/shard_map/ppermute | solution.py:268
  30.3 0.0 collective-permute-done.3
  30.3 1.7 %pad_maximum_fusion.1.group_ref = f32[4,24,8,128]{3,2,1,0:T(8,128)} fusion(f32[1,24,8,128]{3,2,1,0:T(8,128)S(1)} %bitcast.22, f32[1,24,8,128]{3,2,1,0:T(8,128)S(1)} %bitcast.23, f32[1,24,8,128]{3,2,1,0:T(8,128)S(1)} %bitcast.24, f32[1,24,8,128]{3,2,1,0:T(8,128)} %bitcast.18), kind=kLoop, calls=%fused_computation.1 | loop fusion | flops 294912 | bytes 786432 | tf_op jit(solution)/shard_map/stack | solution.py:267
  31.9 2.2 %shard_map.97 = (f32[2,16,512]{2,1,0:T(8,128)}, f32[2,16,512]{2,1,0:T(8,128)}) custom-call(s32[1]{0:T(128)} %bitcast.here_ref, s32[16]{0:T(128)} %length_ref.3, s32[4]{0:T(128)} %energy_ref.3, s32[4]{0:T(128)} %code_ref.1, f32[4,24,8,128]{3,2,1,0:T(8,128)} %pad_maximum_fusion.local_ref, f32[4,24,8,128]{3,2,1,0:T(8,128)} %pad_maximum_fusion.1.group_ref, ...), custom_call_target="tpu_custom_call" | custom-call | tf_op jit(solution)/shard_map/pallas_call | solution.py:283
  34.2 0.9 %broadcast_select_fusion = f32[2,16,512]{2,1,0:T(8,128)S(1)} fusion(f32[2,16,512]{2,1,0:T(8,128)} %get-tuple-element.5, f32[2,16,512]{2,1,0:T(8,128)} %get-tuple-element.4, pred[]{:T(512)S(6)} %eq.3), kind=kLoop, calls=%fused_computation.6 | loop fusion | flops 16384 | bytes 196609 | tf_op jit(solution)/shard_map/jit(_where)/select_n | solution.py:301
  35.1 1.6 %collective-permute-start.6 = (f32[2,16,512]{2,1,0:T(8,128)S(1)}, f32[2,16,512]{2,1,0:T(8,128)S(1)}, u32[]{:S(2)}, u32[]{:S(2)}) collective-permute-start(f32[2,16,512]{2,1,0:T(8,128)S(1)} %broadcast_select_fusion), channel_id=1, source_target_pairs={{0,1},{1,0},{2,3},{3,2},{4,5},{5,4},{6,7},{7,6},{8,9},{9,8},{10,11... | collective-permute-start | bytes 196616 | tf_op jit(solution)/shard_map/ppermute | solution.py:302
  36.7 2.7 %collective-permute-done.6 = f32[2,16,512]{2,1,0:T(8,128)S(1)} collective-permute-done((f32[2,16,512]{2,1,0:T(8,128)S(1)}, f32[2,16,512]{2,1,0:T(8,128)S(1)}, u32[]{:S(2)}, u32[]{:S(2)}) %collective-permute-start.6) | collective-permute-done | bytes 65568 | tf_op jit(solution)/shard_map/ppermute | solution.py:302
  39.4 0.0 copy-done.2
  39.5 0.6 %slice_bitcast_fusion = (f32[16,512]{1,0:T(8,128)}, f32[16,512]{1,0:T(8,128)}) fusion(f32[2,16,512]{2,1,0:T(8,128)S(1)} %select_add_fusion), kind=kLoop, calls=%fused_computation.4 | loop fusion | bytes 131072 | tf_op jit(solution)/shard_map/squeeze | solution.py:307
  (13 shorter events, 0.1 us)
Async XLA Ops:
  0.6 0.8 %copy-start.5 = (f32[4,2,1024]{2,1,0:T(2,128)S(1)}, f32[4,2,1024]{2,1,0:T(2,128)}, u32[]{:S(2)}) copy-start(f32[4,2,1024]{2,1,0:T(2,128)} %param.15) | copy-start | bytes 98308
  0.6 0.9 %copy-start.3 = (f32[16,1024]{1,0:T(8,128)S(1)}, f32[16,1024]{1,0:T(8,128)}, u32[]{:S(2)}) copy-start(f32[16,1024]{1,0:T(8,128)} %param.9) | copy-start | bytes 196612
  1.5 0.7 %copy-start.6 = (f32[1024]{0:T(1024)S(1)}, f32[1024]{0:T(1024)}, u32[]{:S(2)}) copy-start(f32[1024]{0:T(1024)} %param.8) | copy-start | bytes 12292
  2.2 0.8 %copy-start.4 = (f32[16,1024]{1,0:T(8,128)S(1)}, f32[16,1024]{1,0:T(8,128)}, u32[]{:S(2)}) copy-start(f32[16,1024]{1,0:T(8,128)} %param.10) | copy-start | bytes 196612
  3.1 0.7 %copy-start = (f32[48,8,128]{2,1,0:T(8,128)}, f32[48,8,128]{2,1,0:T(8,128)S(1)}, u32[]{:S(2)}) copy-start(f32[48,8,128]{2,1,0:T(8,128)S(1)} %constant_dynamic-update-slice_fusion.table_ref) | copy-start | bytes 589828
  5.5 5.5 %collective-permute-start.2 = (f32[24,8,128]{2,1,0:T(8,128)}, f32[24,8,128]{2,1,0:T(8,128)S(1)}, u32[]{:S(2)}, u32[]{:S(2)}) collective-permute-start(f32[24,8,128]{2,1,0:T(8,128)} %shard_map.95), channel_id=1, source_target_pairs={{0,6},{2,4},{4,2},{6,0},{8,14},{10,12},{12,10},{14,8},{16,22},{18,... | collective-permute-start | bytes 294920 | tf_op jit(solution)/shard_map/ppermute | solution.py:257
  7.8 5.8 %collective-permute-start.1 = (f32[24,8,128]{2,1,0:T(8,128)}, f32[24,8,128]{2,1,0:T(8,128)S(1)}, u32[]{:S(2)}, u32[]{:S(2)}) collective-permute-start(f32[24,8,128]{2,1,0:T(8,128)} %shard_map.95), channel_id=1, source_target_pairs={{0,4},{2,6},{4,0},{6,2},{8,12},{10,14},{12,8},{14,10},{16,20},{18,... | collective-permute-start | bytes 294920 | tf_op jit(solution)/shard_map/ppermute | solution.py:257
  8.7 4.8 %collective-permute-start = (f32[24,8,128]{2,1,0:T(8,128)}, f32[24,8,128]{2,1,0:T(8,128)S(1)}, u32[]{:S(2)}, u32[]{:S(2)}) collective-permute-start(f32[24,8,128]{2,1,0:T(8,128)} %shard_map.95), channel_id=1, source_target_pairs={{0,2},{2,0},{4,6},{6,4},{8,10},{10,8},{12,14},{14,12},{16,18},{18,... | collective-permute-start | bytes 294920 | tf_op jit(solution)/shard_map/ppermute | solution.py:257
  17.0 9.0 %collective-permute-start.5 = (f32[24,8,128]{2,1,0:T(8,128)}, f32[24,8,128]{2,1,0:T(8,128)S(1)}, u32[]{:S(2)}, u32[]{:S(2)}) collective-permute-start(f32[24,8,128]{2,1,0:T(8,128)} %shard_map.96), channel_id=1, source_target_pairs={{0,24},{2,26},{4,28},{6,30},{8,16},{10,18},{12,20},{14,22},{16,8},... | collective-permute-start | bytes 294920 | tf_op jit(solution)/shard_map/ppermute | solution.py:268
  22.1 8.1 %collective-permute-start.4 = (f32[24,8,128]{2,1,0:T(8,128)}, f32[24,8,128]{2,1,0:T(8,128)S(1)}, u32[]{:S(2)}, u32[]{:S(2)}) collective-permute-start(f32[24,8,128]{2,1,0:T(8,128)} %shard_map.96), channel_id=1, source_target_pairs={{0,16},{2,18},{4,20},{6,22},{8,24},{10,26},{12,28},{14,30},{16,0},... | collective-permute-start | bytes 294920 | tf_op jit(solution)/shard_map/ppermute | solution.py:268
  22.1 8.1 %collective-permute-start.3 = (f32[24,8,128]{2,1,0:T(8,128)}, f32[24,8,128]{2,1,0:T(8,128)S(1)}, u32[]{:S(2)}, u32[]{:S(2)}) collective-permute-start(f32[24,8,128]{2,1,0:T(8,128)} %shard_map.96), channel_id=1, source_target_pairs={{0,8},{2,10},{4,12},{6,14},{8,0},{10,2},{12,4},{14,6},{16,24},{18,... | collective-permute-start | bytes 294920 | tf_op jit(solution)/shard_map/ppermute | solution.py:268
  34.2 5.3 %copy-start.1 = (f32[2,16,512]{2,1,0:T(8,128)S(1)}, f32[2,16,512]{2,1,0:T(8,128)}, u32[]{:S(2)}) copy-start(f32[2,16,512]{2,1,0:T(8,128)} %get-tuple-element.4) | copy-start | bytes 196612
  34.2 5.3 %copy-start.2 = (f32[2,16,512]{2,1,0:T(8,128)S(1)}, f32[2,16,512]{2,1,0:T(8,128)}, u32[]{:S(2)}) copy-start(f32[2,16,512]{2,1,0:T(8,128)} %get-tuple-element.5) | copy-start | bytes 196612
  35.1 4.3 %collective-permute-start.6 = (f32[2,16,512]{2,1,0:T(8,128)S(1)}, f32[2,16,512]{2,1,0:T(8,128)S(1)}, u32[]{:S(2)}, u32[]{:S(2)}) collective-permute-start(f32[2,16,512]{2,1,0:T(8,128)S(1)} %broadcast_select_fusion), channel_id=1, source_target_pairs={{0,1},{1,0},{2,3},{3,2},{4,5},{5,4},{6,7},{7,6},{8,9},{9,8},{10,11... | collective-permute-start | bytes 196616 | tf_op jit(solution)/shard_map/ppermute | solution.py:302

commit v10 on v9

--- a/solution.py
+++ b/solution.py
@@ -106,71 +106,82 @@
     return (left[0] + f_re, left[1] + f_im, right[2] + g_re, right[3] + g_im, x_re, x_im)
 
 
-def group_kernel(here_ref, local_ref, out_ref):
-    points = local_ref.shape[1] // 6
-    size = local_ref.shape[0]
+def in_order(refs, own, mixed):
+    loaded = [ref[...] for ref in refs]
+    if not mixed:
+        return loaded
+    ordered = []
+    for position in range(len(refs)):
+        offset = jnp.bitwise_xor(own, position)
+        value = loaded[0]
+        for index in range(1, len(refs)):
+            value = jnp.where(offset == index, loaded[index], value)
+        ordered.append(value)
+    return ordered
+
+
+def split_fields(value, points):
+    return tuple(value[f * points:(f + 1) * points] for f in range(6))
+
+
+def group_kernel(here_ref, *refs):
+    local_refs, out_ref = refs[:-1], refs[-1]
+    points = out_ref.shape[0] // 6
+    size = len(local_refs)
     here = here_ref[0]
-
-    def block(member):
-        index = jnp.bitwise_xor(member, jnp.bitwise_and(here, size - 1))
-        return tuple(local_ref[index, f * points:(f + 1) * points] for f in range(6))
-
-    def body(member, summary):
-        return join_coupled(summary, block(member))
-
-    summary = lax.fori_loop(1, size, body, block(0))
+    blocks = in_order(local_refs, jnp.bitwise_and(here, size - 1), True)
+    summary = split_fields(blocks[0], points)
+    for member in range(1, size):
+        summary = join_coupled(summary, split_fields(blocks[member], points))
     for index, value in enumerate(summary):
         out_ref[index * points:(index + 1) * points] = value
 
 
-def final_kernel(here_ref, length_ref, energy_ref, code_ref, local_ref, group_ref, table_ref,
-                 low_ref, high_ref, left_re_ref, left_im_ref, dens_ref, bond_ref, *,
-                 slots, points, devices, mixed, scale):
-    size = local_ref.shape[0]
-    groups = group_ref.shape[0]
+def final_kernel(here_ref, length_ref, energy_ref, code_ref, *refs,
+                 slots, points, devices, mixed, size, groups, scale):
+    local_refs = refs[:size]
+    group_refs = refs[size:size + groups]
+    table_ref, low_ref, high_ref, left_re_ref, left_im_ref, dens_ref, bond_ref = refs[size + groups:]
     here = here_ref[0]
     count = length_ref[here]
     rows = table_ref.shape[1]
     member_here = here % size
     group_here = here // size
 
-    def field(ref, index_of, position, index):
-        return ref[index_of(position), index * points:(index + 1) * points]
-
-    def local_index(member):
-        return jnp.bitwise_xor(member, member_here) if mixed else member
-
-    def group_index(group):
-        return jnp.bitwise_xor(group, group_here) if mixed else group
-
-    def into_step(ref, index_of):
-        def body(position, run):
-            run_re, run_im = run
-            m_re, m_im = complex_mul(run_re, run_im, field(ref, index_of, position, 0), field(ref, index_of, position, 1))
-            inv_re, inv_im = reciprocal(1.0 - m_re, -m_im)
-            t_re, t_im = complex_mul(field(ref, index_of, position, 4), field(ref, index_of, position, 5), run_re, run_im)
-            t_re, t_im = complex_mul(t_re, t_im, inv_re, inv_im)
-            return (field(ref, index_of, position, 2) + t_re, field(ref, index_of, position, 3) + t_im)
-        return body
-
-    def from_step(ref, index_of, last):
-        def body(step, run):
-            run_re, run_im = run
-            position = last - step
-            m_re, m_im = complex_mul(field(ref, index_of, position, 2), field(ref, index_of, position, 3), run_re, run_im)
-            inv_re, inv_im = reciprocal(1.0 - m_re, -m_im)
-            h_re, h_im = complex_mul(field(ref, index_of, position, 4), field(ref, index_of, position, 5), run_re, run_im)
-            h_re, h_im = complex_mul(h_re, h_im, inv_re, inv_im)
-            return (field(ref, index_of, position, 0) + h_re, field(ref, index_of, position, 1) + h_im)
-        return body
+    def into_step(block, run):
+        run_re, run_im = run
+        m_re, m_im = complex_mul(run_re, run_im, block[0], block[1])
+        inv_re, inv_im = reciprocal(1.0 - m_re, -m_im)
+        t_re, t_im = complex_mul(block[4], block[5], run_re, run_im)
+        t_re, t_im = complex_mul(t_re, t_im, inv_re, inv_im)
+        return (block[2] + t_re, block[3] + t_im)
+
+    def from_step(block, run):
+        run_re, run_im = run
+        m_re, m_im = complex_mul(block[2], block[3], run_re, run_im)
+        inv_re, inv_im = reciprocal(1.0 - m_re, -m_im)
+        h_re, h_im = complex_mul(block[4], block[5], run_re, run_im)
+        h_re, h_im = complex_mul(h_re, h_im, inv_re, inv_im)
+        return (block[0] + h_re, block[1] + h_im)
+
+    def masked(keep, new, old):
+        return tuple(jnp.where(keep, n, o) for n, o in zip(new, old))
 
     zero = jnp.zeros((points,) + table_ref.shape[1:], jnp.float32)
-    into = lax.fori_loop(0, group_here, into_step(group_ref, group_index), (zero, zero))
-    into_re, into_im = lax.fori_loop(0, member_here, into_step(local_ref, local_index), into)
-    outof = lax.fori_loop(0, groups - 1 - group_here, from_step(group_ref, group_index, groups - 1), (zero, zero))
-    from_re, from_im = lax.fori_loop(
-        0, size - 1 - member_here, from_step(local_ref, local_index, size - 1), outof
-    )
+    group_blocks = [split_fields(v, points) for v in in_order(group_refs, group_here, mixed)]
+    local_blocks = [split_fields(v, points) for v in in_order(local_refs, member_here, mixed)]
+    into = (zero, zero)
+    for group in range(groups):
+        into = masked(group < group_here, into_step(group_blocks[group], into), into)
+    for member in range(size):
+        into = masked(member < member_here, into_step(local_blocks[member], into), into)
+    outof = (zero, zero)
+    for group in reversed(range(groups)):
+        outof = masked(group > group_here, from_step(group_blocks[group], outof), outof)
+    for member in reversed(range(size)):
+        outof = masked(member > member_here, from_step(local_blocks[member], outof), outof)
+    into_re, into_im = into
+    from_re, from_im = outof
 
     def onsite(slot):
         return onsite_terms(table_ref, energy_ref, here, count, devices, slots, points, slot)
@@ -253,40 +264,42 @@
     mixed = devices & (devices - 1) == 0 and devices >= 4
     if mixed:
         size = 4
-        local = jnp.stack([packed] + [
+        local = [packed] + [
             lax.ppermute(packed, "slab", [(device, device ^ offset) for device in range(devices)])
             for offset in range(1, size)
-        ])
+        ]
         summary = pl.pallas_call(
             group_kernel,
             out_shape=jax.ShapeDtypeStruct(packed.shape, jnp.float32),
-            in_specs=[smem, vmem],
+            in_specs=[smem] + [vmem] * size,
             out_specs=vmem,
-        )(here_arr, local)
+        )(here_arr, *local)
         if devices == size * size:
-            every = jnp.stack([summary] + [
+            every = [summary] + [
                 lax.ppermute(summary, "slab", [(device, device ^ (offset * size)) for device in range(devices)])
                 for offset in range(1, size)
-            ])
+            ]
         else:
-            every = summary[None]
+            stacked = summary[None]
             distance = size
             while distance < devices:
                 pairs = [(device, device ^ distance) for device in range(devices)]
-                every = jnp.concatenate([every, lax.ppermute(every, "slab", pairs)], axis=0)
+                stacked = jnp.concatenate([stacked, lax.ppermute(stacked, "slab", pairs)], axis=0)
                 distance *= 2
+            every = [stacked[index] for index in range(devices // size)]
     else:
         size = devices
-        local = lax.all_gather(packed, "slab")
-        every = jnp.zeros((1,) + packed.shape, jnp.float32)
+        gathered = lax.all_gather(packed, "slab")
+        local = [gathered[index] for index in range(devices)]
+        every = [jnp.zeros(packed.shape, jnp.float32)]
     half = jax.ShapeDtypeStruct((2, slots, modes // 2), jnp.float32)
     low, high = pl.pallas_call(
         functools.partial(
             final_kernel, slots=slots, points=points, devices=devices, mixed=mixed,
-            scale=1.0 / (32.0 * points * groups),
+            size=len(local), groups=len(every), scale=1.0 / (32.0 * points * groups),
         ),
         out_shape=(half, half),
-        in_specs=[smem, smem, smem, smem, vmem, vmem, vmem],
+        in_specs=[smem] * 4 + [vmem] * (len(local) + len(every) + 1),
         out_specs=(vmem, vmem),
         scratch_shapes=[
             pltpu.VMEM((slots, points, rows, 128), jnp.float32),
@@ -294,7 +307,7 @@
             pltpu.VMEM((slots, rows, 128), jnp.float32),
             pltpu.VMEM((slots, rows, 128), jnp.float32),
         ],
-    )(here_arr, lengths, energy_index, weight_code, local, every, table)
+    )(here_arr, lengths, energy_index, weight_code, *local, *every, table)
     if groups == 2:
         lower = lax.axis_index("energy") == 0
         mine = jnp.where(lower, low, high)

time: 40.7 us -> 40.9 us (level); the launches traced: 40.1 us -> 40.8 us
  other arithmetic: 4.3 us -> 0.94 us
  local copies, waits for them, and re-layouts: 3.67 us -> 6.18 us
  Pallas kernels: 5.71 us -> 7.06 us
  waiting for transfers between devices: 15.1 us -> 16.2 us
  starting transfers between devices: 10.6 us -> 9.67 us
    another operation x2 -> x0, other arithmetic: 3.35 us -> none  [the longest x1 1.68 us: shards(): jnp.stack([summary] + [lax.ppermute(summary, 'slab', [(device, device ^ o...]
    unnamed x19 -> x31, local copies, waits for them, and re-layouts: 2.19 us -> 4.7 us
    pallas_call x1, Pallas kernels: 2.23 us -> 3.07 us  [shards(): pl.pallas_call(functools.partial(final_kernel, slots=slots, points=points...]
    ppermute x3, starting transfers between devices: 3.3 us -> 2.51 us  [shards(): lax.ppermute(packed, 'slab', [(device, device ^ offset) for device in ran...]
    ppermute x3, waiting for transfers between devices: 7.57 us -> 8.33 us  [shards(): lax.ppermute(summary, 'slab', [(device, device ^ offset * size) for devic...]
    pallas_call x1, Pallas kernels: 1.73 us -> 2.15 us  [shards(): pl.pallas_call(functools.partial(summary_kernel, slots=slots, points=poin...]
where the time goes in v10:
time: 40.9 us; the launch traced here: 40.8 us
  waiting for transfers between devices  16.2 us (40%)
  starting transfers between devices  9.67 us (24%)
  Pallas kernels  7.06 us (17%)
  local copies, waits for them, and re-layouts  6.18 us (15%)
  other arithmetic  0.94 us (2%)
  between operations  0.78 us (2%)
    ppermute x3, waiting for transfers between devices, shards(): lax.ppermute(summary, 'slab', [(device, device ^ offset * size) for devic...  8.33 us
    ppermute x3, starting transfers between devices, shards(): lax.ppermute(summary, 'slab', [(device, device ^ offset * size) for devic...  5.58 us
    ppermute x3, waiting for transfers between devices, shards(): lax.ppermute(packed, 'slab', [(device, device ^ offset) for device in ran...  5.11 us
    unnamed x31, local copies, waits for them, and re-layouts  4.7 us
    pallas_call x1, Pallas kernels, shards(): pl.pallas_call(functools.partial(final_kernel, slots=slots, points=points...  3.07 us
    ppermute x1, waiting for transfers between devices, shards(): both = mine + lax.ppermute(theirs, 'energy', [(0, 1), (1, 0)])  2.75 us
    ppermute x3, starting transfers between devices, shards(): lax.ppermute(packed, 'slab', [(device, device ^ offset) for device in ran...  2.51 us
    pallas_call x1, Pallas kernels, shards(): pl.pallas_call(functools.partial(summary_kernel, slots=slots, points=poin...  2.15 us
  transfers between devices with their start and end apart: 7, of which 5 were waited for; matrix products, arithmetic and copies ran while one was open for 0% of the time, Pallas kernels for 0%

profile of v10, /device:TPU:0, one launch (start us, length us, event | category | flops | bytes accessed | tf_op | source)
XLA Modules:
  0.0 40.8 jit_solution(5784255919818770102)
XLA Ops:
  0.6 0.0 copy-start.11
  0.6 0.0 copy-start.9
  0.7 0.8 %concatenate.14 = f32[8,8,128]{2,1,0:T(8,128)S(1)} reshape(f32[4,2,1024]{2,1,0:T(2,128)} %param.14) | data formatting | bytes 65536 | tf_op jit(solution)/shard_map/concatenate | solution.py:245
  1.5 0.0 copy-done.11
  1.5 0.0 copy-start.12
  1.5 0.6 %copy-done.12 = f32[1024]{0:T(1024)S(1)} copy-done((f32[1024]{0:T(1024)S(1)}, f32[1024]{0:T(1024)}, u32[]{:S(2)}) %copy-start.12) | copy-done | bytes 4120
  2.2 0.8 %copy-done.10 = f32[16,1024]{1,0:T(8,128)S(1)} copy-done((f32[16,1024]{1,0:T(8,128)S(1)}, f32[16,1024]{1,0:T(8,128)}, u32[]{:S(2)}) %copy-start.10) | copy-done | bytes 65560
  3.1 0.7 %copy-done = f32[48,8,128]{2,1,0:T(8,128)} copy-done((f32[48,8,128]{2,1,0:T(8,128)}, f32[48,8,128]{2,1,0:T(8,128)S(1)}, u32[]{:S(2)}) %copy-start) | copy-done | bytes 196632
  3.8 2.1 %shard_map.95.refs_0_ = f32[24,8,128]{2,1,0:T(8,128)} custom-call(s32[1]{0:T(128)} %bitcast.here_ref, s32[16]{0:T(128)} %length_ref.3, s32[4]{0:T(128)} %energy_ref.3, f32[48,8,128]{2,1,0:T(8,128)} %copy-done), custom_call_target="tpu_custom_call" | custom-call | tf_op jit(solution)/shard_map/pallas_call | solution.py:258
  5.9 2.0 %collective-permute-start.2 = (f32[24,8,128]{2,1,0:T(8,128)}, f32[24,8,128]{2,1,0:T(8,128)S(1)}, u32[]{:S(2)}, u32[]{:S(2)}) collective-permute-start(f32[24,8,128]{2,1,0:T(8,128)} %shard_map.95.refs_0_), channel_id=1, source_target_pairs={{0,6},{2,4},{4,2},{6,0},{8,14},{10,12},{12,10},{14,8},{16,22},{18,... | collective-permute-start | bytes 294920 | tf_op jit(solution)/shard_map/ppermute | solution.py:268
  7.9 0.5 %collective-permute-start.1 = (f32[24,8,128]{2,1,0:T(8,128)}, f32[24,8,128]{2,1,0:T(8,128)S(1)}, u32[]{:S(2)}, u32[]{:S(2)}) collective-permute-start(f32[24,8,128]{2,1,0:T(8,128)} %shard_map.95.refs_0_), channel_id=1, source_target_pairs={{0,4},{2,6},{4,0},{6,2},{8,12},{10,14},{12,8},{14,10},{16,20},{18,... | collective-permute-start | bytes 294920 | tf_op jit(solution)/shard_map/ppermute | solution.py:268
  8.3 0.1 collective-permute-start
  8.4 2.9 %collective-permute-done.2.refs_3_ = f32[24,8,128]{2,1,0:T(8,128)S(1)} collective-permute-done((f32[24,8,128]{2,1,0:T(8,128)}, f32[24,8,128]{2,1,0:T(8,128)S(1)}, u32[]{:S(2)}, u32[]{:S(2)}) %collective-permute-start.2) | collective-permute-done | bytes 98336 | tf_op jit(solution)/shard_map/ppermute | solution.py:268
  11.4 2.2 %collective-permute-done.1.refs_2_ = f32[24,8,128]{2,1,0:T(8,128)S(1)} collective-permute-done((f32[24,8,128]{2,1,0:T(8,128)}, f32[24,8,128]{2,1,0:T(8,128)S(1)}, u32[]{:S(2)}, u32[]{:S(2)}) %collective-permute-start.1) | collective-permute-done | bytes 98336 | tf_op jit(solution)/shard_map/ppermute | solution.py:268
  13.5 0.0 collective-permute-done.refs_1_
  13.5 0.6 %copy-done.2 = f32[24,8,128]{2,1,0:T(8,128)} copy-done((f32[24,8,128]{2,1,0:T(8,128)}, f32[24,8,128]{2,1,0:T(8,128)S(1)}, u32[]{:S(2)}) %copy-start.2) | copy-done | bytes 98328
  14.2 0.6 %copy-done.3 = f32[24,8,128]{2,1,0:T(8,128)} copy-done((f32[24,8,128]{2,1,0:T(8,128)}, f32[24,8,128]{2,1,0:T(8,128)S(1)}, u32[]{:S(2)}) %copy-start.3) | copy-done | bytes 98328
  14.8 1.8 %shard_map.96.refs_4_ = f32[24,8,128]{2,1,0:T(8,128)} custom-call(s32[1]{0:T(128)} %bitcast.here_ref, f32[24,8,128]{2,1,0:T(8,128)} %shard_map.95.refs_0_, f32[24,8,128]{2,1,0:T(8,128)} %copy-done.3, f32[24,8,128]{2,1,0:T(8,128)} %copy-done.2, f32[24,8,128]{2,1,0:T(8,128)} %copy-done.1), custom_call_target="tpu_custom_call" | custom-call | tf_op jit(solution)/shard_map/pallas_call | solution.py:271
  16.6 5.0 %collective-permute-start.5 = (f32[24,8,128]{2,1,0:T(8,128)}, f32[24,8,128]{2,1,0:T(8,128)S(1)}, u32[]{:S(2)}, u32[]{:S(2)}) collective-permute-start(f32[24,8,128]{2,1,0:T(8,128)} %shard_map.96.refs_4_), channel_id=1, source_target_pairs={{0,24},{2,26},{4,28},{6,30},{8,16},{10,18},{12,20},{14,22},{16,8},... | collective-permute-start | bytes 294920 | tf_op jit(solution)/shard_map/ppermute | solution.py:279
  21.7 0.0 collective-permute-start.4
  21.7 0.6 %collective-permute-start.3 = (f32[24,8,128]{2,1,0:T(8,128)}, f32[24,8,128]{2,1,0:T(8,128)S(1)}, u32[]{:S(2)}, u32[]{:S(2)}) collective-permute-start(f32[24,8,128]{2,1,0:T(8,128)} %shard_map.96.refs_4_), channel_id=1, source_target_pairs={{0,8},{2,10},{4,12},{6,14},{8,0},{10,2},{12,4},{14,6},{16,24},{18,... | collective-permute-start | bytes 294920 | tf_op jit(solution)/shard_map/ppermute | solution.py:279
  22.2 3.4 %collective-permute-done.5.refs_7_ = f32[24,8,128]{2,1,0:T(8,128)S(1)} collective-permute-done((f32[24,8,128]{2,1,0:T(8,128)}, f32[24,8,128]{2,1,0:T(8,128)S(1)}, u32[]{:S(2)}, u32[]{:S(2)}) %collective-permute-start.5) | collective-permute-done | bytes 98336 | tf_op jit(solution)/shard_map/ppermute | solution.py:279
  25.6 5.0 %collective-permute-done.4.refs_6_ = f32[24,8,128]{2,1,0:T(8,128)S(1)} collective-permute-done((f32[24,8,128]{2,1,0:T(8,128)}, f32[24,8,128]{2,1,0:T(8,128)S(1)}, u32[]{:S(2)}, u32[]{:S(2)}) %collective-permute-start.4) | collective-permute-done | bytes 98336 | tf_op jit(solution)/shard_map/ppermute | solution.py:279
  30.6 0.0 collective-permute-done.3.refs_5_
  30.6 0.0 copy-done.6
  30.6 0.6 %copy-done.7 = f32[24,8,128]{2,1,0:T(8,128)} copy-done((f32[24,8,128]{2,1,0:T(8,128)}, f32[24,8,128]{2,1,0:T(8,128)S(1)}, u32[]{:S(2)}) %copy-start.7) | copy-done | bytes 98328
  31.2 0.6 %copy-done.8 = f32[24,8,128]{2,1,0:T(8,128)} copy-done((f32[24,8,128]{2,1,0:T(8,128)}, f32[24,8,128]{2,1,0:T(8,128)S(1)}, u32[]{:S(2)}) %copy-start.8) | copy-done | bytes 98328
  31.8 3.1 %shard_map.97 = (f32[2,16,512]{2,1,0:T(8,128)}, f32[2,16,512]{2,1,0:T(8,128)}) custom-call(s32[1]{0:T(128)} %bitcast.here_ref, s32[16]{0:T(128)} %length_ref.3, s32[4]{0:T(128)} %energy_ref.3, s32[4]{0:T(128)} %code_ref.1, f32[24,8,128]{2,1,0:T(8,128)} %shard_map.95.refs_0_, f32[24,8,128]{2,1,0:T(8,128)} %copy-done.3, f32[24,8,128]{2,1,0:T(8,128)} %copy-done.2, ...), custom_call_target="tpu_custom_call" | custom-call | tf_op jit(solution)/shard_map/pallas_call | solution.py:296
  34.9 0.9 %broadcast_select_fusion = f32[2,16,512]{2,1,0:T(8,128)S(1)} fusion(f32[2,16,512]{2,1,0:T(8,128)} %get-tuple-element.5, f32[2,16,512]{2,1,0:T(8,128)} %get-tuple-element.4, pred[]{:T(512)S(6)} %eq.3), kind=kLoop, calls=%fused_computation.4 | loop fusion | flops 16384 | bytes 196609 | tf_op jit(solution)/shard_map/jit(_where)/select_n | solution.py:314
  35.8 1.6 %collective-permute-start.6 = (f32[2,16,512]{2,1,0:T(8,128)S(1)}, f32[2,16,512]{2,1,0:T(8,128)S(1)}, u32[]{:S(2)}, u32[]{:S(2)}) collective-permute-start(f32[2,16,512]{2,1,0:T(8,128)S(1)} %broadcast_select_fusion), channel_id=1, source_target_pairs={{0,1},{1,0},{2,3},{3,2},{4,5},{5,4},{6,7},{7,6},{8,9},{9,8},{10,11... | collective-permute-start | bytes 196616 | tf_op jit(solution)/shard_map/ppermute | solution.py:315
  37.4 2.7 %collective-permute-done.6 = f32[2,16,512]{2,1,0:T(8,128)S(1)} collective-permute-done((f32[2,16,512]{2,1,0:T(8,128)S(1)}, f32[2,16,512]{2,1,0:T(8,128)S(1)}, u32[]{:S(2)}, u32[]{:S(2)}) %collective-permute-start.6) | collective-permute-done | bytes 65568 | tf_op jit(solution)/shard_map/ppermute | solution.py:315
  40.2 0.6 %slice_bitcast_fusion = (f32[16,512]{1,0:T(8,128)}, f32[16,512]{1,0:T(8,128)}) fusion(f32[2,16,512]{2,1,0:T(8,128)S(1)} %select_add_fusion), kind=kLoop, calls=%fused_computation.2 | loop fusion | bytes 131072 | tf_op jit(solution)/shard_map/squeeze | solution.py:320
  (23 shorter events, 0.1 us)
Async XLA Ops:
  0.6 0.8 %copy-start.11 = (f32[4,2,1024]{2,1,0:T(2,128)S(1)}, f32[4,2,1024]{2,1,0:T(2,128)}, u32[]{:S(2)}) copy-start(f32[4,2,1024]{2,1,0:T(2,128)} %param.15) | copy-start | bytes 98308
  0.6 0.9 %copy-start.9 = (f32[16,1024]{1,0:T(8,128)S(1)}, f32[16,1024]{1,0:T(8,128)}, u32[]{:S(2)}) copy-start(f32[16,1024]{1,0:T(8,128)} %param.9) | copy-start | bytes 196612
  1.5 0.7 %copy-start.12 = (f32[1024]{0:T(1024)S(1)}, f32[1024]{0:T(1024)}, u32[]{:S(2)}) copy-start(f32[1024]{0:T(1024)} %param.8) | copy-start | bytes 12292
  2.2 0.8 %copy-start.10 = (f32[16,1024]{1,0:T(8,128)S(1)}, f32[16,1024]{1,0:T(8,128)}, u32[]{:S(2)}) copy-start(f32[16,1024]{1,0:T(8,128)} %param.10) | copy-start | bytes 196612
  3.1 0.7 %copy-start = (f32[48,8,128]{2,1,0:T(8,128)}, f32[48,8,128]{2,1,0:T(8,128)S(1)}, u32[]{:S(2)}) copy-start(f32[48,8,128]{2,1,0:T(8,128)S(1)} %constant_dynamic-update-slice_fusion.table_ref.refs_8_) | copy-start | bytes 589828
  5.9 5.5 %collective-permute-start.2 = (f32[24,8,128]{2,1,0:T(8,128)}, f32[24,8,128]{2,1,0:T(8,128)S(1)}, u32[]{:S(2)}, u32[]{:S(2)}) collective-permute-start(f32[24,8,128]{2,1,0:T(8,128)} %shard_map.95.refs_0_), channel_id=1, source_target_pairs={{0,6},{2,4},{4,2},{6,0},{8,14},{10,12},{12,10},{14,8},{16,22},{18,... | collective-permute-start | bytes 294920 | tf_op jit(solution)/shard_map/ppermute | solution.py:268
  7.9 5.7 %collective-permute-start.1 = (f32[24,8,128]{2,1,0:T(8,128)}, f32[24,8,128]{2,1,0:T(8,128)S(1)}, u32[]{:S(2)}, u32[]{:S(2)}) collective-permute-start(f32[24,8,128]{2,1,0:T(8,128)} %shard_map.95.refs_0_), channel_id=1, source_target_pairs={{0,4},{2,6},{4,0},{6,2},{8,12},{10,14},{12,8},{14,10},{16,20},{18,... | collective-permute-start | bytes 294920 | tf_op jit(solution)/shard_map/ppermute | solution.py:268
  8.3 5.2 %collective-permute-start = (f32[24,8,128]{2,1,0:T(8,128)}, f32[24,8,128]{2,1,0:T(8,128)S(1)}, u32[]{:S(2)}, u32[]{:S(2)}) collective-permute-start(f32[24,8,128]{2,1,0:T(8,128)} %shard_map.95.refs_0_), channel_id=1, source_target_pairs={{0,2},{2,0},{4,6},{6,4},{8,10},{10,8},{12,14},{14,12},{16,18},{18,... | collective-permute-start | bytes 294920 | tf_op jit(solution)/shard_map/ppermute | solution.py:268
  11.4 2.2 %copy-start.1 = (f32[24,8,128]{2,1,0:T(8,128)}, f32[24,8,128]{2,1,0:T(8,128)S(1)}, u32[]{:S(2)}) copy-start(f32[24,8,128]{2,1,0:T(8,128)S(1)} %collective-permute-done.2.refs_3_) | copy-start | bytes 294916
  13.5 0.6 %copy-start.2 = (f32[24,8,128]{2,1,0:T(8,128)}, f32[24,8,128]{2,1,0:T(8,128)S(1)}, u32[]{:S(2)}) copy-start(f32[24,8,128]{2,1,0:T(8,128)S(1)} %collective-permute-done.1.refs_2_) | copy-start | bytes 294916
  14.2 0.6 %copy-start.3 = (f32[24,8,128]{2,1,0:T(8,128)}, f32[24,8,128]{2,1,0:T(8,128)S(1)}, u32[]{:S(2)}) copy-start(f32[24,8,128]{2,1,0:T(8,128)S(1)} %collective-permute-done.refs_1_) | copy-start | bytes 294916
  16.6 8.9 %collective-permute-start.5 = (f32[24,8,128]{2,1,0:T(8,128)}, f32[24,8,128]{2,1,0:T(8,128)S(1)}, u32[]{:S(2)}, u32[]{:S(2)}) collective-permute-start(f32[24,8,128]{2,1,0:T(8,128)} %shard_map.96.refs_4_), channel_id=1, source_target_pairs={{0,24},{2,26},{4,28},{6,30},{8,16},{10,18},{12,20},{14,22},{16,8},... | collective-permute-start | bytes 294920 | tf_op jit(solution)/shard_map/ppermute | solution.py:279
  21.7 8.9 %collective-permute-start.4 = (f32[24,8,128]{2,1,0:T(8,128)}, f32[24,8,128]{2,1,0:T(8,128)S(1)}, u32[]{:S(2)}, u32[]{:S(2)}) collective-permute-start(f32[24,8,128]{2,1,0:T(8,128)} %shard_map.96.refs_4_), channel_id=1, source_target_pairs={{0,16},{2,18},{4,20},{6,22},{8,24},{10,26},{12,28},{14,30},{16,0},... | collective-permute-start | bytes 294920 | tf_op jit(solution)/shard_map/ppermute | solution.py:279
  21.7 8.9 %collective-permute-start.3 = (f32[24,8,128]{2,1,0:T(8,128)}, f32[24,8,128]{2,1,0:T(8,128)S(1)}, u32[]{:S(2)}, u32[]{:S(2)}) collective-permute-start(f32[24,8,128]{2,1,0:T(8,128)} %shard_map.96.refs_4_), channel_id=1, source_target_pairs={{0,8},{2,10},{4,12},{6,14},{8,0},{10,2},{12,4},{14,6},{16,24},{18,... | collective-permute-start | bytes 294920 | tf_op jit(solution)/shard_map/ppermute | solution.py:279
  25.6 5.0 %copy-start.6 = (f32[24,8,128]{2,1,0:T(8,128)}, f32[24,8,128]{2,1,0:T(8,128)S(1)}, u32[]{:S(2)}) copy-start(f32[24,8,128]{2,1,0:T(8,128)S(1)} %collective-permute-done.5.refs_7_) | copy-start | bytes 294916
  30.6 0.6 %copy-start.7 = (f32[24,8,128]{2,1,0:T(8,128)}, f32[24,8,128]{2,1,0:T(8,128)S(1)}, u32[]{:S(2)}) copy-start(f32[24,8,128]{2,1,0:T(8,128)S(1)} %collective-permute-done.4.refs_6_) | copy-start | bytes 294916
  31.2 0.6 %copy-start.8 = (f32[24,8,128]{2,1,0:T(8,128)}, f32[24,8,128]{2,1,0:T(8,128)S(1)}, u32[]{:S(2)}) copy-start(f32[24,8,128]{2,1,0:T(8,128)S(1)} %collective-permute-done.3.refs_5_) | copy-start | bytes 294916
  34.9 5.3 %copy-start.4 = (f32[2,16,512]{2,1,0:T(8,128)S(1)}, f32[2,16,512]{2,1,0:T(8,128)}, u32[]{:S(2)}) copy-start(f32[2,16,512]{2,1,0:T(8,128)} %get-tuple-element.4) | copy-start | bytes 196612
  34.9 5.3 %copy-start.5 = (f32[2,16,512]{2,1,0:T(8,128)S(1)}, f32[2,16,512]{2,1,0:T(8,128)}, u32[]{:S(2)}) copy-start(f32[2,16,512]{2,1,0:T(8,128)} %get-tuple-element.5) | copy-start | bytes 196612
  35.8 4.3 %collective-permute-start.6 = (f32[2,16,512]{2,1,0:T(8,128)S(1)}, f32[2,16,512]{2,1,0:T(8,128)S(1)}, u32[]{:S(2)}, u32[]{:S(2)}) collective-permute-start(f32[2,16,512]{2,1,0:T(8,128)S(1)} %broadcast_select_fusion), channel_id=1, source_target_pairs={{0,1},{1,0},{2,3},{3,2},{4,5},{5,4},{6,7},{7,6},{8,9},{9,8},{10,11... | collective-permute-start | bytes 196616 | tf_op jit(solution)/shard_map/ppermute | solution.py:315
